TPU v7x, 256 devices: a whole 4x4x8 slice. The times are simulated.
256 devices in a mesh: act: 32 (over x, y, core), pix: 8 (over z).
Axes of the slice: x: 4, y: 4, z: 8, core: 2. Of those that a mesh axis runs over, the one named last changes fastest.
Arguments:
- pixel_index: int32 [8, 512], P('pix'), may hold values from 0 to 65535
- act_map: int32 [32768], P('act'), may hold values from 0 to 32767, each once
- omega: bfloat16 [32768, 128], P('act'), may hold values from -6 to 6
- pupil_field: float32 [8, 2, 32768], P('pix', None, 'act'), may hold values from -6 to 6
- channel_scale: float32 [8], P('pix'), may hold values from 0.9 to 1.1
- channel_flux: float32 [8], P('pix'), may hold values from 0.3 to 3
Outputs:
- basis_out: float32 [8, 1024, 128], P('pix', 'act')
- projection: float32 [128, 32768], P('pix', 'act')
- r_factor: float32 [128, 128], replicated
Inputs may be any that keep to these rules, and one draw needn't show every extreme that they name: `act_map`: every number of 0 to 32767 appears once. `pixel_index`: pixels of a channel may repeat.
All inputs are finite; a program needn't handle non-finite values.
Results may differ from a plain program's by a relative error of at most 0.0048.
Values may be sent and summed in bfloat16 or wider, within the bound.
No kernel may reach another device: no remote copies, remote signals or barrier semaphores. Data moves between devices by JAX's collectives and lax.ppermute only.
A program may use at most 64 MiB of HBM per device.

v0:
```python
import math

import jax
import jax.numpy as jnp
from jax import lax
from jax.sharding import PartitionSpec as P

GRID = 128
FOCAL = 256
RANK = 128
ACT = 32768


TWO_PI = 2.0 * math.pi
INFL_RATE = 4.5
DEFOCUS_RATE = 6.0


def rows_for(lines, count):
    spare = -len(lines) % count
    return jnp.pad(lines, [(0, spare)] + [(0, 0)] * (lines.ndim - 1))


def sent_to_all(value, axis):
    copies = jnp.broadcast_to(value, (lax.axis_size(axis), *value.shape))
    return lax.all_to_all(copies, axis, split_axis=0, concat_axis=0, tiled=True)


def laid_out(parts, dim):
    shape = list(parts.shape[1:])
    shape[dim] *= parts.shape[0]
    return jnp.moveaxis(parts, 0, dim).reshape(shape)


def collect(value, axis, dim):
    parts = sent_to_all(value, axis)
    return laid_out(parts, dim)


def in_blocks(value, dim, count):
    before, after = (value.shape[:dim], value.shape[dim + 1 :])
    return jnp.moveaxis(value.reshape(*before, count, -1, *after), dim, 0)


def summed_on_arrival(value, axis, dim):
    parts = in_blocks(value, dim, lax.axis_size(axis))
    arrived = lax.all_to_all(parts, axis, split_axis=0, concat_axis=0, tiled=True)
    return arrived.sum(axis=0)


def sum_by_parts(value, axes):
    lines = value.reshape(-1, value.shape[-1])
    padded = rows_for(lines, lax.axis_size(axes))
    whole = collect(summed_on_arrival(padded, axes, 0), axes, 0)
    return lax.slice_in_dim(whole, 0, len(lines)).reshape(value.shape)


def over_copies(value, axis):
    return sent_to_all(value, axis).sum(axis=0)


def jacobian_rows(pixels, wave_scale, flux_level, codes, field_re, field_im):
    delta_u = pixels // FOCAL - FOCAL // 2
    delta_v = pixels % FOCAL - FOCAL // 2
    mirror = codes // (GRID * GRID)
    column_x = codes // GRID % GRID - GRID // 2
    column_y = codes % GRID - GRID // 2
    phase_int = delta_u[:, None] * column_x[None, :] + delta_v[:, None] * column_y[None, :]
    radius = (delta_u * delta_u + delta_v * delta_v).astype(jnp.float32)
    amplitude = flux_level * jnp.exp(-INFL_RATE * radius / (FOCAL * FOCAL))
    defocus = radius * (TWO_PI * DEFOCUS_RATE / (FOCAL * FOCAL)) / wave_scale
    phase_angle = mirror.astype(jnp.float32)[None, :] * defocus[
        :, None
    ] - TWO_PI / FOCAL * wave_scale * phase_int.astype(jnp.float32)
    cosine = jnp.cos(phase_angle)
    sine_part = jnp.sin(phase_angle)
    real_part = amplitude[:, None] * (field_re[None, :] * cosine - field_im[None, :] * sine_part)
    imag_part = amplitude[:, None] * (field_re[None, :] * sine_part + field_im[None, :] * cosine)
    stacked = jnp.stack([real_part, imag_part], axis=1)
    return stacked.reshape(2 * pixels.shape[0], codes.shape[0]).astype(jnp.bfloat16)


def gram_of(sketch):
    return lax.dot_general(
        sketch,
        sketch,
        (((0,), (0,)), ((), ())),
        precision=lax.Precision.HIGHEST,
        preferred_element_type=jnp.float32,
    )


def orthonormal(sketch, gram_matrix):
    lower_factor = jnp.linalg.cholesky(gram_matrix)
    basis = jax.scipy.linalg.solve_triangular(lower_factor, sketch.T, lower=True).T
    return (lower_factor, basis)


def on_device(pixel_index, act_map, omega, pupil_field, channel_scale, channel_flux):
    pixels = pixel_index[0]
    rows_dev = 2 * pixels.shape[0]
    act_cols = act_map.shape[0]
    act_count = lax.axis_size("act")
    pix_count = lax.axis_size("pix")
    total_rows = rows_dev * pix_count
    share_rows = rows_dev // act_count
    wave_scale = channel_scale[0]
    flux_level = channel_flux[0]
    field_re = pupil_field[0, 0]
    field_im = pupil_field[0, 1]
    padded = jnp.concatenate([pixels, pixels[:1]])
    rows_all = jacobian_rows(padded, wave_scale, flux_level, act_map, field_re, field_im)
    stored = lax.dynamic_slice_in_dim(rows_all, 0 % 2, rows_dev, 0)

    def rows_of():
        return stored

    sketch = sum_by_parts(jnp.dot(rows_of(), omega, preferred_element_type=jnp.float32), "act")
    gram_matrix = over_copies(gram_of(sketch), "pix")
    lower_factor, basis = orthonormal(sketch, gram_matrix)
    own_basis = lax.dynamic_slice_in_dim(basis, lax.axis_index("act") * share_rows, share_rows, 0)
    coarse = basis.astype(jnp.bfloat16)
    block_rows = math.gcd(rows_dev, 2048)

    def add_block(block_id, total_sum):
        jacobian = rows_of()
        return total_sum + lax.dot_general(
            coarse, jacobian, (((0,), (0,)), ((), ())), preferred_element_type=jnp.float32
        )

    partial_value = lax.fori_loop(
        0, rows_dev // block_rows, add_block, jnp.zeros((RANK, act_cols), jnp.float32)
    )
    projection = summed_on_arrival(partial_value, "pix", 0)
    basis_out = (own_basis * math.sqrt(total_rows)).reshape(1, share_rows, RANK)
    r_factor = lower_factor.T / math.sqrt(total_rows * ACT)
    return (basis_out, projection, r_factor)


def solution(mesh):
    return jax.shard_map(
        on_device,
        mesh=mesh,
        in_specs=(
            P("pix", None),
            P("act"),
            P("act", None),
            P("pix", None, "act"),
            P("pix"),
            P("pix"),
        ),
        out_specs=(P("pix", "act", None), P("pix", "act"), P()),
        check_vma=False,
    )
```

profile of v0, /device:TPU:1, one launch (start us, length us, event | category | flops | bytes accessed | tf_op | source)
XLA Modules:
  0.0 250.5 jit_solution(2375972208156320024)
XLA Ops:
  0.6 1.2 slice.23
  2.5 1.3 fusion.6
  3.9 1.4 exponential_multiply_fusion
  5.9 0.7 fusion.8
  6.6 0.8 fusion.20
  7.4 1.3 multiply_divide_fusion
  8.7 60.7 %fusion.19 = (f32[513,1,1024]{2,1,0:T(1,128)S(1)}, f32[513,1,1024]{2,1,0:T(1,128)S(1)}) fusion(s32[1024]{0:T(1024)S(1)} %get-tuple-element.32, s32[513]{0:T(1024)S(1)} %fusion.6, s32[1024]{0:T(1024)S(1)} %get-tuple-element.33, s32[513]{0:T(1024)S(1)} %get-tuple-element.22, f32[]{:T(128)S(6)} %mul_shard_map.3, f32[513]{0:T(1024)S(1)} %multiply_divide_fusion, ...), kind=kLoop, calls=%fused_computation.54 | loop fusion | flops 3677184 | bytes 4220944 | tf_op jit(solution)/shard_map/sin | solution.py:76
  69.4 59.8 %multiply_convert_fusion.1 = (bf16[513,1,1024]{2,1,0:T(2,128)(2,1)S(1)}, bf16[513,1,1024]{2,1,0:T(2,128)(2,1)S(1)}) fusion(f32[513,1,1024]{2,1,0:T(1,128)S(1)} %get-tuple-element.23, f32[1024]{0:T(1024)S(1)} %bitcast.39, f32[1024]{0:T(1024)S(1)} %bitcast.38, f32[513]{0:T(1024)S(1)} %get-tuple-element.21, f32[513,1,1024]{2,1,0:T(1,128)S(1)} %get-tuple-element.24), kind=kLoop, calls=%fused_computation.1 | loop fusion | flops 5253120 | bytes 6313988 | tf_op jit(solution)/shard_map/convert
  129.2 8.7 %pad_maximum_fusion = bf16[512,2,1024]{2,1,0:T(2,128)(2,1)} fusion(bf16[513,1,1024]{2,1,0:T(2,128)(2,1)S(1)} %get-tuple-element.26, bf16[513,1,1024]{2,1,0:T(2,128)(2,1)S(1)} %get-tuple-element.25), kind=kLoop, calls=%fused_computation.3 | loop fusion | flops 4194304 | bytes 4198400 | tf_op jit(solution)/shard_map/stack | solution.py:79
  137.9 2.7 %dynamic_slice.9 = bf16[1024,1024]{1,0:T(8,128)(2,1)S(1)} reshape(bf16[512,2,1024]{2,1,0:T(2,128)(2,1)} %pad_maximum_fusion) | data formatting | bytes 4194304 | tf_op jit(solution)/shard_map/dynamic_slice | solution.py:113
  140.7 0.7 fusion.21
  141.4 20.0 %all_to_all.20 = f32[32,32,128]{2,1,0:T(8,128)S(1)} all-to-all(f32[32,32,128]{2,1,0:T(8,128)S(1)} %bitcast.34), channel_id=1, replica_groups=mesh['act'=32,'pix'=8] {'act'}, dimensions={0} | all-to-all | bytes 1048576 | tf_op jit(solution)/shard_map/all_to_all | solution.py:47
  161.5 15.0 %all_to_all.21 = f32[32,32,128]{2,1,0:T(8,128)S(1)} all-to-all(f32[32,32,128]{2,1,0:T(8,128)S(1)} %broadcast_in_dim.5), channel_id=1, replica_groups=mesh['act'=32,'pix'=8] {'act'}, dimensions={0} | all-to-all | bytes 1048576 | tf_op jit(solution)/shard_map/all_to_all | solution.py:26
  176.5 1.0 convolution_bitcast_fusion
  177.6 26.0 %all_to_all.22 = f32[8,128,128]{2,1,0:T(8,128)S(1)} all-to-all(f32[8,128,128]{2,1,0:T(8,128)S(1)} %broadcast_in_dim.6), channel_id=1, replica_groups=mesh['act'=32,'pix'=8] {'pix'}, dimensions={0} | all-to-all | bytes 1048576 | tf_op jit(solution)/shard_map/all_to_all | solution.py:26
  203.7 11.7 %cholesky.16 = f32[128,128]{1,0:T(8,128)S(1)} custom-call(f32[128,128]{1,0:T(8,128)S(1)} %fusion.4), custom_call_target="Cholesky" | custom-call | tf_op jit(solution)/shard_map/jit(cholesky)/cholesky | solution.py:94
  215.5 0.6 compare_reduce_fusion
  216.1 0.7 multiply_bitcast_fusion
  216.8 9.8 %custom-call.7 = f32[1,128,128]{1,2,0:T(8,128)S(1)} custom-call(f32[1,128,128]{2,1,0:T(8,128)S(1)} %get-tuple-element.28), custom_call_target="InvertDiagBlocksLowerTriangular" | custom-call | tf_op jit(solution)/shard_map/jit(_solve_triangular)/triangular_solve | solution.py:95
  227.2 1.3 fusion
  228.4 3.5 %all-to-all-start.3 = ((f32[8,16,1024]{2,1,0:T(8,128)}), f32[8,16,1024]{2,1,0:T(8,128)S(1)}, u32[]{:S(2)}, u32[]{:S(2)}) async-start(f32[8,16,1024]{2,1,0:T(8,128)} %bitcast.13), calls=%async_computation.3 | async-start | bytes 1048576 | tf_op jit(solution)/shard_map/all_to_all | solution.py:47
  231.9 0.7 copy.12
  233.3 16.5 %all-to-all-done.3 = f32[8,16,1024]{2,1,0:T(8,128)S(1)} async-done(((f32[8,16,1024]{2,1,0:T(8,128)}), f32[8,16,1024]{2,1,0:T(8,128)S(1)}, u32[]{:S(2)}, u32[]{:S(2)}) %all-to-all-start.3) | async-done | bytes 524320 | tf_op jit(solution)/shard_map/all_to_all | solution.py:47
  249.8 0.7 reduce_sum.29
  (11 shorter events, 1.5 us)
Async XLA Ops:
  0.6 140.1 %copy-start = (bf16[1024,128]{1,0:T(8,128)(2,1)S(1)}, bf16[1024,128]{1,0:T(8,128)(2,1)}, u32[]{:S(2)}) copy-start(bf16[1024,128]{1,0:T(8,128)(2,1)} %param.8) | copy-start | bytes 786436
  228.4 21.4 %all-to-all-start.3 = ((f32[8,16,1024]{2,1,0:T(8,128)}), f32[8,16,1024]{2,1,0:T(8,128)S(1)}, u32[]{:S(2)}, u32[]{:S(2)}) async-start(f32[8,16,1024]{2,1,0:T(8,128)} %bitcast.13), calls=%async_computation.3 | async-start | bytes 1048576 | tf_op jit(solution)/shard_map/all_to_all | solution.py:47
where the time goes:
time: 251 us; the launch traced here: 250 us
  other arithmetic  158 us (63%)
  blocking collectives  61 us (24%)
  waiting for transfers between devices  16.5 us (7%)
  local copies, waits for them, and re-layouts  5.65 us (2%)
  matrix products  3.55 us (1%)
  starting transfers between devices  3.49 us (1%)
    sin x1, other arithmetic, jacobian_rows(): sine_part = jnp.sin(phase_angle)  60.7 us
    another operation x1, other arithmetic  59.8 us
    all_to_all x2, blocking collectives, sent_to_all(): return lax.all_to_all(copies, axis, split_axis=0, concat_axis=0, tiled=True)  41 us
    all_to_all x1, blocking collectives, summed_on_arrival(): lax.all_to_all(parts, axis, split_axis=0, concat_axis=0, tiled=True)  20 us
    all_to_all x1, waiting for transfers between devices, summed_on_arrival(): lax.all_to_all(parts, axis, split_axis=0, concat_axis=0, tiled=True)  16.5 us
    another operation x3, other arithmetic, orthonormal(): lower_factor = jnp.linalg.cholesky(gram_matrix)  12.4 us
    another operation x1, other arithmetic, orthonormal(): jax.scipy.linalg.solve_triangular(lower_factor, sketch.T, lower=True)  9.81 us
    another operation x1, other arithmetic, jacobian_rows(): stacked = jnp.stack([real_part, imag_part], axis=1)  8.74 us
  transfers between devices with their start and end apart: 1, of which 1 were waited for; matrix products, arithmetic and copies ran while one was open for 1% of the time, Pallas kernels for 0%

commit v1 on v0

v1 whole, which is shorter than its diff:
```python
import math

import jax
import jax.numpy as jnp
from jax import lax
from jax.sharding import PartitionSpec as P

GRID = 128
FOCAL = 256
RANK = 128
ACT = 32768


TWO_PI = 2.0 * math.pi
INFL_RATE = 4.5
DEFOCUS_RATE = 6.0


def jacobian_planes(pixels, wave_scale, flux_level, codes, field_re, field_im):
    delta_u = pixels // FOCAL - FOCAL // 2
    delta_v = pixels % FOCAL - FOCAL // 2
    mirror = codes // (GRID * GRID)
    column_x = codes // GRID % GRID - GRID // 2
    column_y = codes % GRID - GRID // 2
    phase_int = delta_u[:, None] * column_x[None, :] + delta_v[:, None] * column_y[None, :]
    radius = (delta_u * delta_u + delta_v * delta_v).astype(jnp.float32)
    amplitude = flux_level * jnp.exp(-INFL_RATE * radius / (FOCAL * FOCAL))
    defocus = radius * (TWO_PI * DEFOCUS_RATE / (FOCAL * FOCAL)) / wave_scale
    phase_angle = mirror.astype(jnp.float32)[None, :] * defocus[
        :, None
    ] - TWO_PI / FOCAL * wave_scale * phase_int.astype(jnp.float32)
    cosine = jnp.cos(phase_angle)
    sine_part = jnp.sin(phase_angle)
    real_part = amplitude[:, None] * (field_re[None, :] * cosine - field_im[None, :] * sine_part)
    imag_part = amplitude[:, None] * (field_re[None, :] * sine_part + field_im[None, :] * cosine)
    return real_part.astype(jnp.bfloat16), imag_part.astype(jnp.bfloat16)


def gram_of(sketch):
    return lax.dot_general(
        sketch,
        sketch,
        (((0,), (0,)), ((), ())),
        precision=lax.Precision.HIGHEST,
        preferred_element_type=jnp.float32,
    )


def on_device(pixel_index, act_map, omega, pupil_field, channel_scale, channel_flux):
    pixels = pixel_index[0]
    npix = pixels.shape[0]
    rows_dev = 2 * npix
    act_count = lax.axis_size("act")
    pix_count = lax.axis_size("pix")
    total_rows = rows_dev * pix_count
    share_pix = npix // act_count
    real_rows, imag_rows = jacobian_planes(
        pixels, channel_scale[0], channel_flux[0], act_map, pupil_field[0, 0], pupil_field[0, 1]
    )
    jac = jnp.concatenate([real_rows, imag_rows], axis=0)
    partial_sketch = jnp.dot(jac, omega, preferred_element_type=jnp.float32)
    sketch = lax.psum(partial_sketch, "act")
    gram_matrix = lax.psum(gram_of(sketch), "pix")
    lower_factor = jnp.linalg.cholesky(gram_matrix)
    basis = jax.scipy.linalg.solve_triangular(lower_factor, sketch.T, lower=True).T
    first = lax.axis_index("act") * share_pix
    own_re = lax.dynamic_slice_in_dim(basis, first, share_pix, 0)
    own_im = lax.dynamic_slice_in_dim(basis, npix + first, share_pix, 0)
    own_basis = jnp.stack([own_re, own_im], axis=1).reshape(2 * share_pix, RANK)
    coarse = basis.astype(jnp.bfloat16)
    partial_value = lax.dot_general(
        coarse, jac, (((0,), (0,)), ((), ())), preferred_element_type=jnp.float32
    )
    projection = lax.psum_scatter(partial_value, "pix", scatter_dimension=0, tiled=True)
    basis_out = (own_basis * math.sqrt(total_rows)).reshape(1, 2 * share_pix, RANK)
    r_factor = lower_factor.T / math.sqrt(total_rows * ACT)
    return (basis_out, projection, r_factor)


def solution(mesh):
    return jax.shard_map(
        on_device,
        mesh=mesh,
        in_specs=(
            P("pix", None),
            P("act"),
            P("act", None),
            P("pix", None, "act"),
            P("pix"),
            P("pix"),
        ),
        out_specs=(P("pix", "act", None), P("pix", "act"), P()),
        check_vma=False,
    )
```

time: 251 us -> 285 us (1.14); the launches traced: 250 us -> 281 us
  waiting for transfers between devices: 16.5 us -> 221 us
  other arithmetic: 158 us -> 36.2 us
  blocking collectives: 61 us -> 0 us
  between operations: 2.07 us -> 15.2 us
  starting transfers between devices: 3.49 us -> 0.12 us
  local copies, waits for them, and re-layouts: 5.65 us -> 2.45 us
    psum x0 -> x2, waiting for transfers between devices: none -> 186 us  [the longest x1 118 us: on_device(): sketch = lax.psum(partial_sketch, 'act')]
    another operation x6 -> x4, other arithmetic: 90.8 us -> 22.2 us  [the longest x3 12.4 us: on_device(): lower_factor = jnp.linalg.cholesky(gram_matrix)]
    all_to_all x3 -> x0, blocking collectives: 61 us -> none  [the longest x2 41 us: sent_to_all(): return lax.all_to_all(copies, axis, split_axis=0, concat_axis=0, tiled=True)]
    sin x1 -> x0, other arithmetic: 60.7 us -> none  [jacobian_rows(): sine_part = jnp.sin(phase_angle)]
    reduce_scatter x0 -> x1, waiting for transfers between devices: none -> 35.2 us  [on_device(): lax.psum_scatter(partial_value, 'pix', scatter_dimension=0, tiled=True)]
    all_to_all x1 -> x0, waiting for transfers between devices: 16.5 us -> none  [summed_on_arrival(): lax.all_to_all(parts, axis, split_axis=0, concat_axis=0, tiled=True)]
    convert_element_type x1 -> x2, other arithmetic: 0.71 us -> 9.76 us  [the longest x1 9.06 us: jacobian_planes(): return (real_part.astype(jnp.bfloat16), imag_part.astype(jnp.bfloat16))]
    all_to_all x1 -> x0, starting transfers between devices: 3.49 us -> none  [summed_on_arrival(): lax.all_to_all(parts, axis, split_axis=0, concat_axis=0, tiled=True)]
  transfers between devices with their start and end apart: 1 -> 3, of which waited for: 1 -> 3; matrix products, arithmetic and copies ran while one was open for 1% -> 0% of each run, Pallas kernels for 0% -> 0%
where the time goes in v1:
time: 285 us; the launch traced here: 281 us
  waiting for transfers between devices  221 us (78%)
  other arithmetic  36.2 us (13%)
  between operations  15.2 us (5%)
  matrix products  6.23 us (2%)
    psum x1, waiting for transfers between devices, on_device(): sketch = lax.psum(partial_sketch, 'act')  118 us
    psum x1, waiting for transfers between devices, on_device(): gram_matrix = lax.psum(gram_of(sketch), 'pix')  67.3 us
    reduce_scatter x1, waiting for transfers between devices, on_device(): lax.psum_scatter(partial_value, 'pix', scatter_dimension=0, tiled=True)  35.2 us
    another operation x3, other arithmetic, on_device(): lower_factor = jnp.linalg.cholesky(gram_matrix)  12.4 us
    another operation x1, other arithmetic, on_device(): jax.scipy.linalg.solve_triangular(lower_factor, sketch.T, lower=True)  9.81 us
    convert_element_type x1, other arithmetic, jacobian_planes(): return (real_part.astype(jnp.bfloat16), imag_part.astype(jnp.bfloat16))  9.06 us
  transfers between devices with their start and end apart: 3, of which 3 were waited for; matrix products, arithmetic and copies ran while one was open for 0% of the time, Pallas kernels for 0%

profile of v1, /device:TPU:1, one launch (start us, length us, event | category | flops | bytes accessed | tf_op | source)
XLA Modules:
  0.0 281.0 jit_solution(6364925790602597482)
XLA Ops:
  7.2 0.0 all-reduce.3.cloned.1.call-start
  7.9 0.7 fusion.16
  8.6 0.7 exponential_multiply_fusion
  10.0 0.7 fusion.9
  10.7 0.8 fusion.21
  11.4 0.7 multiply_divide_fusion
  12.1 9.1 %multiply_convert_fusion.1 = (bf16[512,1024]{1,0:T(8,128)(2,1)S(1)}, bf16[512,1024]{1,0:T(8,128)(2,1)S(1)}) fusion(f32[1024]{0:T(1024)S(1)} %bitcast.32, s32[1024]{0:T(1024)S(1)} %get-tuple-element.17, s32[512]{0:T(512)S(1)} %fusion.16, s32[1024]{0:T(1024)S(1)} %get-tuple-element.18, s32[512]{0:T(512)S(1)} %get-tuple-element.7, f32[]{:T(128)S(6)} %mul_shard_map.3, ...), kind=kLoop, calls=%fused_computation.2 | loop fusion | flops 8912896 | bytes 2125828 | tf_op jit(solution)/shard_map/convert_element_type | solution.py:36
  21.2 1.5 fusion.3
  22.8 0.0 all-reduce.5.cloned.1.call-start
  22.8 118.3 %all-reduce.3.cloned.1.call-done = f32[1024,128]{1,0:T(8,128)} async-done(((f32[1024,128]{1,0:T(8,128)}), f32[1024,128]{1,0:T(8,128)}) %all-reduce.3.cloned.1.call-update) | async-done | bytes 524304 | tf_op jit(solution)/shard_map/psum | solution.py:62
  141.1 2.9 %fusion.22 = f32[128,128]{0,1:T(8,128)} fusion(f32[1024,128]{1,0:T(8,128)} %all-reduce.3.cloned.1.call-done), kind=kOutput, calls=%fused_computation.58 | convolution fusion | flops 201326592 | bytes 589824 | tf_op jit(solution)/shard_map/dot_general | solution.py:40
  144.0 0.0 reduce-scatter.2.cloned.1.call-start
  144.0 67.3 %all-reduce.5.cloned.1.call-done = f32[128,128]{0,1:T(8,128)} async-done(((f32[128,128]{0,1:T(8,128)}), f32[128,128]{0,1:T(8,128)}) %all-reduce.5.cloned.1.call-update) | async-done | bytes 65552 | tf_op jit(solution)/shard_map/psum | solution.py:63
  211.3 0.9 copy.10
  212.3 0.9 fusion.7
  213.1 11.7 %cholesky.16 = f32[128,128]{1,0:T(8,128)S(1)} custom-call(f32[128,128]{1,0:T(8,128)S(1)} %fusion.7), custom_call_target="Cholesky" | custom-call | tf_op jit(solution)/shard_map/jit(cholesky)/cholesky | solution.py:64
  224.9 0.6 compare_reduce_fusion
  225.5 0.7 multiply_bitcast_fusion
  226.2 9.8 %custom-call.7 = f32[1,128,128]{1,2,0:T(8,128)S(1)} custom-call(f32[1,128,128]{2,1,0:T(8,128)S(1)} %get-tuple-element.11), custom_call_target="InvertDiagBlocksLowerTriangular" | custom-call | tf_op jit(solution)/shard_map/jit(_solve_triangular)/triangular_solve | solution.py:65
  236.0 0.6 fusion.5
  236.6 1.3 fusion.2
  237.9 0.7 copy.11
  238.6 0.6 maximum_multiply_fusion
  239.3 35.2 %reduce-scatter.2.cloned.1.call-done = f32[16,1024]{1,0:T(8,128)} async-done(((f32[128,1024]{1,0:T(8,128)}), f32[16,1024]{1,0:T(8,128)}) %reduce-scatter.2.cloned.1.call-update) | async-done | bytes 65552 | tf_op jit(solution)/shard_map/reduce_scatter | solution.py:74
  (9 shorter events, 0.1 us)
Async XLA Ops:
  7.2 14.1 %copy-start = (bf16[1024,128]{1,0:T(8,128)(2,1)S(1)}, bf16[1024,128]{1,0:T(8,128)(2,1)}, u32[]{:S(2)}) copy-start(bf16[1024,128]{1,0:T(8,128)(2,1)} %param.8) | copy-start | bytes 786436
  7.2 133.9 %all-reduce.3.cloned.1.call-start = ((), (), s32[]{:S(2)}) async-start(), calls=%async_computation.1 | async-start | bytes 1048576 | tf_op jit(solution)/shard_map/psum | solution.py:62
  22.8 188.6 %all-reduce.5.cloned.1.call-start = ((), (), s32[]{:S(2)}) async-start(), calls=%async_computation.2 | async-start | bytes 131072 | tf_op jit(solution)/shard_map/psum | solution.py:63
  141.1 94.9 %copy-start.1 = (f32[1024,128]{1,0:T(8,128)S(1)}, f32[1024,128]{1,0:T(8,128)}, u32[]{:S(2)}) copy-start(f32[1024,128]{1,0:T(8,128)} %all-reduce.3.cloned.1.call-done) | copy-start | bytes 1572868
  144.0 130.4 %reduce-scatter.2.cloned.1.call-start = ((), (), s32[]{:S(2)}) async-start(), calls=%async_computation.3 | async-start | bytes 589824 | tf_op jit(solution)/shard_map/reduce_scatter | solution.py:74
Sparse Core Ops, SparseCore 0:
  22.9 118.1 all-reduce.2
  144.1 67.1 all-reduce.4
  238.0 36.3 reduce-scatter.1

commit v2 on v1

--- a/solution.py
+++ b/solution.py
@@ -14,6 +14,55 @@
 TWO_PI = 2.0 * math.pi
 INFL_RATE = 4.5
 DEFOCUS_RATE = 6.0
+
+
+def rows_for(lines, count):
+    spare = -len(lines) % count
+    return jnp.pad(lines, [(0, spare)] + [(0, 0)] * (lines.ndim - 1))
+
+
+def sent_to_all(value, axis):
+    copies = jnp.broadcast_to(value, (lax.axis_size(axis), *value.shape))
+    return lax.all_to_all(copies, axis, split_axis=0, concat_axis=0, tiled=True)
+
+
+def laid_out(parts, dim):
+    shape = list(parts.shape[1:])
+    shape[dim] *= parts.shape[0]
+    return jnp.moveaxis(parts, 0, dim).reshape(shape)
+
+
+def collect(value, axis, dim):
+    parts = sent_to_all(value, axis)
+    return laid_out(parts, dim)
+
+
+def in_blocks(value, dim, count):
+    before, after = (value.shape[:dim], value.shape[dim + 1 :])
+    return jnp.moveaxis(value.reshape(*before, count, -1, *after), dim, 0)
+
+
+def summed_on_arrival(value, axis, dim):
+    parts = in_blocks(value, dim, lax.axis_size(axis))
+    arrived = lax.all_to_all(parts, axis, split_axis=0, concat_axis=0, tiled=True)
+    return arrived.sum(axis=0)
+
+
+def sum_by_parts(value, axes):
+    lines = value.reshape(-1, value.shape[-1])
+    padded = rows_for(lines, lax.axis_size(axes))
+    whole = collect(summed_on_arrival(padded, axes, 0), axes, 0)
+    return lax.slice_in_dim(whole, 0, len(lines)).reshape(value.shape)
+
+
+def butterfly_sum(value, axis):
+    count = lax.axis_size(axis)
+    step = 1
+    while step < count:
+        pairs = [(i, i ^ step) for i in range(count)]
+        value = value + lax.ppermute(value, axis, pairs)
+        step *= 2
+    return value
 
 
 def jacobian_planes(pixels, wave_scale, flux_level, codes, field_re, field_im):
@@ -59,8 +108,8 @@
     )
     jac = jnp.concatenate([real_rows, imag_rows], axis=0)
     partial_sketch = jnp.dot(jac, omega, preferred_element_type=jnp.float32)
-    sketch = lax.psum(partial_sketch, "act")
-    gram_matrix = lax.psum(gram_of(sketch), "pix")
+    sketch = sum_by_parts(partial_sketch, "act")
+    gram_matrix = butterfly_sum(gram_of(sketch), "pix")
     lower_factor = jnp.linalg.cholesky(gram_matrix)
     basis = jax.scipy.linalg.solve_triangular(lower_factor, sketch.T, lower=True).T
     first = lax.axis_index("act") * share_pix
@@ -71,7 +120,7 @@
     partial_value = lax.dot_general(
         coarse, jac, (((0,), (0,)), ((), ())), preferred_element_type=jnp.float32
     )
-    projection = lax.psum_scatter(partial_value, "pix", scatter_dimension=0, tiled=True)
+    projection = summed_on_arrival(partial_value, "pix", 0)
     basis_out = (own_basis * math.sqrt(total_rows)).reshape(1, 2 * share_pix, RANK)
     r_factor = lower_factor.T / math.sqrt(total_rows * ACT)
     return (basis_out, projection, r_factor)

time: 285 us -> 119 us (0.42); the launches traced: 281 us -> 118 us
  waiting for transfers between devices: 221 us -> 20.7 us
  blocking collectives: 0 us -> 35 us
  starting transfers between devices: 0.12 us -> 19.3 us
  between operations: 15.2 us -> 2.08 us
    psum x2 -> x0, waiting for transfers between devices: 186 us -> none  [the longest x1 118 us: on_device(): sketch = lax.psum(partial_sketch, 'act')]
    reduce_scatter x1 -> x0, waiting for transfers between devices: 35.2 us -> none  [on_device(): lax.psum_scatter(partial_value, 'pix', scatter_dimension=0, tiled=True)]
    all_to_all x0 -> x2, blocking collectives: none -> 35 us  [the longest x1 20 us: summed_on_arrival(): lax.all_to_all(parts, axis, split_axis=0, concat_axis=0, tiled=True)]
    all_to_all x0 -> x1, waiting for transfers between devices: none -> 14.2 us  [summed_on_arrival(): lax.all_to_all(parts, axis, split_axis=0, concat_axis=0, tiled=True)]
    ppermute x0 -> x3, starting transfers between devices: none -> 12.4 us  [butterfly_sum(): value = value + lax.ppermute(value, axis, pairs)]
    all_to_all x0 -> x1, starting transfers between devices: none -> 6.86 us  [summed_on_arrival(): lax.all_to_all(parts, axis, split_axis=0, concat_axis=0, tiled=True)]
    ppermute x0 -> x3, waiting for transfers between devices: none -> 6.48 us  [butterfly_sum(): value = value + lax.ppermute(value, axis, pairs)]
  transfers between devices with their start and end apart: 3 -> 4, of which waited for: 3 -> 4; matrix products, arithmetic and copies ran while one was open for 0% -> 1% of each run, Pallas kernels for 0% -> 0%
where the time goes in v2:
time: 119 us; the launch traced here: 118 us
  other arithmetic  36.1 us (30%)
  blocking collectives  35 us (29%)
  waiting for transfers between devices  20.7 us (17%)
  starting transfers between devices  19.3 us (16%)
  matrix products  3.54 us (3%)
  between operations  2.08 us (2%)
  local copies, waits for them, and re-layouts  1.66 us (1%)
    all_to_all x1, blocking collectives, summed_on_arrival(): lax.all_to_all(parts, axis, split_axis=0, concat_axis=0, tiled=True)  20 us
    all_to_all x1, blocking collectives, sent_to_all(): return lax.all_to_all(copies, axis, split_axis=0, concat_axis=0, tiled=True)  15 us
    all_to_all x1, waiting for transfers between devices, summed_on_arrival(): lax.all_to_all(parts, axis, split_axis=0, concat_axis=0, tiled=True)  14.2 us
    ppermute x3, starting transfers between devices, butterfly_sum(): value = value + lax.ppermute(value, axis, pairs)  12.4 us
    another operation x3, other arithmetic, on_device(): lower_factor = jnp.linalg.cholesky(gram_matrix)  12.4 us
    another operation x1, other arithmetic, on_device(): jax.scipy.linalg.solve_triangular(lower_factor, sketch.T, lower=True)  9.81 us
    convert_element_type x1, other arithmetic, jacobian_planes(): return (real_part.astype(jnp.bfloat16), imag_part.astype(jnp.bfloat16))  9.06 us
    all_to_all x1, starting transfers between devices, summed_on_arrival(): lax.all_to_all(parts, axis, split_axis=0, concat_axis=0, tiled=True)  6.86 us
  transfers between devices with their start and end apart: 4, of which 4 were waited for; matrix products, arithmetic and copies ran while one was open for 1% of the time, Pallas kernels for 0%

profile of v2, /device:TPU:1, one launch (start us, length us, event | category | flops | bytes accessed | tf_op | source)
XLA Modules:
  0.0 118.4 jit_solution(1458462496036863031)
XLA Ops:
  1.3 0.7 fusion.16
  2.0 0.7 exponential_multiply_fusion
  3.4 0.7 fusion.9
  4.1 0.8 fusion.21
  4.9 0.7 multiply_divide_fusion
  5.6 9.1 %multiply_convert_fusion.1 = (bf16[512,1024]{1,0:T(8,128)(2,1)S(1)}, bf16[512,1024]{1,0:T(8,128)(2,1)S(1)}) fusion(f32[1024]{0:T(1024)S(1)} %bitcast.41, s32[1024]{0:T(1024)S(1)} %get-tuple-element.17, s32[512]{0:T(512)S(1)} %fusion.16, s32[1024]{0:T(1024)S(1)} %get-tuple-element.18, s32[512]{0:T(512)S(1)} %get-tuple-element.7, f32[]{:T(128)S(6)} %mul_shard_map.3, ...), kind=kLoop, calls=%fused_computation.2 | loop fusion | flops 8912896 | bytes 2125828 | tf_op jit(solution)/shard_map/convert_element_type | solution.py:85
  14.7 0.7 fusion.3
  15.4 20.0 %all_to_all.15 = f32[32,32,128]{2,1,0:T(8,128)S(1)} all-to-all(f32[32,32,128]{2,1,0:T(8,128)S(1)} %bitcast.34), channel_id=1, replica_groups=mesh['act'=32,'pix'=8] {'act'}, dimensions={0} | all-to-all | bytes 1048576 | tf_op jit(solution)/shard_map/all_to_all | solution.py:47
  35.4 15.0 %all_to_all.16 = f32[32,32,128]{2,1,0:T(8,128)S(1)} all-to-all(f32[32,32,128]{2,1,0:T(8,128)S(1)} %broadcast_in_dim.3), channel_id=1, replica_groups=mesh['act'=32,'pix'=8] {'act'}, dimensions={0} | all-to-all | bytes 1048576 | tf_op jit(solution)/shard_map/all_to_all | solution.py:26
  50.5 1.0 convolution_bitcast_fusion
  51.5 1.7 %collective-permute-start = (f32[128,128]{0,1:T(8,128)S(1)}, f32[128,128]{0,1:T(8,128)S(1)}, u32[]{:S(2)}, u32[]{:S(2)}) collective-permute-start(f32[128,128]{0,1:T(8,128)S(1)} %convolution_bitcast_fusion), channel_id=1, source_target_pairs={{0,1},{1,0},{2,3},{3,2},{4,5},{5,4},{6,7},{7,6},{8,9},{9,8},{10,11... | collective-permute-start | bytes 196616 | tf_op jit(solution)/shard_map/ppermute | solution.py:63
  53.2 2.6 %collective-permute-done = f32[128,128]{0,1:T(8,128)S(1)} collective-permute-done((f32[128,128]{0,1:T(8,128)S(1)}, f32[128,128]{0,1:T(8,128)S(1)}, u32[]{:S(2)}, u32[]{:S(2)}) %collective-permute-start) | collective-permute-done | bytes 65568 | tf_op jit(solution)/shard_map/ppermute | solution.py:63
  55.8 3.1 %collective-permute-start.1 = (f32[128,128]{0,1:T(8,128)S(1)}, f32[128,128]{0,1:T(8,128)S(1)}, u32[]{:S(2)}, u32[]{:S(2)}) collective-permute-start(f32[128,128]{0,1:T(8,128)S(1)} %add.114), channel_id=1, source_target_pairs={{0,2},{1,3},{2,0},{3,1},{4,6},{5,7},{6,4},{7,5},{8,10},{9,11},{10,... | collective-permute-start | bytes 196616 | tf_op jit(solution)/shard_map/ppermute | solution.py:63
  58.9 2.1 %collective-permute-done.1 = f32[128,128]{0,1:T(8,128)S(1)} collective-permute-done((f32[128,128]{0,1:T(8,128)S(1)}, f32[128,128]{0,1:T(8,128)S(1)}, u32[]{:S(2)}, u32[]{:S(2)}) %collective-permute-start.1) | collective-permute-done | bytes 65568 | tf_op jit(solution)/shard_map/ppermute | solution.py:63
  61.0 7.6 %collective-permute-start.2 = (f32[128,128]{0,1:T(8,128)S(1)}, f32[128,128]{0,1:T(8,128)S(1)}, u32[]{:S(2)}, u32[]{:S(2)}) collective-permute-start(f32[128,128]{0,1:T(8,128)S(1)} %add.115), channel_id=1, source_target_pairs={{0,4},{1,5},{2,6},{3,7},{4,0},{5,1},{6,2},{7,3},{8,12},{9,13},{10,... | collective-permute-start | bytes 196616 | tf_op jit(solution)/shard_map/ppermute | solution.py:63
  68.6 1.8 %collective-permute-done.2 = f32[128,128]{0,1:T(8,128)S(1)} collective-permute-done((f32[128,128]{0,1:T(8,128)S(1)}, f32[128,128]{0,1:T(8,128)S(1)}, u32[]{:S(2)}, u32[]{:S(2)}) %collective-permute-start.2) | collective-permute-done | bytes 65568 | tf_op jit(solution)/shard_map/ppermute | solution.py:63
  70.5 11.7 %cholesky.16 = f32[128,128]{1,0:T(8,128)S(1)} custom-call(f32[128,128]{1,0:T(8,128)S(1)} %fusion.7), custom_call_target="Cholesky" | custom-call | tf_op jit(solution)/shard_map/jit(cholesky)/cholesky | solution.py:113
  82.9 0.7 multiply_bitcast_fusion
  83.6 9.8 %custom-call.7 = f32[1,128,128]{1,2,0:T(8,128)S(1)} custom-call(f32[1,128,128]{2,1,0:T(8,128)S(1)} %get-tuple-element.11), custom_call_target="InvertDiagBlocksLowerTriangular" | custom-call | tf_op jit(solution)/shard_map/jit(_solve_triangular)/triangular_solve | solution.py:114
  94.0 1.3 %fusion.2 = f32[128,1024]{1,0:T(8,128)} fusion(bf16[512,1024]{1,0:T(8,128)(2,1)S(1)} %get-tuple-element.13, bf16[512,1024]{1,0:T(8,128)(2,1)S(1)} %get-tuple-element.12, f32[1024,128]{1,0:T(8,128)S(1)} %fusion.5), kind=kOutput, calls=%fused_computation.6 | convolution fusion | flops 272760832 | bytes 3145728 | tf_op jit(solution)/shard_map/dot_general | solution.py:120
  95.2 6.9 %all-to-all-start.2 = ((f32[8,16,1024]{2,1,0:T(8,128)}), f32[8,16,1024]{2,1,0:T(8,128)S(1)}, u32[]{:S(2)}, u32[]{:S(2)}) async-start(f32[8,16,1024]{2,1,0:T(8,128)} %bitcast.16), calls=%async_computation.2 | async-start | bytes 1048576 | tf_op jit(solution)/shard_map/all_to_all | solution.py:47
  102.1 0.7 copy.12
  103.5 14.2 %all-to-all-done.2 = f32[8,16,1024]{2,1,0:T(8,128)S(1)} async-done(((f32[8,16,1024]{2,1,0:T(8,128)}), f32[8,16,1024]{2,1,0:T(8,128)S(1)}, u32[]{:S(2)}, u32[]{:S(2)}) %all-to-all-start.2) | async-done | bytes 524320 | tf_op jit(solution)/shard_map/all_to_all | solution.py:47
  117.7 0.7 reduce_sum.19
  (14 shorter events, 2.1 us)
Async XLA Ops:
  0.6 14.0 %copy-start = (bf16[1024,128]{1,0:T(8,128)(2,1)S(1)}, bf16[1024,128]{1,0:T(8,128)(2,1)}, u32[]{:S(2)}) copy-start(bf16[1024,128]{1,0:T(8,128)(2,1)} %param.8) | copy-start | bytes 786436
  51.5 4.4 %collective-permute-start = (f32[128,128]{0,1:T(8,128)S(1)}, f32[128,128]{0,1:T(8,128)S(1)}, u32[]{:S(2)}, u32[]{:S(2)}) collective-permute-start(f32[128,128]{0,1:T(8,128)S(1)} %convolution_bitcast_fusion), channel_id=1, source_target_pairs={{0,1},{1,0},{2,3},{3,2},{4,5},{5,4},{6,7},{7,6},{8,9},{9,8},{10,11... | collective-permute-start | bytes 196616 | tf_op jit(solution)/shard_map/ppermute | solution.py:63
  55.8 5.2 %collective-permute-start.1 = (f32[128,128]{0,1:T(8,128)S(1)}, f32[128,128]{0,1:T(8,128)S(1)}, u32[]{:S(2)}, u32[]{:S(2)}) collective-permute-start(f32[128,128]{0,1:T(8,128)S(1)} %add.114), channel_id=1, source_target_pairs={{0,2},{1,3},{2,0},{3,1},{4,6},{5,7},{6,4},{7,5},{8,10},{9,11},{10,... | collective-permute-start | bytes 196616 | tf_op jit(solution)/shard_map/ppermute | solution.py:63
  61.0 9.4 %collective-permute-start.2 = (f32[128,128]{0,1:T(8,128)S(1)}, f32[128,128]{0,1:T(8,128)S(1)}, u32[]{:S(2)}, u32[]{:S(2)}) collective-permute-start(f32[128,128]{0,1:T(8,128)S(1)} %add.115), channel_id=1, source_target_pairs={{0,4},{1,5},{2,6},{3,7},{4,0},{5,1},{6,2},{7,3},{8,12},{9,13},{10,... | collective-permute-start | bytes 196616 | tf_op jit(solution)/shard_map/ppermute | solution.py:63
  95.2 22.5 %all-to-all-start.2 = ((f32[8,16,1024]{2,1,0:T(8,128)}), f32[8,16,1024]{2,1,0:T(8,128)S(1)}, u32[]{:S(2)}, u32[]{:S(2)}) async-start(f32[8,16,1024]{2,1,0:T(8,128)} %bitcast.16), calls=%async_computation.2 | async-start | bytes 1048576 | tf_op jit(solution)/shard_map/all_to_all | solution.py:47

commit v3 on v2

--- a/solution.py
+++ b/solution.py
@@ -3,6 +3,8 @@
 import jax
 import jax.numpy as jnp
 from jax import lax
+from jax.experimental import pallas as pl
+from jax.experimental.pallas import tpu as pltpu
 from jax.sharding import PartitionSpec as P
 
 GRID = 128
@@ -65,6 +67,46 @@
     return value
 
 
+def chol_inv_kernel(g_ref, lt_ref, inv_ref):
+    n = g_ref.shape[0]
+    lt_ref[...] = g_ref[...]
+    rows = lax.broadcasted_iota(jnp.int32, (n, n), 0)
+    cols = lax.broadcasted_iota(jnp.int32, (n, n), 1)
+    inv_ref[...] = jnp.where(rows == cols, 1.0, 0.0).astype(jnp.float32)
+    lane = lax.broadcasted_iota(jnp.int32, (1, n), 1)
+    sub = lax.broadcasted_iota(jnp.int32, (n, 1), 0)
+
+    def step(j, carry):
+        a = lt_ref[...]
+        row = lt_ref[pl.ds(j, 1), :]
+        d = jnp.sum(jnp.where(lane == j, row, 0.0), axis=1, keepdims=True)
+        r = lax.rsqrt(d)
+        l = jnp.where(lane >= j, row * r, 0.0)
+        colj = jnp.sum(jnp.where(cols == j, a, 0.0), axis=1, keepdims=True)
+        c = jnp.where(sub > j, colj * r, 0.0)
+        b_row = inv_ref[pl.ds(j, 1), :] * r
+        lt_ref[...] = a - c * l
+        inv_ref[...] = inv_ref[...] - c * b_row
+        lt_ref[pl.ds(j, 1), :] = l
+        inv_ref[pl.ds(j, 1), :] = b_row
+        return carry
+
+    lax.fori_loop(0, n, step, 0)
+
+
+def chol_inv(g):
+    n = g.shape[0]
+    return pl.pallas_call(
+        chol_inv_kernel,
+        out_shape=(
+            jax.ShapeDtypeStruct((n, n), jnp.float32),
+            jax.ShapeDtypeStruct((n, n), jnp.float32),
+        ),
+        in_specs=[pl.BlockSpec(memory_space=pltpu.VMEM)],
+        out_specs=(pl.BlockSpec(memory_space=pltpu.VMEM), pl.BlockSpec(memory_space=pltpu.VMEM)),
+    )(g)
+
+
 def jacobian_planes(pixels, wave_scale, flux_level, codes, field_re, field_im):
     delta_u = pixels // FOCAL - FOCAL // 2
     delta_v = pixels % FOCAL - FOCAL // 2
@@ -110,8 +152,14 @@
     partial_sketch = jnp.dot(jac, omega, preferred_element_type=jnp.float32)
     sketch = sum_by_parts(partial_sketch, "act")
     gram_matrix = butterfly_sum(gram_of(sketch), "pix")
-    lower_factor = jnp.linalg.cholesky(gram_matrix)
-    basis = jax.scipy.linalg.solve_triangular(lower_factor, sketch.T, lower=True).T
+    upper_factor, lower_inverse = chol_inv(gram_matrix)
+    basis = lax.dot_general(
+        sketch,
+        lower_inverse,
+        (((1,), (1,)), ((), ())),
+        precision=lax.Precision.HIGHEST,
+        preferred_element_type=jnp.float32,
+    )
     first = lax.axis_index("act") * share_pix
     own_re = lax.dynamic_slice_in_dim(basis, first, share_pix, 0)
     own_im = lax.dynamic_slice_in_dim(basis, npix + first, share_pix, 0)
@@ -122,7 +170,7 @@
     )
     projection = summed_on_arrival(partial_value, "pix", 0)
     basis_out = (own_basis * math.sqrt(total_rows)).reshape(1, 2 * share_pix, RANK)
-    r_factor = lower_factor.T / math.sqrt(total_rows * ACT)
+    r_factor = upper_factor / math.sqrt(total_rows * ACT)
     return (basis_out, projection, r_factor)
 
 

time: 119 us -> 112 us (0.941)
  other arithmetic: 36.1 us -> 14.5 us
  Pallas kernels: 0 us -> 14.9 us
    another operation x4 -> x0, other arithmetic: 22.2 us -> none  [the longest x3 12.4 us: on_device(): lower_factor = jnp.linalg.cholesky(gram_matrix)]
    pallas_call x0 -> x1, Pallas kernels: none -> 14.9 us  [chol_inv(): pl.pallas_call(chol_inv_kernel, out_shape=(jax.ShapeDtypeStruct((n, n), j...]
    dot_general x0 -> x1, matrix products: none -> 1.41 us  [on_device(): lax.dot_general(sketch, lower_inverse, (((1,), (1,)), ((), ())), precisio...]
where the time goes in v3:
time: 112 us
  blocking collectives  35 us (31%)
  waiting for transfers between devices  20.8 us (19%)
  starting transfers between devices  19.3 us (17%)
  Pallas kernels  14.9 us (13%)
  other arithmetic  14.5 us (13%)
  matrix products  4.39 us (4%)
  between operations  2.05 us (2%)
    all_to_all x1, blocking collectives, summed_on_arrival(): lax.all_to_all(parts, axis, split_axis=0, concat_axis=0, tiled=True)  20 us
    all_to_all x1, blocking collectives, sent_to_all(): return lax.all_to_all(copies, axis, split_axis=0, concat_axis=0, tiled=True)  15 us
    pallas_call x1, Pallas kernels, chol_inv(): pl.pallas_call(chol_inv_kernel, out_shape=(jax.ShapeDtypeStruct((n, n), j...  14.9 us
    all_to_all x1, waiting for transfers between devices, summed_on_arrival(): lax.all_to_all(parts, axis, split_axis=0, concat_axis=0, tiled=True)  14.3 us
    ppermute x3, starting transfers between devices, butterfly_sum(): value = value + lax.ppermute(value, axis, pairs)  12.2 us
    convert_element_type x1, other arithmetic, jacobian_planes(): return (real_part.astype(jnp.bfloat16), imag_part.astype(jnp.bfloat16))  9.06 us
    all_to_all x1, starting transfers between devices, summed_on_arrival(): lax.all_to_all(parts, axis, split_axis=0, concat_axis=0, tiled=True)  7.01 us
    ppermute x3, waiting for transfers between devices, butterfly_sum(): value = value + lax.ppermute(value, axis, pairs)  6.48 us
  transfers between devices with their start and end apart: 4, of which 4 were waited for; matrix products, arithmetic and copies ran while one was open for 1% of the time, Pallas kernels for 0%

profile of v3, /device:TPU:1, one launch (start us, length us, event | category | flops | bytes accessed | tf_op | source)
XLA Modules:
  0.0 111.8 jit_solution(6763525303862220427)
XLA Ops:
  1.3 0.7 fusion.13
  2.0 0.7 exponential_multiply_fusion
  3.4 0.7 fusion.6
  4.1 0.8 fusion.18
  4.9 0.7 multiply_divide_fusion
  5.6 9.1 %multiply_convert_fusion.1 = (bf16[512,1024]{1,0:T(8,128)(2,1)S(1)}, bf16[512,1024]{1,0:T(8,128)(2,1)S(1)}) fusion(f32[1024]{0:T(1024)S(1)} %bitcast.29, s32[1024]{0:T(1024)S(1)} %get-tuple-element.16, s32[512]{0:T(512)S(1)} %fusion.13, s32[1024]{0:T(1024)S(1)} %get-tuple-element.17, s32[512]{0:T(512)S(1)} %get-tuple-element.8, f32[]{:T(128)S(6)} %mul_shard_map.3, ...), kind=kLoop, calls=%fused_computation.2 | loop fusion | flops 8912896 | bytes 2125828 | tf_op jit(solution)/shard_map/convert_element_type | solution.py:127
  14.7 0.7 fusion.3
  15.4 20.0 %all_to_all.15 = f32[32,32,128]{2,1,0:T(8,128)S(1)} all-to-all(f32[32,32,128]{2,1,0:T(8,128)S(1)} %bitcast.22), channel_id=1, replica_groups=mesh['act'=32,'pix'=8] {'act'}, dimensions={0} | all-to-all | bytes 1048576 | tf_op jit(solution)/shard_map/all_to_all | solution.py:49
  35.4 15.0 %all_to_all.16 = f32[32,32,128]{2,1,0:T(8,128)S(1)} all-to-all(f32[32,32,128]{2,1,0:T(8,128)S(1)} %broadcast_in_dim.2), channel_id=1, replica_groups=mesh['act'=32,'pix'=8] {'act'}, dimensions={0} | all-to-all | bytes 1048576 | tf_op jit(solution)/shard_map/all_to_all | solution.py:28
  50.5 1.0 convolution_bitcast_fusion
  51.5 1.7 %collective-permute-start = (f32[128,128]{1,0:T(8,128)S(1)}, f32[128,128]{1,0:T(8,128)S(1)}, u32[]{:S(2)}, u32[]{:S(2)}) collective-permute-start(f32[128,128]{1,0:T(8,128)S(1)} %convolution_bitcast_fusion), channel_id=1, source_target_pairs={{0,1},{1,0},{2,3},{3,2},{4,5},{5,4},{6,7},{7,6},{8,9},{9,8},{10,11... | collective-permute-start | bytes 196616 | tf_op jit(solution)/shard_map/ppermute | solution.py:65
  53.2 2.6 %collective-permute-done = f32[128,128]{1,0:T(8,128)S(1)} collective-permute-done((f32[128,128]{1,0:T(8,128)S(1)}, f32[128,128]{1,0:T(8,128)S(1)}, u32[]{:S(2)}, u32[]{:S(2)}) %collective-permute-start) | collective-permute-done | bytes 65568 | tf_op jit(solution)/shard_map/ppermute | solution.py:65
  55.9 3.1 %collective-permute-start.1 = (f32[128,128]{1,0:T(8,128)S(1)}, f32[128,128]{1,0:T(8,128)S(1)}, u32[]{:S(2)}, u32[]{:S(2)}) collective-permute-start(f32[128,128]{1,0:T(8,128)S(1)} %add.102), channel_id=1, source_target_pairs={{0,2},{1,3},{2,0},{3,1},{4,6},{5,7},{6,4},{7,5},{8,10},{9,11},{10,... | collective-permute-start | bytes 196616 | tf_op jit(solution)/shard_map/ppermute | solution.py:65
  58.9 2.1 %collective-permute-done.1 = f32[128,128]{1,0:T(8,128)S(1)} collective-permute-done((f32[128,128]{1,0:T(8,128)S(1)}, f32[128,128]{1,0:T(8,128)S(1)}, u32[]{:S(2)}, u32[]{:S(2)}) %collective-permute-start.1) | collective-permute-done | bytes 65568 | tf_op jit(solution)/shard_map/ppermute | solution.py:65
  61.0 7.4 %collective-permute-start.2 = (f32[128,128]{1,0:T(8,128)S(1)}, f32[128,128]{1,0:T(8,128)S(1)}, u32[]{:S(2)}, u32[]{:S(2)}) collective-permute-start(f32[128,128]{1,0:T(8,128)S(1)} %add.103), channel_id=1, source_target_pairs={{0,4},{1,5},{2,6},{3,7},{4,0},{5,1},{6,2},{7,3},{8,12},{9,13},{10,... | collective-permute-start | bytes 196616 | tf_op jit(solution)/shard_map/ppermute | solution.py:65
  68.5 1.8 %collective-permute-done.2 = f32[128,128]{1,0:T(8,128)S(1)} collective-permute-done((f32[128,128]{1,0:T(8,128)S(1)}, f32[128,128]{1,0:T(8,128)S(1)}, u32[]{:S(2)}, u32[]{:S(2)}) %collective-permute-start.2) | collective-permute-done | bytes 65568 | tf_op jit(solution)/shard_map/ppermute | solution.py:65
  70.2 0.6 add.104.g_ref
  70.9 14.9 %shard_map.85 = (f32[128,128]{1,0:T(8,128)}, f32[128,128]{1,0:T(8,128)}) custom-call(f32[128,128]{1,0:T(8,128)} %add.104.g_ref), custom_call_target="tpu_custom_call" | custom-call | tf_op jit(solution)/shard_map/pallas_call | solution.py:99
  85.8 1.4 %fusion.19 = f32[1024,128]{1,0:T(8,128)S(1)} fusion(f32[1024,128]{1,0:T(8,128)S(1)} %bitcast.21, f32[128,128]{1,0:T(8,128)} %get-tuple-element.5), kind=kOutput, calls=%fused_computation.49 | convolution fusion | flops 201326592 | bytes 1114112 | tf_op jit(solution)/shard_map/dot_general | solution.py:156
  87.2 1.3 %fusion.2 = f32[128,1024]{1,0:T(8,128)} fusion(bf16[512,1024]{1,0:T(8,128)(2,1)S(1)} %get-tuple-element.12, bf16[512,1024]{1,0:T(8,128)(2,1)S(1)} %get-tuple-element.11, f32[1024,128]{1,0:T(8,128)S(1)} %fusion.19), kind=kOutput, calls=%fused_computation.6 | convolution fusion | flops 272760832 | bytes 3145728 | tf_op jit(solution)/shard_map/dot_general | solution.py:168
  88.5 7.0 %all-to-all-start.2 = ((f32[8,16,1024]{2,1,0:T(8,128)}), f32[8,16,1024]{2,1,0:T(8,128)S(1)}, u32[]{:S(2)}, u32[]{:S(2)}) async-start(f32[8,16,1024]{2,1,0:T(8,128)} %bitcast.11), calls=%async_computation.2 | async-start | bytes 1048576 | tf_op jit(solution)/shard_map/all_to_all | solution.py:49
  96.1 0.6 broadcast_multiply_fusion
  96.8 14.3 %all-to-all-done.2 = f32[8,16,1024]{2,1,0:T(8,128)S(1)} async-done(((f32[8,16,1024]{2,1,0:T(8,128)}), f32[8,16,1024]{2,1,0:T(8,128)S(1)}, u32[]{:S(2)}, u32[]{:S(2)}) %all-to-all-start.2) | async-done | bytes 524320 | tf_op jit(solution)/shard_map/all_to_all | solution.py:49
  111.1 0.7 reduce_sum.19
  (10 shorter events, 0.8 us)
Async XLA Ops:
  0.6 14.0 %copy-start = (bf16[1024,128]{1,0:T(8,128)(2,1)S(1)}, bf16[1024,128]{1,0:T(8,128)(2,1)}, u32[]{:S(2)}) copy-start(bf16[1024,128]{1,0:T(8,128)(2,1)} %param.8) | copy-start | bytes 786436
  51.5 4.4 %collective-permute-start = (f32[128,128]{1,0:T(8,128)S(1)}, f32[128,128]{1,0:T(8,128)S(1)}, u32[]{:S(2)}, u32[]{:S(2)}) collective-permute-start(f32[128,128]{1,0:T(8,128)S(1)} %convolution_bitcast_fusion), channel_id=1, source_target_pairs={{0,1},{1,0},{2,3},{3,2},{4,5},{5,4},{6,7},{7,6},{8,9},{9,8},{10,11... | collective-permute-start | bytes 196616 | tf_op jit(solution)/shard_map/ppermute | solution.py:65
  55.9 5.1 %collective-permute-start.1 = (f32[128,128]{1,0:T(8,128)S(1)}, f32[128,128]{1,0:T(8,128)S(1)}, u32[]{:S(2)}, u32[]{:S(2)}) collective-permute-start(f32[128,128]{1,0:T(8,128)S(1)} %add.102), channel_id=1, source_target_pairs={{0,2},{1,3},{2,0},{3,1},{4,6},{5,7},{6,4},{7,5},{8,10},{9,11},{10,... | collective-permute-start | bytes 196616 | tf_op jit(solution)/shard_map/ppermute | solution.py:65
  61.0 9.2 %collective-permute-start.2 = (f32[128,128]{1,0:T(8,128)S(1)}, f32[128,128]{1,0:T(8,128)S(1)}, u32[]{:S(2)}, u32[]{:S(2)}) collective-permute-start(f32[128,128]{1,0:T(8,128)S(1)} %add.103), channel_id=1, source_target_pairs={{0,4},{1,5},{2,6},{3,7},{4,0},{5,1},{6,2},{7,3},{8,12},{9,13},{10,... | collective-permute-start | bytes 196616 | tf_op jit(solution)/shard_map/ppermute | solution.py:65
  88.5 7.6 %copy-start.1 = (f32[128,128]{1,0:T(8,128)S(1)}, f32[128,128]{1,0:T(8,128)}, u32[]{:S(2)}) copy-start(f32[128,128]{1,0:T(8,128)} %get-tuple-element.6) | copy-start | bytes 196612
  88.5 22.6 %all-to-all-start.2 = ((f32[8,16,1024]{2,1,0:T(8,128)}), f32[8,16,1024]{2,1,0:T(8,128)S(1)}, u32[]{:S(2)}, u32[]{:S(2)}) async-start(f32[8,16,1024]{2,1,0:T(8,128)} %bitcast.11), calls=%async_computation.2 | async-start | bytes 1048576 | tf_op jit(solution)/shard_map/all_to_all | solution.py:49

commit v4 on v3

--- a/solution.py
+++ b/solution.py
@@ -75,23 +75,20 @@
     inv_ref[...] = jnp.where(rows == cols, 1.0, 0.0).astype(jnp.float32)
     lane = lax.broadcasted_iota(jnp.int32, (1, n), 1)
     sub = lax.broadcasted_iota(jnp.int32, (n, 1), 0)
-
-    def step(j, carry):
-        a = lt_ref[...]
-        row = lt_ref[pl.ds(j, 1), :]
+    for j in range(n):
+        row = lt_ref[j : j + 1, :]
         d = jnp.sum(jnp.where(lane == j, row, 0.0), axis=1, keepdims=True)
         r = lax.rsqrt(d)
         l = jnp.where(lane >= j, row * r, 0.0)
-        colj = jnp.sum(jnp.where(cols == j, a, 0.0), axis=1, keepdims=True)
-        c = jnp.where(sub > j, colj * r, 0.0)
-        b_row = inv_ref[pl.ds(j, 1), :] * r
-        lt_ref[...] = a - c * l
-        inv_ref[...] = inv_ref[...] - c * b_row
-        lt_ref[pl.ds(j, 1), :] = l
-        inv_ref[pl.ds(j, 1), :] = b_row
-        return carry
-
-    lax.fori_loop(0, n, step, 0)
+        b_row = inv_ref[j : j + 1, :] * r
+        if j + 1 < n:
+            t = (j + 1) // 8 * 8
+            col = jnp.broadcast_to(l, (8, n)).T[:, 0:1]
+            c = jnp.where(sub > j, col, 0.0)[t:]
+            lt_ref[t:, :] = lt_ref[t:, :] - c * l
+            inv_ref[t:, :] = inv_ref[t:, :] - c * b_row
+        lt_ref[j : j + 1, :] = l
+        inv_ref[j : j + 1, :] = b_row
 
 
 def chol_inv(g):

time: 112 us -> 130 us (1.16)
  Pallas kernels: 14.9 us -> 32.5 us
    pallas_call x1, Pallas kernels: 14.9 us -> 32.5 us  [chol_inv(): pl.pallas_call(chol_inv_kernel, out_shape=(jax.ShapeDtypeStruct((n, n), j...]
where the time goes in v4:
time: 130 us; the launch traced here: 129 us
  blocking collectives  35 us (27%)
  Pallas kernels  32.5 us (25%)
  waiting for transfers between devices  20.8 us (16%)
  starting transfers between devices  19.4 us (15%)
  other arithmetic  14.5 us (11%)
  matrix products  4.39 us (3%)
  between operations  2.05 us (2%)
    pallas_call x1, Pallas kernels, chol_inv(): pl.pallas_call(chol_inv_kernel, out_shape=(jax.ShapeDtypeStruct((n, n), j...  32.5 us
    all_to_all x1, blocking collectives, summed_on_arrival(): lax.all_to_all(parts, axis, split_axis=0, concat_axis=0, tiled=True)  20 us
    all_to_all x1, blocking collectives, sent_to_all(): return lax.all_to_all(copies, axis, split_axis=0, concat_axis=0, tiled=True)  15 us
    all_to_all x1, waiting for transfers between devices, summed_on_arrival(): lax.all_to_all(parts, axis, split_axis=0, concat_axis=0, tiled=True)  14.3 us
    ppermute x3, starting transfers between devices, butterfly_sum(): value = value + lax.ppermute(value, axis, pairs)  12.4 us
    convert_element_type x1, other arithmetic, jacobian_planes(): return (real_part.astype(jnp.bfloat16), imag_part.astype(jnp.bfloat16))  9.06 us
    all_to_all x1, starting transfers between devices, summed_on_arrival(): lax.all_to_all(parts, axis, split_axis=0, concat_axis=0, tiled=True)  7 us
    ppermute x3, waiting for transfers between devices, butterfly_sum(): value = value + lax.ppermute(value, axis, pairs)  6.48 us
  transfers between devices with their start and end apart: 4, of which 4 were waited for; matrix products, arithmetic and copies ran while one was open for 1% of the time, Pallas kernels for 0%

profile of v4, /device:TPU:1, one launch (start us, length us, event | category | flops | bytes accessed | tf_op | source)
XLA Modules:
  0.0 129.5 jit_solution(268153541913112929)
XLA Ops:
  1.3 0.7 fusion.13
  2.0 0.7 exponential_multiply_fusion
  3.4 0.7 fusion.6
  4.1 0.8 fusion.18
  4.9 0.7 multiply_divide_fusion
  5.6 9.1 %multiply_convert_fusion.1 = (bf16[512,1024]{1,0:T(8,128)(2,1)S(1)}, bf16[512,1024]{1,0:T(8,128)(2,1)S(1)}) fusion(f32[1024]{0:T(1024)S(1)} %bitcast.29, s32[1024]{0:T(1024)S(1)} %get-tuple-element.16, s32[512]{0:T(512)S(1)} %fusion.13, s32[1024]{0:T(1024)S(1)} %get-tuple-element.17, s32[512]{0:T(512)S(1)} %get-tuple-element.8, f32[]{:T(128)S(6)} %mul_shard_map.3, ...), kind=kLoop, calls=%fused_computation.2 | loop fusion | flops 8912896 | bytes 2125828 | tf_op jit(solution)/shard_map/convert_element_type | solution.py:124
  14.7 0.7 fusion.3
  15.4 20.0 %all_to_all.15 = f32[32,32,128]{2,1,0:T(8,128)S(1)} all-to-all(f32[32,32,128]{2,1,0:T(8,128)S(1)} %bitcast.22), channel_id=1, replica_groups=mesh['act'=32,'pix'=8] {'act'}, dimensions={0} | all-to-all | bytes 1048576 | tf_op jit(solution)/shard_map/all_to_all | solution.py:49
  35.4 15.0 %all_to_all.16 = f32[32,32,128]{2,1,0:T(8,128)S(1)} all-to-all(f32[32,32,128]{2,1,0:T(8,128)S(1)} %broadcast_in_dim.2), channel_id=1, replica_groups=mesh['act'=32,'pix'=8] {'act'}, dimensions={0} | all-to-all | bytes 1048576 | tf_op jit(solution)/shard_map/all_to_all | solution.py:28
  50.5 1.0 convolution_bitcast_fusion
  51.5 1.7 %collective-permute-start = (f32[128,128]{1,0:T(8,128)S(1)}, f32[128,128]{1,0:T(8,128)S(1)}, u32[]{:S(2)}, u32[]{:S(2)}) collective-permute-start(f32[128,128]{1,0:T(8,128)S(1)} %convolution_bitcast_fusion), channel_id=1, source_target_pairs={{0,1},{1,0},{2,3},{3,2},{4,5},{5,4},{6,7},{7,6},{8,9},{9,8},{10,11... | collective-permute-start | bytes 196616 | tf_op jit(solution)/shard_map/ppermute | solution.py:65
  53.2 2.6 %collective-permute-done = f32[128,128]{1,0:T(8,128)S(1)} collective-permute-done((f32[128,128]{1,0:T(8,128)S(1)}, f32[128,128]{1,0:T(8,128)S(1)}, u32[]{:S(2)}, u32[]{:S(2)}) %collective-permute-start) | collective-permute-done | bytes 65568 | tf_op jit(solution)/shard_map/ppermute | solution.py:65
  55.9 3.1 %collective-permute-start.1 = (f32[128,128]{1,0:T(8,128)S(1)}, f32[128,128]{1,0:T(8,128)S(1)}, u32[]{:S(2)}, u32[]{:S(2)}) collective-permute-start(f32[128,128]{1,0:T(8,128)S(1)} %add.102), channel_id=1, source_target_pairs={{0,2},{1,3},{2,0},{3,1},{4,6},{5,7},{6,4},{7,5},{8,10},{9,11},{10,... | collective-permute-start | bytes 196616 | tf_op jit(solution)/shard_map/ppermute | solution.py:65
  58.9 2.1 %collective-permute-done.1 = f32[128,128]{1,0:T(8,128)S(1)} collective-permute-done((f32[128,128]{1,0:T(8,128)S(1)}, f32[128,128]{1,0:T(8,128)S(1)}, u32[]{:S(2)}, u32[]{:S(2)}) %collective-permute-start.1) | collective-permute-done | bytes 65568 | tf_op jit(solution)/shard_map/ppermute | solution.py:65
  61.0 7.6 %collective-permute-start.2 = (f32[128,128]{1,0:T(8,128)S(1)}, f32[128,128]{1,0:T(8,128)S(1)}, u32[]{:S(2)}, u32[]{:S(2)}) collective-permute-start(f32[128,128]{1,0:T(8,128)S(1)} %add.103), channel_id=1, source_target_pairs={{0,4},{1,5},{2,6},{3,7},{4,0},{5,1},{6,2},{7,3},{8,12},{9,13},{10,... | collective-permute-start | bytes 196616 | tf_op jit(solution)/shard_map/ppermute | solution.py:65
  68.6 1.8 %collective-permute-done.2 = f32[128,128]{1,0:T(8,128)S(1)} collective-permute-done((f32[128,128]{1,0:T(8,128)S(1)}, f32[128,128]{1,0:T(8,128)S(1)}, u32[]{:S(2)}, u32[]{:S(2)}) %collective-permute-start.2) | collective-permute-done | bytes 65568 | tf_op jit(solution)/shard_map/ppermute | solution.py:65
  70.4 0.6 add.104.g_ref
  71.0 32.5 %shard_map.85 = (f32[128,128]{1,0:T(8,128)}, f32[128,128]{1,0:T(8,128)}) custom-call(f32[128,128]{1,0:T(8,128)} %add.104.g_ref), custom_call_target="tpu_custom_call" | custom-call | tf_op jit(solution)/shard_map/pallas_call | solution.py:96
  103.5 1.4 %fusion.19 = f32[1024,128]{1,0:T(8,128)S(1)} fusion(f32[1024,128]{1,0:T(8,128)S(1)} %bitcast.21, f32[128,128]{1,0:T(8,128)} %get-tuple-element.5), kind=kOutput, calls=%fused_computation.49 | convolution fusion | flops 201326592 | bytes 1114112 | tf_op jit(solution)/shard_map/dot_general | solution.py:153
  105.0 1.3 fusion.2
  106.2 7.0 %all-to-all-start.2 = ((f32[8,16,1024]{2,1,0:T(8,128)}), f32[8,16,1024]{2,1,0:T(8,128)S(1)}, u32[]{:S(2)}, u32[]{:S(2)}) async-start(f32[8,16,1024]{2,1,0:T(8,128)} %bitcast.11), calls=%async_computation.2 | async-start | bytes 1048576 | tf_op jit(solution)/shard_map/all_to_all | solution.py:49
  113.9 0.6 broadcast_multiply_fusion
  114.5 14.3 %all-to-all-done.2 = f32[8,16,1024]{2,1,0:T(8,128)S(1)} async-done(((f32[8,16,1024]{2,1,0:T(8,128)}), f32[8,16,1024]{2,1,0:T(8,128)S(1)}, u32[]{:S(2)}, u32[]{:S(2)}) %all-to-all-start.2) | async-done | bytes 524320 | tf_op jit(solution)/shard_map/all_to_all | solution.py:49
  128.8 0.7 reduce_sum.19
  (10 shorter events, 0.8 us)
Async XLA Ops:
  0.6 14.0 %copy-start = (bf16[1024,128]{1,0:T(8,128)(2,1)S(1)}, bf16[1024,128]{1,0:T(8,128)(2,1)}, u32[]{:S(2)}) copy-start(bf16[1024,128]{1,0:T(8,128)(2,1)} %param.8) | copy-start | bytes 786436
  51.5 4.4 %collective-permute-start = (f32[128,128]{1,0:T(8,128)S(1)}, f32[128,128]{1,0:T(8,128)S(1)}, u32[]{:S(2)}, u32[]{:S(2)}) collective-permute-start(f32[128,128]{1,0:T(8,128)S(1)} %convolution_bitcast_fusion), channel_id=1, source_target_pairs={{0,1},{1,0},{2,3},{3,2},{4,5},{5,4},{6,7},{7,6},{8,9},{9,8},{10,11... | collective-permute-start | bytes 196616 | tf_op jit(solution)/shard_map/ppermute | solution.py:65
  55.9 5.2 %collective-permute-start.1 = (f32[128,128]{1,0:T(8,128)S(1)}, f32[128,128]{1,0:T(8,128)S(1)}, u32[]{:S(2)}, u32[]{:S(2)}) collective-permute-start(f32[128,128]{1,0:T(8,128)S(1)} %add.102), channel_id=1, source_target_pairs={{0,2},{1,3},{2,0},{3,1},{4,6},{5,7},{6,4},{7,5},{8,10},{9,11},{10,... | collective-permute-start | bytes 196616 | tf_op jit(solution)/shard_map/ppermute | solution.py:65
  61.0 9.4 %collective-permute-start.2 = (f32[128,128]{1,0:T(8,128)S(1)}, f32[128,128]{1,0:T(8,128)S(1)}, u32[]{:S(2)}, u32[]{:S(2)}) collective-permute-start(f32[128,128]{1,0:T(8,128)S(1)} %add.103), channel_id=1, source_target_pairs={{0,4},{1,5},{2,6},{3,7},{4,0},{5,1},{6,2},{7,3},{8,12},{9,13},{10,... | collective-permute-start | bytes 196616 | tf_op jit(solution)/shard_map/ppermute | solution.py:65
  106.2 7.6 %copy-start.1 = (f32[128,128]{1,0:T(8,128)S(1)}, f32[128,128]{1,0:T(8,128)}, u32[]{:S(2)}) copy-start(f32[128,128]{1,0:T(8,128)} %get-tuple-element.6) | copy-start | bytes 196612
  106.2 22.6 %all-to-all-start.2 = ((f32[8,16,1024]{2,1,0:T(8,128)}), f32[8,16,1024]{2,1,0:T(8,128)S(1)}, u32[]{:S(2)}, u32[]{:S(2)}) async-start(f32[8,16,1024]{2,1,0:T(8,128)} %bitcast.11), calls=%async_computation.2 | async-start | bytes 1048576 | tf_op jit(solution)/shard_map/all_to_all | solution.py:49

commit v5 on v3

--- a/solution.py
+++ b/solution.py
@@ -151,24 +151,33 @@
     jac = jnp.concatenate([real_rows, imag_rows], axis=0)
     partial_sketch = jnp.dot(jac, omega, preferred_element_type=jnp.float32)
     sketch = sum_by_parts(partial_sketch, "act")
-    gram_matrix = butterfly_sum(gram_of(sketch), "pix")
+    through = lax.dot_general(
+        sketch,
+        jac,
+        (((0,), (0,)), ((), ())),
+        precision=lax.Precision.HIGH,
+        preferred_element_type=jnp.float32,
+    )
+    summed = butterfly_sum(jnp.concatenate([gram_of(sketch), through], axis=1), "pix")
+    gram_matrix = summed[:, :RANK]
+    through_sum = summed[:, RANK:]
     upper_factor, lower_inverse = chol_inv(gram_matrix)
-    basis = lax.dot_general(
-        sketch,
+    first = lax.axis_index("act") * share_pix
+    own_re = lax.dynamic_slice_in_dim(sketch, first, share_pix, 0)
+    own_im = lax.dynamic_slice_in_dim(sketch, npix + first, share_pix, 0)
+    own_sketch = jnp.stack([own_re, own_im], axis=1).reshape(2 * share_pix, RANK)
+    own_basis = lax.dot_general(
+        own_sketch,
         lower_inverse,
         (((1,), (1,)), ((), ())),
         precision=lax.Precision.HIGHEST,
         preferred_element_type=jnp.float32,
     )
-    first = lax.axis_index("act") * share_pix
-    own_re = lax.dynamic_slice_in_dim(basis, first, share_pix, 0)
-    own_im = lax.dynamic_slice_in_dim(basis, npix + first, share_pix, 0)
-    own_basis = jnp.stack([own_re, own_im], axis=1).reshape(2 * share_pix, RANK)
-    coarse = basis.astype(jnp.bfloat16)
-    partial_value = lax.dot_general(
-        coarse, jac, (((0,), (0,)), ((), ())), preferred_element_type=jnp.float32
-    )
-    projection = summed_on_arrival(partial_value, "pix", 0)
+    rank_rows = RANK // pix_count
+    own_inverse = lax.dynamic_slice_in_dim(lower_inverse, lax.axis_index("pix") * rank_rows, rank_rows, 0)
+    projection = jnp.dot(
+        own_inverse, through_sum, precision=lax.Precision.HIGHEST, preferred_element_type=jnp.float32
+    )
     basis_out = (own_basis * math.sqrt(total_rows)).reshape(1, 2 * share_pix, RANK)
     r_factor = upper_factor / math.sqrt(total_rows * ACT)
     return (basis_out, projection, r_factor)

time: 112 us -> 150 us (1.34)
  waiting for transfers between devices: 20.8 us -> 65.4 us
  starting transfers between devices: 19.3 us -> 10.8 us
    ppermute x3, waiting for transfers between devices: 6.48 us -> 65.4 us  [butterfly_sum(): value = value + lax.ppermute(value, axis, pairs)]
    all_to_all x1 -> x0, waiting for transfers between devices: 14.3 us -> none  [summed_on_arrival(): lax.all_to_all(parts, axis, split_axis=0, concat_axis=0, tiled=True)]
    all_to_all x1 -> x0, starting transfers between devices: 7.01 us -> none  [summed_on_arrival(): lax.all_to_all(parts, axis, split_axis=0, concat_axis=0, tiled=True)]
    dot_general x2 -> x3, matrix products: 2.68 us -> 4.16 us  [the longest x1 1.69 us: on_device(): jnp.dot(own_inverse, through_sum, precision=lax.Precision.HIGHEST, prefer...]
  transfers between devices with their start and end apart: 4 -> 3, of which waited for: 4 -> 3; matrix products, arithmetic and copies ran while one was open for 1% -> 0% of each run, Pallas kernels for 0% -> 0%
where the time goes in v5:
time: 150 us; the launch traced here: 149 us
  waiting for transfers between devices  65.4 us (44%)
  blocking collectives  35 us (23%)
  Pallas kernels  14.9 us (10%)
  other arithmetic  13.6 us (9%)
  starting transfers between devices  10.8 us (7%)
  matrix products  5.87 us (4%)
  between operations  2.06 us (1%)
    ppermute x3, waiting for transfers between devices, butterfly_sum(): value = value + lax.ppermute(value, axis, pairs)  65.4 us
    all_to_all x1, blocking collectives, summed_on_arrival(): lax.all_to_all(parts, axis, split_axis=0, concat_axis=0, tiled=True)  20 us
    all_to_all x1, blocking collectives, sent_to_all(): return lax.all_to_all(copies, axis, split_axis=0, concat_axis=0, tiled=True)  15 us
    pallas_call x1, Pallas kernels, chol_inv(): pl.pallas_call(chol_inv_kernel, out_shape=(jax.ShapeDtypeStruct((n, n), j...  14.9 us
    ppermute x3, starting transfers between devices, butterfly_sum(): value = value + lax.ppermute(value, axis, pairs)  10.8 us
    convert_element_type x1, other arithmetic, jacobian_planes(): return (real_part.astype(jnp.bfloat16), imag_part.astype(jnp.bfloat16))  9.06 us
  transfers between devices with their start and end apart: 3, of which 3 were waited for; matrix products, arithmetic and copies ran while one was open for 0% of the time, Pallas kernels for 0%

profile of v5, /device:TPU:1, one launch (start us, length us, event | category | flops | bytes accessed | tf_op | source)
XLA Modules:
  0.0 149.2 jit_solution(5523640299431226305)
XLA Ops:
  1.3 0.7 fusion.16
  2.0 0.7 exponential_multiply_fusion
  3.4 0.7 fusion.9
  4.1 0.8 fusion.23
  4.9 0.7 multiply_divide_fusion
  5.6 9.1 %multiply_convert_fusion.1 = (bf16[512,1024]{1,0:T(8,128)(2,1)S(1)}, bf16[512,1024]{1,0:T(8,128)(2,1)S(1)}) fusion(f32[1024]{0:T(1024)S(1)} %bitcast.33, s32[1024]{0:T(1024)S(1)} %get-tuple-element.16, s32[512]{0:T(512)S(1)} %fusion.16, s32[1024]{0:T(1024)S(1)} %get-tuple-element.17, s32[512]{0:T(512)S(1)} %get-tuple-element.8, f32[]{:T(128)S(6)} %mul_shard_map.3, ...), kind=kLoop, calls=%fused_computation.2 | loop fusion | flops 8912896 | bytes 2125828 | tf_op jit(solution)/shard_map/convert_element_type | solution.py:127
  14.7 0.7 fusion.3
  15.4 20.0 %all_to_all.10 = f32[32,32,128]{2,1,0:T(8,128)S(1)} all-to-all(f32[32,32,128]{2,1,0:T(8,128)S(1)} %bitcast.25), channel_id=1, replica_groups=mesh['act'=32,'pix'=8] {'act'}, dimensions={0} | all-to-all | bytes 1048576 | tf_op jit(solution)/shard_map/all_to_all | solution.py:49
  35.4 15.0 %all_to_all.11 = f32[32,32,128]{2,1,0:T(8,128)S(1)} all-to-all(f32[32,32,128]{2,1,0:T(8,128)S(1)} %broadcast_in_dim.2), channel_id=1, replica_groups=mesh['act'=32,'pix'=8] {'act'}, dimensions={0} | all-to-all | bytes 1048576 | tf_op jit(solution)/shard_map/all_to_all | solution.py:28
  50.5 0.8 fusion.2
  51.3 1.0 convolution_bitcast_fusion
  52.3 1.7 %collective-permute-start = (f32[128,1152]{1,0:T(8,128)S(1)}, f32[128,1152]{1,0:T(8,128)S(1)}, u32[]{:S(2)}, u32[]{:S(2)}) collective-permute-start(f32[128,1152]{1,0:T(8,128)S(1)} %pad_maximum_fusion.3), channel_id=1, source_target_pairs={{0,1},{1,0},{2,3},{3,2},{4,5},{5,4},{6,7},{7,6},{8,9},{9,8},{10,11... | collective-permute-start | bytes 1769480 | tf_op jit(solution)/shard_map/ppermute | solution.py:65
  54.0 13.9 %collective-permute-done = f32[128,1152]{1,0:T(8,128)S(1)} collective-permute-done((f32[128,1152]{1,0:T(8,128)S(1)}, f32[128,1152]{1,0:T(8,128)S(1)}, u32[]{:S(2)}, u32[]{:S(2)}) %collective-permute-start) | collective-permute-done | bytes 589856 | tf_op jit(solution)/shard_map/ppermute | solution.py:65
  67.9 0.1 fusion.21
  68.0 3.1 %collective-permute-start.1 = (f32[128,1152]{1,0:T(8,128)S(1)}, f32[128,1152]{1,0:T(8,128)S(1)}, u32[]{:S(2)}, u32[]{:S(2)}) collective-permute-start(f32[128,1152]{1,0:T(8,128)S(1)} %fusion.21), channel_id=1, source_target_pairs={{0,2},{1,3},{2,0},{3,1},{4,6},{5,7},{6,4},{7,5},{8,10},{9,11},{10,... | collective-permute-start | bytes 1769480 | tf_op jit(solution)/shard_map/ppermute | solution.py:65
  71.1 25.9 %collective-permute-done.1 = f32[128,1152]{1,0:T(8,128)S(1)} collective-permute-done((f32[128,1152]{1,0:T(8,128)S(1)}, f32[128,1152]{1,0:T(8,128)S(1)}, u32[]{:S(2)}, u32[]{:S(2)}) %collective-permute-start.1) | collective-permute-done | bytes 589856 | tf_op jit(solution)/shard_map/ppermute | solution.py:65
  97.0 0.1 add.108
  97.1 6.0 %collective-permute-start.2 = (f32[128,1152]{1,0:T(8,128)S(1)}, f32[128,1152]{1,0:T(8,128)S(1)}, u32[]{:S(2)}, u32[]{:S(2)}) collective-permute-start(f32[128,1152]{1,0:T(8,128)S(1)} %add.108), channel_id=1, source_target_pairs={{0,4},{1,5},{2,6},{3,7},{4,0},{5,1},{6,2},{7,3},{8,12},{9,13},{10,... | collective-permute-start | bytes 1769480 | tf_op jit(solution)/shard_map/ppermute | solution.py:65
  103.2 25.6 %collective-permute-done.2 = f32[128,1152]{1,0:T(8,128)S(1)} collective-permute-done((f32[128,1152]{1,0:T(8,128)S(1)}, f32[128,1152]{1,0:T(8,128)S(1)}, u32[]{:S(2)}, u32[]{:S(2)}) %collective-permute-start.2) | collective-permute-done | bytes 589856 | tf_op jit(solution)/shard_map/ppermute | solution.py:65
  128.8 0.6 slice.16.g_ref
  129.4 14.9 %shard_map.85 = (f32[128,128]{1,0:T(8,128)}, f32[128,128]{1,0:T(8,128)}) custom-call(f32[128,128]{1,0:T(8,128)} %slice.16.g_ref), custom_call_target="tpu_custom_call" | custom-call | tf_op jit(solution)/shard_map/pallas_call | solution.py:99
  144.4 1.5 broadcast_multiply_fusion
  145.9 1.7 %fusion.5 = f32[16,1024]{1,0:T(8,128)} fusion(f32[128,1152]{1,0:T(8,128)S(1)} %add.109, f32[128,128]{1,0:T(8,128)} %get-tuple-element.5, s32[]{:T(128)S(6)} %select_n.67), kind=kOutput, calls=%fused_computation.12 | convolution fusion | flops 25165824 | bytes 598020 | tf_op jit(solution)/shard_map/dot_general | solution.py:178
  147.6 1.7 %fusion.4 = f32[1,32,128]{2,1,0:T(8,128)} fusion(f32[32,128]{1,0:T(8,128)S(1)} %bitcast.26, f32[128,128]{1,0:T(8,128)} %get-tuple-element.5), kind=kOutput, calls=%fused_computation.10 | convolution fusion | flops 6295552 | bytes 98304 | tf_op jit(solution)/shard_map/dot_general | solution.py:169
  (8 shorter events, 0.2 us)
Async XLA Ops:
  0.6 14.0 %copy-start = (bf16[1024,128]{1,0:T(8,128)(2,1)S(1)}, bf16[1024,128]{1,0:T(8,128)(2,1)}, u32[]{:S(2)}) copy-start(bf16[1024,128]{1,0:T(8,128)(2,1)} %param.8) | copy-start | bytes 786436
  52.3 15.6 %collective-permute-start = (f32[128,1152]{1,0:T(8,128)S(1)}, f32[128,1152]{1,0:T(8,128)S(1)}, u32[]{:S(2)}, u32[]{:S(2)}) collective-permute-start(f32[128,1152]{1,0:T(8,128)S(1)} %pad_maximum_fusion.3), channel_id=1, source_target_pairs={{0,1},{1,0},{2,3},{3,2},{4,5},{5,4},{6,7},{7,6},{8,9},{9,8},{10,11... | collective-permute-start | bytes 1769480 | tf_op jit(solution)/shard_map/ppermute | solution.py:65
  68.0 29.0 %collective-permute-start.1 = (f32[128,1152]{1,0:T(8,128)S(1)}, f32[128,1152]{1,0:T(8,128)S(1)}, u32[]{:S(2)}, u32[]{:S(2)}) collective-permute-start(f32[128,1152]{1,0:T(8,128)S(1)} %fusion.21), channel_id=1, source_target_pairs={{0,2},{1,3},{2,0},{3,1},{4,6},{5,7},{6,4},{7,5},{8,10},{9,11},{10,... | collective-permute-start | bytes 1769480 | tf_op jit(solution)/shard_map/ppermute | solution.py:65
  97.1 31.6 %collective-permute-start.2 = (f32[128,1152]{1,0:T(8,128)S(1)}, f32[128,1152]{1,0:T(8,128)S(1)}, u32[]{:S(2)}, u32[]{:S(2)}) collective-permute-start(f32[128,1152]{1,0:T(8,128)S(1)} %add.108), channel_id=1, source_target_pairs={{0,4},{1,5},{2,6},{3,7},{4,0},{5,1},{6,2},{7,3},{8,12},{9,13},{10,... | collective-permute-start | bytes 1769480 | tf_op jit(solution)/shard_map/ppermute | solution.py:65

commit v6 on v3

--- a/solution.py
+++ b/solution.py
@@ -168,7 +168,9 @@
     partial_value = lax.dot_general(
         coarse, jac, (((0,), (0,)), ((), ())), preferred_element_type=jnp.float32
     )
-    projection = summed_on_arrival(partial_value, "pix", 0)
+    parts = in_blocks(partial_value.astype(jnp.bfloat16), 0, pix_count)
+    arrived = lax.all_to_all(parts, "pix", split_axis=0, concat_axis=0, tiled=True)
+    projection = arrived.astype(jnp.float32).sum(axis=0)
     basis_out = (own_basis * math.sqrt(total_rows)).reshape(1, 2 * share_pix, RANK)
     r_factor = upper_factor / math.sqrt(total_rows * ACT)
     return (basis_out, projection, r_factor)

time: 112 us -> 106 us (0.946)
  waiting for transfers between devices: 20.8 us -> 14.8 us
    all_to_all x1, waiting for transfers between devices: 14.3 us -> 8.3 us  [on_device(): lax.all_to_all(parts, 'pix', split_axis=0, concat_axis=0, tiled=True)]
where the time goes in v6:
time: 106 us
  blocking collectives  35 us (33%)
  starting transfers between devices  19.1 us (18%)
  Pallas kernels  14.9 us (14%)
  waiting for transfers between devices  14.8 us (14%)
  other arithmetic  14.5 us (14%)
  matrix products  4.3 us (4%)
  between operations  2.06 us (2%)
    all_to_all x1, blocking collectives, summed_on_arrival(): lax.all_to_all(parts, axis, split_axis=0, concat_axis=0, tiled=True)  20 us
    all_to_all x1, blocking collectives, sent_to_all(): return lax.all_to_all(copies, axis, split_axis=0, concat_axis=0, tiled=True)  15 us
    pallas_call x1, Pallas kernels, chol_inv(): pl.pallas_call(chol_inv_kernel, out_shape=(jax.ShapeDtypeStruct((n, n), j...  14.9 us
    ppermute x3, starting transfers between devices, butterfly_sum(): value = value + lax.ppermute(value, axis, pairs)  12.2 us
    convert_element_type x1, other arithmetic, jacobian_planes(): return (real_part.astype(jnp.bfloat16), imag_part.astype(jnp.bfloat16))  9.06 us
    all_to_all x1, waiting for transfers between devices, on_device(): lax.all_to_all(parts, 'pix', split_axis=0, concat_axis=0, tiled=True)  8.3 us
    all_to_all x1, starting transfers between devices, on_device(): lax.all_to_all(parts, 'pix', split_axis=0, concat_axis=0, tiled=True)  6.88 us
    ppermute x3, waiting for transfers between devices, butterfly_sum(): value = value + lax.ppermute(value, axis, pairs)  6.48 us
  transfers between devices with their start and end apart: 4, of which 4 were waited for; matrix products, arithmetic and copies ran while one was open for 1% of the time, Pallas kernels for 0%

profile of v6, /device:TPU:1, one launch (start us, length us, event | category | flops | bytes accessed | tf_op | source)
XLA Modules:
  0.0 105.5 jit_solution(12903806270130787692)
XLA Ops:
  1.3 0.7 fusion.14
  2.0 0.7 exponential_multiply_fusion
  3.4 0.7 fusion.7
  4.1 0.8 fusion.19
  4.9 0.7 multiply_divide_fusion
  5.6 9.1 %multiply_convert_fusion.1 = (bf16[512,1024]{1,0:T(8,128)(2,1)S(1)}, bf16[512,1024]{1,0:T(8,128)(2,1)S(1)}) fusion(f32[1024]{0:T(1024)S(1)} %bitcast.29, s32[1024]{0:T(1024)S(1)} %get-tuple-element.16, s32[512]{0:T(512)S(1)} %fusion.14, s32[1024]{0:T(1024)S(1)} %get-tuple-element.17, s32[512]{0:T(512)S(1)} %get-tuple-element.8, f32[]{:T(128)S(6)} %mul_shard_map.3, ...), kind=kLoop, calls=%fused_computation.2 | loop fusion | flops 8912896 | bytes 2125828 | tf_op jit(solution)/shard_map/convert_element_type | solution.py:127
  14.7 0.7 fusion.3
  15.4 20.0 %all_to_all.15 = f32[32,32,128]{2,1,0:T(8,128)S(1)} all-to-all(f32[32,32,128]{2,1,0:T(8,128)S(1)} %bitcast.22), channel_id=1, replica_groups=mesh['act'=32,'pix'=8] {'act'}, dimensions={0} | all-to-all | bytes 1048576 | tf_op jit(solution)/shard_map/all_to_all | solution.py:49
  35.4 15.0 %all_to_all.16 = f32[32,32,128]{2,1,0:T(8,128)S(1)} all-to-all(f32[32,32,128]{2,1,0:T(8,128)S(1)} %broadcast_in_dim.2), channel_id=1, replica_groups=mesh['act'=32,'pix'=8] {'act'}, dimensions={0} | all-to-all | bytes 1048576 | tf_op jit(solution)/shard_map/all_to_all | solution.py:28
  50.5 1.0 convolution_bitcast_fusion
  51.5 1.7 %collective-permute-start = (f32[128,128]{1,0:T(8,128)S(1)}, f32[128,128]{1,0:T(8,128)S(1)}, u32[]{:S(2)}, u32[]{:S(2)}) collective-permute-start(f32[128,128]{1,0:T(8,128)S(1)} %convolution_bitcast_fusion), channel_id=1, source_target_pairs={{0,1},{1,0},{2,3},{3,2},{4,5},{5,4},{6,7},{7,6},{8,9},{9,8},{10,11... | collective-permute-start | bytes 196616 | tf_op jit(solution)/shard_map/ppermute | solution.py:65
  53.2 2.6 %collective-permute-done = f32[128,128]{1,0:T(8,128)S(1)} collective-permute-done((f32[128,128]{1,0:T(8,128)S(1)}, f32[128,128]{1,0:T(8,128)S(1)}, u32[]{:S(2)}, u32[]{:S(2)}) %collective-permute-start) | collective-permute-done | bytes 65568 | tf_op jit(solution)/shard_map/ppermute | solution.py:65
  55.9 3.1 %collective-permute-start.1 = (f32[128,128]{1,0:T(8,128)S(1)}, f32[128,128]{1,0:T(8,128)S(1)}, u32[]{:S(2)}, u32[]{:S(2)}) collective-permute-start(f32[128,128]{1,0:T(8,128)S(1)} %add.102), channel_id=1, source_target_pairs={{0,2},{1,3},{2,0},{3,1},{4,6},{5,7},{6,4},{7,5},{8,10},{9,11},{10,... | collective-permute-start | bytes 196616 | tf_op jit(solution)/shard_map/ppermute | solution.py:65
  58.9 2.1 %collective-permute-done.1 = f32[128,128]{1,0:T(8,128)S(1)} collective-permute-done((f32[128,128]{1,0:T(8,128)S(1)}, f32[128,128]{1,0:T(8,128)S(1)}, u32[]{:S(2)}, u32[]{:S(2)}) %collective-permute-start.1) | collective-permute-done | bytes 65568 | tf_op jit(solution)/shard_map/ppermute | solution.py:65
  61.0 7.4 %collective-permute-start.2 = (f32[128,128]{1,0:T(8,128)S(1)}, f32[128,128]{1,0:T(8,128)S(1)}, u32[]{:S(2)}, u32[]{:S(2)}) collective-permute-start(f32[128,128]{1,0:T(8,128)S(1)} %add.103), channel_id=1, source_target_pairs={{0,4},{1,5},{2,6},{3,7},{4,0},{5,1},{6,2},{7,3},{8,12},{9,13},{10,... | collective-permute-start | bytes 196616 | tf_op jit(solution)/shard_map/ppermute | solution.py:65
  68.5 1.8 %collective-permute-done.2 = f32[128,128]{1,0:T(8,128)S(1)} collective-permute-done((f32[128,128]{1,0:T(8,128)S(1)}, f32[128,128]{1,0:T(8,128)S(1)}, u32[]{:S(2)}, u32[]{:S(2)}) %collective-permute-start.2) | collective-permute-done | bytes 65568 | tf_op jit(solution)/shard_map/ppermute | solution.py:65
  70.2 0.6 add.104.g_ref
  70.9 14.9 %shard_map.85 = (f32[128,128]{1,0:T(8,128)}, f32[128,128]{1,0:T(8,128)}) custom-call(f32[128,128]{1,0:T(8,128)} %add.104.g_ref), custom_call_target="tpu_custom_call" | custom-call | tf_op jit(solution)/shard_map/pallas_call | solution.py:99
  85.8 1.4 %fusion.20 = f32[1024,128]{1,0:T(8,128)S(1)} fusion(f32[1024,128]{1,0:T(8,128)S(1)} %bitcast.21, f32[128,128]{1,0:T(8,128)} %get-tuple-element.5), kind=kOutput, calls=%fused_computation.51 | convolution fusion | flops 201326592 | bytes 1114112 | tf_op jit(solution)/shard_map/dot_general | solution.py:156
  87.2 1.2 %fusion.4 = bf16[128,1024]{1,0:T(8,128)(2,1)} fusion(bf16[512,1024]{1,0:T(8,128)(2,1)S(1)} %get-tuple-element.12, bf16[512,1024]{1,0:T(8,128)(2,1)S(1)} %get-tuple-element.11, f32[1024,128]{1,0:T(8,128)S(1)} %fusion.20), kind=kOutput, calls=%fused_computation.8 | convolution fusion | flops 272891904 | bytes 2883584 | tf_op jit(solution)/shard_map/dot_general | solution.py:168
  88.4 6.9 %all-to-all-start.2 = ((bf16[8,16,1024]{2,1,0:T(8,128)(2,1)}), bf16[8,16,1024]{2,1,0:T(8,128)(2,1)S(1)}, u32[]{:S(2)}, u32[]{:S(2)}) async-start(bf16[8,16,1024]{2,1,0:T(8,128)(2,1)} %bitcast.11), calls=%async_computation.2 | async-start | bytes 524288 | tf_op jit(solution)/shard_map/all_to_all | solution.py:172
  95.9 0.6 broadcast_multiply_fusion
  96.6 8.3 %all-to-all-done.2 = bf16[8,16,1024]{2,1,0:T(8,128)(2,1)S(1)} async-done(((bf16[8,16,1024]{2,1,0:T(8,128)(2,1)}), bf16[8,16,1024]{2,1,0:T(8,128)(2,1)S(1)}, u32[]{:S(2)}, u32[]{:S(2)}) %all-to-all-start.2) | async-done | bytes 262176 | tf_op jit(solution)/shard_map/all_to_all | solution.py:172
  104.9 0.7 convert_reduce_fusion
  (10 shorter events, 0.8 us)
Async XLA Ops:
  0.6 14.0 %copy-start = (bf16[1024,128]{1,0:T(8,128)(2,1)S(1)}, bf16[1024,128]{1,0:T(8,128)(2,1)}, u32[]{:S(2)}) copy-start(bf16[1024,128]{1,0:T(8,128)(2,1)} %param.8) | copy-start | bytes 786436
  51.5 4.4 %collective-permute-start = (f32[128,128]{1,0:T(8,128)S(1)}, f32[128,128]{1,0:T(8,128)S(1)}, u32[]{:S(2)}, u32[]{:S(2)}) collective-permute-start(f32[128,128]{1,0:T(8,128)S(1)} %convolution_bitcast_fusion), channel_id=1, source_target_pairs={{0,1},{1,0},{2,3},{3,2},{4,5},{5,4},{6,7},{7,6},{8,9},{9,8},{10,11... | collective-permute-start | bytes 196616 | tf_op jit(solution)/shard_map/ppermute | solution.py:65
  55.9 5.1 %collective-permute-start.1 = (f32[128,128]{1,0:T(8,128)S(1)}, f32[128,128]{1,0:T(8,128)S(1)}, u32[]{:S(2)}, u32[]{:S(2)}) collective-permute-start(f32[128,128]{1,0:T(8,128)S(1)} %add.102), channel_id=1, source_target_pairs={{0,2},{1,3},{2,0},{3,1},{4,6},{5,7},{6,4},{7,5},{8,10},{9,11},{10,... | collective-permute-start | bytes 196616 | tf_op jit(solution)/shard_map/ppermute | solution.py:65
  61.0 9.2 %collective-permute-start.2 = (f32[128,128]{1,0:T(8,128)S(1)}, f32[128,128]{1,0:T(8,128)S(1)}, u32[]{:S(2)}, u32[]{:S(2)}) collective-permute-start(f32[128,128]{1,0:T(8,128)S(1)} %add.103), channel_id=1, source_target_pairs={{0,4},{1,5},{2,6},{3,7},{4,0},{5,1},{6,2},{7,3},{8,12},{9,13},{10,... | collective-permute-start | bytes 196616 | tf_op jit(solution)/shard_map/ppermute | solution.py:65
  87.2 8.7 %copy-start.1 = (f32[128,128]{1,0:T(8,128)S(1)}, f32[128,128]{1,0:T(8,128)}, u32[]{:S(2)}) copy-start(f32[128,128]{1,0:T(8,128)} %get-tuple-element.6) | copy-start | bytes 196612
  88.4 16.4 %all-to-all-start.2 = ((bf16[8,16,1024]{2,1,0:T(8,128)(2,1)}), bf16[8,16,1024]{2,1,0:T(8,128)(2,1)S(1)}, u32[]{:S(2)}, u32[]{:S(2)}) async-start(bf16[8,16,1024]{2,1,0:T(8,128)(2,1)} %bitcast.11), calls=%async_computation.2 | async-start | bytes 524288 | tf_op jit(solution)/shard_map/all_to_all | solution.py:172

commit v7 on v6

--- a/solution.py
+++ b/solution.py
@@ -67,31 +67,44 @@
     return value
 
 
+PANEL = 8
+
+
 def chol_inv_kernel(g_ref, lt_ref, inv_ref):
     n = g_ref.shape[0]
     lt_ref[...] = g_ref[...]
     rows = lax.broadcasted_iota(jnp.int32, (n, n), 0)
     cols = lax.broadcasted_iota(jnp.int32, (n, n), 1)
     inv_ref[...] = jnp.where(rows == cols, 1.0, 0.0).astype(jnp.float32)
-    lane = lax.broadcasted_iota(jnp.int32, (1, n), 1)
-    sub = lax.broadcasted_iota(jnp.int32, (n, 1), 0)
-
-    def step(j, carry):
-        a = lt_ref[...]
-        row = lt_ref[pl.ds(j, 1), :]
-        d = jnp.sum(jnp.where(lane == j, row, 0.0), axis=1, keepdims=True)
-        r = lax.rsqrt(d)
-        l = jnp.where(lane >= j, row * r, 0.0)
-        colj = jnp.sum(jnp.where(cols == j, a, 0.0), axis=1, keepdims=True)
-        c = jnp.where(sub > j, colj * r, 0.0)
-        b_row = inv_ref[pl.ds(j, 1), :] * r
-        lt_ref[...] = a - c * l
-        inv_ref[...] = inv_ref[...] - c * b_row
-        lt_ref[pl.ds(j, 1), :] = l
-        inv_ref[pl.ds(j, 1), :] = b_row
-        return carry
-
-    lax.fori_loop(0, n, step, 0)
+    lane = lax.broadcasted_iota(jnp.int32, (PANEL, n), 1)
+    sub = lax.broadcasted_iota(jnp.int32, (PANEL, n), 0)
+    dims = (((0,), (0,)), ((), ()))
+    for p0 in range(0, n, PANEL):
+        a = lt_ref[p0 : p0 + PANEL, :]
+        b = inv_ref[p0 : p0 + PANEL, :]
+        for i in range(PANEL):
+            j = p0 + i
+            row = jnp.sum(jnp.where(sub == i, a, 0.0), axis=0, keepdims=True)
+            d = jnp.sum(jnp.where(lane[:1] == j, row, 0.0), axis=1, keepdims=True)
+            r = lax.rsqrt(d)
+            l = jnp.where(lane[:1] >= j, row * r, 0.0)
+            b_row = jnp.sum(jnp.where(sub == i, b, 0.0), axis=0, keepdims=True) * r
+            col = jnp.sum(jnp.where(lane == j, a, 0.0), axis=1, keepdims=True)
+            c = jnp.where(sub[:, :1] > i, col * r, 0.0)
+            a = jnp.where(sub == i, l, a - c * l)
+            b = jnp.where(sub == i, b_row, b - c * b_row)
+        lt_ref[p0 : p0 + PANEL, :] = a
+        inv_ref[p0 : p0 + PANEL, :] = b
+        rest = p0 + PANEL
+        if rest < n:
+            upd_a = lax.dot_general(
+                a, a, dims, precision=lax.Precision.HIGHEST, preferred_element_type=jnp.float32
+            )
+            upd_b = lax.dot_general(
+                a, b, dims, precision=lax.Precision.HIGHEST, preferred_element_type=jnp.float32
+            )
+            lt_ref[rest:, :] = lt_ref[rest:, :] - upd_a[rest:]
+            inv_ref[rest:, :] = inv_ref[rest:, :] - upd_b[rest:]
 
 
 def chol_inv(g):

time: 106 us -> 109 us (1.028)
  Pallas kernels: 14.9 us -> 17.9 us
    pallas_call x1, Pallas kernels: 14.9 us -> 17.9 us  [chol_inv(): pl.pallas_call(chol_inv_kernel, out_shape=(jax.ShapeDtypeStruct((n, n), j...]
where the time goes in v7:
time: 109 us; the launch traced here: 108 us
  blocking collectives  35 us (32%)
  starting transfers between devices  19.1 us (18%)
  Pallas kernels  17.9 us (16%)
  waiting for transfers between devices  14.8 us (14%)
  other arithmetic  14.5 us (13%)
  matrix products  4.3 us (4%)
  between operations  2.06 us (2%)
    all_to_all x1, blocking collectives, summed_on_arrival(): lax.all_to_all(parts, axis, split_axis=0, concat_axis=0, tiled=True)  20 us
    pallas_call x1, Pallas kernels, chol_inv(): pl.pallas_call(chol_inv_kernel, out_shape=(jax.ShapeDtypeStruct((n, n), j...  17.9 us
    all_to_all x1, blocking collectives, sent_to_all(): return lax.all_to_all(copies, axis, split_axis=0, concat_axis=0, tiled=True)  15 us
    ppermute x3, starting transfers between devices, butterfly_sum(): value = value + lax.ppermute(value, axis, pairs)  12.2 us
    convert_element_type x1, other arithmetic, jacobian_planes(): return (real_part.astype(jnp.bfloat16), imag_part.astype(jnp.bfloat16))  9.06 us
    all_to_all x1, waiting for transfers between devices, on_device(): lax.all_to_all(parts, 'pix', split_axis=0, concat_axis=0, tiled=True)  8.28 us
    all_to_all x1, starting transfers between devices, on_device(): lax.all_to_all(parts, 'pix', split_axis=0, concat_axis=0, tiled=True)  6.87 us
    ppermute x3, waiting for transfers between devices, butterfly_sum(): value = value + lax.ppermute(value, axis, pairs)  6.48 us
  transfers between devices with their start and end apart: 4, of which 4 were waited for; matrix products, arithmetic and copies ran while one was open for 1% of the time, Pallas kernels for 0%

profile of v7, /device:TPU:1, one launch (start us, length us, event | category | flops | bytes accessed | tf_op | source)
XLA Modules:
  0.0 108.4 jit_solution(5971103653510738518)
XLA Ops:
  1.3 0.7 fusion.14
  2.0 0.7 exponential_multiply_fusion
  3.4 0.7 fusion.7
  4.1 0.8 fusion.19
  4.9 0.7 multiply_divide_fusion
  5.6 9.1 %multiply_convert_fusion.1 = (bf16[512,1024]{1,0:T(8,128)(2,1)S(1)}, bf16[512,1024]{1,0:T(8,128)(2,1)S(1)}) fusion(f32[1024]{0:T(1024)S(1)} %bitcast.29, s32[1024]{0:T(1024)S(1)} %get-tuple-element.16, s32[512]{0:T(512)S(1)} %fusion.14, s32[1024]{0:T(1024)S(1)} %get-tuple-element.17, s32[512]{0:T(512)S(1)} %get-tuple-element.8, f32[]{:T(128)S(6)} %mul_shard_map.3, ...), kind=kLoop, calls=%fused_computation.2 | loop fusion | flops 8912896 | bytes 2125828 | tf_op jit(solution)/shard_map/convert_element_type | solution.py:140
  14.7 0.7 fusion.3
  15.4 20.0 %all_to_all.15 = f32[32,32,128]{2,1,0:T(8,128)S(1)} all-to-all(f32[32,32,128]{2,1,0:T(8,128)S(1)} %bitcast.22), channel_id=1, replica_groups=mesh['act'=32,'pix'=8] {'act'}, dimensions={0} | all-to-all | bytes 1048576 | tf_op jit(solution)/shard_map/all_to_all | solution.py:49
  35.4 15.0 %all_to_all.16 = f32[32,32,128]{2,1,0:T(8,128)S(1)} all-to-all(f32[32,32,128]{2,1,0:T(8,128)S(1)} %broadcast_in_dim.2), channel_id=1, replica_groups=mesh['act'=32,'pix'=8] {'act'}, dimensions={0} | all-to-all | bytes 1048576 | tf_op jit(solution)/shard_map/all_to_all | solution.py:28
  50.5 1.0 convolution_bitcast_fusion
  51.5 1.7 %collective-permute-start = (f32[128,128]{1,0:T(8,128)S(1)}, f32[128,128]{1,0:T(8,128)S(1)}, u32[]{:S(2)}, u32[]{:S(2)}) collective-permute-start(f32[128,128]{1,0:T(8,128)S(1)} %convolution_bitcast_fusion), channel_id=1, source_target_pairs={{0,1},{1,0},{2,3},{3,2},{4,5},{5,4},{6,7},{7,6},{8,9},{9,8},{10,11... | collective-permute-start | bytes 196616 | tf_op jit(solution)/shard_map/ppermute | solution.py:65
  53.2 2.6 %collective-permute-done = f32[128,128]{1,0:T(8,128)S(1)} collective-permute-done((f32[128,128]{1,0:T(8,128)S(1)}, f32[128,128]{1,0:T(8,128)S(1)}, u32[]{:S(2)}, u32[]{:S(2)}) %collective-permute-start) | collective-permute-done | bytes 65568 | tf_op jit(solution)/shard_map/ppermute | solution.py:65
  55.9 3.1 %collective-permute-start.1 = (f32[128,128]{1,0:T(8,128)S(1)}, f32[128,128]{1,0:T(8,128)S(1)}, u32[]{:S(2)}, u32[]{:S(2)}) collective-permute-start(f32[128,128]{1,0:T(8,128)S(1)} %add.102), channel_id=1, source_target_pairs={{0,2},{1,3},{2,0},{3,1},{4,6},{5,7},{6,4},{7,5},{8,10},{9,11},{10,... | collective-permute-start | bytes 196616 | tf_op jit(solution)/shard_map/ppermute | solution.py:65
  58.9 2.1 %collective-permute-done.1 = f32[128,128]{1,0:T(8,128)S(1)} collective-permute-done((f32[128,128]{1,0:T(8,128)S(1)}, f32[128,128]{1,0:T(8,128)S(1)}, u32[]{:S(2)}, u32[]{:S(2)}) %collective-permute-start.1) | collective-permute-done | bytes 65568 | tf_op jit(solution)/shard_map/ppermute | solution.py:65
  61.0 7.4 %collective-permute-start.2 = (f32[128,128]{1,0:T(8,128)S(1)}, f32[128,128]{1,0:T(8,128)S(1)}, u32[]{:S(2)}, u32[]{:S(2)}) collective-permute-start(f32[128,128]{1,0:T(8,128)S(1)} %add.103), channel_id=1, source_target_pairs={{0,4},{1,5},{2,6},{3,7},{4,0},{5,1},{6,2},{7,3},{8,12},{9,13},{10,... | collective-permute-start | bytes 196616 | tf_op jit(solution)/shard_map/ppermute | solution.py:65
  68.5 1.8 %collective-permute-done.2 = f32[128,128]{1,0:T(8,128)S(1)} collective-permute-done((f32[128,128]{1,0:T(8,128)S(1)}, f32[128,128]{1,0:T(8,128)S(1)}, u32[]{:S(2)}, u32[]{:S(2)}) %collective-permute-start.2) | collective-permute-done | bytes 65568 | tf_op jit(solution)/shard_map/ppermute | solution.py:65
  70.2 0.6 add.104.g_ref
  70.9 17.9 %shard_map.85 = (f32[128,128]{1,0:T(8,128)}, f32[128,128]{1,0:T(8,128)}) custom-call(f32[128,128]{1,0:T(8,128)} %add.104.g_ref), custom_call_target="tpu_custom_call" | custom-call | tf_op jit(solution)/shard_map/pallas_call | solution.py:112
  88.7 1.4 %fusion.20 = f32[1024,128]{1,0:T(8,128)S(1)} fusion(f32[1024,128]{1,0:T(8,128)S(1)} %bitcast.21, f32[128,128]{1,0:T(8,128)} %get-tuple-element.5), kind=kOutput, calls=%fused_computation.51 | convolution fusion | flops 201326592 | bytes 1114112 | tf_op jit(solution)/shard_map/dot_general | solution.py:169
  90.2 1.2 %fusion.4 = bf16[128,1024]{1,0:T(8,128)(2,1)} fusion(bf16[512,1024]{1,0:T(8,128)(2,1)S(1)} %get-tuple-element.12, bf16[512,1024]{1,0:T(8,128)(2,1)S(1)} %get-tuple-element.11, f32[1024,128]{1,0:T(8,128)S(1)} %fusion.20), kind=kOutput, calls=%fused_computation.8 | convolution fusion | flops 272891904 | bytes 2883584 | tf_op jit(solution)/shard_map/dot_general | solution.py:181
  91.4 6.9 %all-to-all-start.2 = ((bf16[8,16,1024]{2,1,0:T(8,128)(2,1)}), bf16[8,16,1024]{2,1,0:T(8,128)(2,1)S(1)}, u32[]{:S(2)}, u32[]{:S(2)}) async-start(bf16[8,16,1024]{2,1,0:T(8,128)(2,1)} %bitcast.11), calls=%async_computation.2 | async-start | bytes 524288 | tf_op jit(solution)/shard_map/all_to_all | solution.py:185
  98.9 0.6 broadcast_multiply_fusion
  99.5 8.3 %all-to-all-done.2 = bf16[8,16,1024]{2,1,0:T(8,128)(2,1)S(1)} async-done(((bf16[8,16,1024]{2,1,0:T(8,128)(2,1)}), bf16[8,16,1024]{2,1,0:T(8,128)(2,1)S(1)}, u32[]{:S(2)}, u32[]{:S(2)}) %all-to-all-start.2) | async-done | bytes 262176 | tf_op jit(solution)/shard_map/all_to_all | solution.py:185
  107.8 0.7 convert_reduce_fusion
  (10 shorter events, 0.8 us)
Async XLA Ops:
  0.6 14.0 %copy-start = (bf16[1024,128]{1,0:T(8,128)(2,1)S(1)}, bf16[1024,128]{1,0:T(8,128)(2,1)}, u32[]{:S(2)}) copy-start(bf16[1024,128]{1,0:T(8,128)(2,1)} %param.8) | copy-start | bytes 786436
  51.5 4.4 %collective-permute-start = (f32[128,128]{1,0:T(8,128)S(1)}, f32[128,128]{1,0:T(8,128)S(1)}, u32[]{:S(2)}, u32[]{:S(2)}) collective-permute-start(f32[128,128]{1,0:T(8,128)S(1)} %convolution_bitcast_fusion), channel_id=1, source_target_pairs={{0,1},{1,0},{2,3},{3,2},{4,5},{5,4},{6,7},{7,6},{8,9},{9,8},{10,11... | collective-permute-start | bytes 196616 | tf_op jit(solution)/shard_map/ppermute | solution.py:65
  55.9 5.1 %collective-permute-start.1 = (f32[128,128]{1,0:T(8,128)S(1)}, f32[128,128]{1,0:T(8,128)S(1)}, u32[]{:S(2)}, u32[]{:S(2)}) collective-permute-start(f32[128,128]{1,0:T(8,128)S(1)} %add.102), channel_id=1, source_target_pairs={{0,2},{1,3},{2,0},{3,1},{4,6},{5,7},{6,4},{7,5},{8,10},{9,11},{10,... | collective-permute-start | bytes 196616 | tf_op jit(solution)/shard_map/ppermute | solution.py:65
  61.0 9.2 %collective-permute-start.2 = (f32[128,128]{1,0:T(8,128)S(1)}, f32[128,128]{1,0:T(8,128)S(1)}, u32[]{:S(2)}, u32[]{:S(2)}) collective-permute-start(f32[128,128]{1,0:T(8,128)S(1)} %add.103), channel_id=1, source_target_pairs={{0,4},{1,5},{2,6},{3,7},{4,0},{5,1},{6,2},{7,3},{8,12},{9,13},{10,... | collective-permute-start | bytes 196616 | tf_op jit(solution)/shard_map/ppermute | solution.py:65
  90.2 8.7 %copy-start.1 = (f32[128,128]{1,0:T(8,128)S(1)}, f32[128,128]{1,0:T(8,128)}, u32[]{:S(2)}) copy-start(f32[128,128]{1,0:T(8,128)} %get-tuple-element.6) | copy-start | bytes 196612
  91.4 16.4 %all-to-all-start.2 = ((bf16[8,16,1024]{2,1,0:T(8,128)(2,1)}), bf16[8,16,1024]{2,1,0:T(8,128)(2,1)S(1)}, u32[]{:S(2)}, u32[]{:S(2)}) async-start(bf16[8,16,1024]{2,1,0:T(8,128)(2,1)} %bitcast.11), calls=%async_computation.2 | async-start | bytes 524288 | tf_op jit(solution)/shard_map/all_to_all | solution.py:185

commit v8 on v6

--- a/solution.py
+++ b/solution.py
@@ -107,6 +107,25 @@
     )(g)
 
 
+HALF_PI_HI = 1.5703125
+HALF_PI_LO = 4.8382679e-04
+
+
+def sin_cos(angle):
+    turns = jnp.round(angle * (2.0 / math.pi))
+    rest = (angle - turns * HALF_PI_HI) - turns * HALF_PI_LO
+    quadrant = turns.astype(jnp.int32) & 3
+    sq = rest * rest
+    sine = rest + rest * sq * (-1.0 / 6 + sq * (1.0 / 120 + sq * (-1.0 / 5040 + sq * (1.0 / 362880))))
+    cosine = 1.0 + sq * (-0.5 + sq * (1.0 / 24 + sq * (-1.0 / 720 + sq * (1.0 / 40320))))
+    swap = (quadrant & 1) == 1
+    sin_v = jnp.where(swap, cosine, sine)
+    cos_v = jnp.where(swap, sine, cosine)
+    sin_v = jnp.where(quadrant >= 2, -sin_v, sin_v)
+    cos_v = jnp.where((quadrant == 1) | (quadrant == 2), -cos_v, cos_v)
+    return sin_v, cos_v
+
+
 def jacobian_planes(pixels, wave_scale, flux_level, codes, field_re, field_im):
     delta_u = pixels // FOCAL - FOCAL // 2
     delta_v = pixels % FOCAL - FOCAL // 2
@@ -120,8 +139,7 @@
     phase_angle = mirror.astype(jnp.float32)[None, :] * defocus[
         :, None
     ] - TWO_PI / FOCAL * wave_scale * phase_int.astype(jnp.float32)
-    cosine = jnp.cos(phase_angle)
-    sine_part = jnp.sin(phase_angle)
+    sine_part, cosine = sin_cos(phase_angle)
     real_part = amplitude[:, None] * (field_re[None, :] * cosine - field_im[None, :] * sine_part)
     imag_part = amplitude[:, None] * (field_re[None, :] * sine_part + field_im[None, :] * cosine)
     return real_part.astype(jnp.bfloat16), imag_part.astype(jnp.bfloat16)

time: 106 us -> 101 us (0.953)
  other arithmetic: 14.5 us -> 9.51 us
    convert_element_type x1, other arithmetic: 9.06 us -> 4.08 us  [jacobian_planes(): return (real_part.astype(jnp.bfloat16), imag_part.astype(jnp.bfloat16))]
where the time goes in v8:
time: 101 us
  blocking collectives  35 us (35%)
  starting transfers between devices  19.1 us (19%)
  Pallas kernels  14.9 us (15%)
  waiting for transfers between devices  14.8 us (15%)
  other arithmetic  9.51 us (9%)
  matrix products  4.3 us (4%)
  between operations  2.05 us (2%)
    all_to_all x1, blocking collectives, summed_on_arrival(): lax.all_to_all(parts, axis, split_axis=0, concat_axis=0, tiled=True)  20 us
    all_to_all x1, blocking collectives, sent_to_all(): return lax.all_to_all(copies, axis, split_axis=0, concat_axis=0, tiled=True)  15 us
    pallas_call x1, Pallas kernels, chol_inv(): pl.pallas_call(chol_inv_kernel, out_shape=(jax.ShapeDtypeStruct((n, n), j...  14.9 us
    ppermute x3, starting transfers between devices, butterfly_sum(): value = value + lax.ppermute(value, axis, pairs)  12.2 us
    all_to_all x1, waiting for transfers between devices, on_device(): lax.all_to_all(parts, 'pix', split_axis=0, concat_axis=0, tiled=True)  8.27 us
    all_to_all x1, starting transfers between devices, on_device(): lax.all_to_all(parts, 'pix', split_axis=0, concat_axis=0, tiled=True)  6.88 us
    ppermute x3, waiting for transfers between devices, butterfly_sum(): value = value + lax.ppermute(value, axis, pairs)  6.48 us
    convert_element_type x1, other arithmetic, jacobian_planes(): return (real_part.astype(jnp.bfloat16), imag_part.astype(jnp.bfloat16))  4.08 us
  transfers between devices with their start and end apart: 4, of which 4 were waited for; matrix products, arithmetic and copies ran while one was open for 1% of the time, Pallas kernels for 0%

profile of v8, /device:TPU:1, one launch (start us, length us, event | category | flops | bytes accessed | tf_op | source)
XLA Modules:
  0.0 100.5 jit_solution(15843145149620010721)
XLA Ops:
  1.3 0.7 fusion.21
  2.0 0.7 multiply_divide_fusion
  3.4 0.7 fusion.14
  4.1 0.8 fusion.26
  4.9 0.7 exponential_multiply_fusion
  5.6 4.1 %multiply_convert_fusion.1 = (bf16[512,1024]{1,0:T(8,128)(2,1)S(1)}, bf16[512,1024]{1,0:T(8,128)(2,1)S(1)}) fusion(f32[1024]{0:T(1024)S(1)} %bitcast.29, f32[1024]{0:T(1024)S(1)} %bitcast.28, f32[512]{0:T(512)S(1)} %exponential_multiply_fusion, s32[1024]{0:T(1024)S(1)} %get-tuple-element.16, s32[512]{0:T(512)S(1)} %fusion.21, ...), kind=kLoop, calls=%fused_computation.21 | loop fusion | flops 28835840 | bytes 2125828 | tf_op jit(solution)/shard_map/convert_element_type | solution.py:145
  9.7 0.7 fusion.10
  10.4 20.0 %all_to_all.15 = f32[32,32,128]{2,1,0:T(8,128)S(1)} all-to-all(f32[32,32,128]{2,1,0:T(8,128)S(1)} %bitcast.22), channel_id=1, replica_groups=mesh['act'=32,'pix'=8] {'act'}, dimensions={0} | all-to-all | bytes 1048576 | tf_op jit(solution)/shard_map/all_to_all | solution.py:49
  30.5 15.0 %all_to_all.16 = f32[32,32,128]{2,1,0:T(8,128)S(1)} all-to-all(f32[32,32,128]{2,1,0:T(8,128)S(1)} %broadcast_in_dim.2), channel_id=1, replica_groups=mesh['act'=32,'pix'=8] {'act'}, dimensions={0} | all-to-all | bytes 1048576 | tf_op jit(solution)/shard_map/all_to_all | solution.py:28
  45.5 1.0 %convolution_bitcast_fusion = f32[128,128]{1,0:T(8,128)S(1)} fusion(f32[32,32,128]{2,1,0:T(8,128)S(1)} %all_to_all.16), kind=kOutput, calls=%fused_computation.30 | convolution fusion | flops 201326592 | bytes 589824 | tf_op jit(solution)/shard_map/dot_general | solution.py:149
  46.5 1.7 %collective-permute-start = (f32[128,128]{1,0:T(8,128)S(1)}, f32[128,128]{1,0:T(8,128)S(1)}, u32[]{:S(2)}, u32[]{:S(2)}) collective-permute-start(f32[128,128]{1,0:T(8,128)S(1)} %convolution_bitcast_fusion), channel_id=1, source_target_pairs={{0,1},{1,0},{2,3},{3,2},{4,5},{5,4},{6,7},{7,6},{8,9},{9,8},{10,11... | collective-permute-start | bytes 196616 | tf_op jit(solution)/shard_map/ppermute | solution.py:65
  48.2 2.6 %collective-permute-done = f32[128,128]{1,0:T(8,128)S(1)} collective-permute-done((f32[128,128]{1,0:T(8,128)S(1)}, f32[128,128]{1,0:T(8,128)S(1)}, u32[]{:S(2)}, u32[]{:S(2)}) %collective-permute-start) | collective-permute-done | bytes 65568 | tf_op jit(solution)/shard_map/ppermute | solution.py:65
  50.9 3.1 %collective-permute-start.1 = (f32[128,128]{1,0:T(8,128)S(1)}, f32[128,128]{1,0:T(8,128)S(1)}, u32[]{:S(2)}, u32[]{:S(2)}) collective-permute-start(f32[128,128]{1,0:T(8,128)S(1)} %add.162), channel_id=1, source_target_pairs={{0,2},{1,3},{2,0},{3,1},{4,6},{5,7},{6,4},{7,5},{8,10},{9,11},{10,... | collective-permute-start | bytes 196616 | tf_op jit(solution)/shard_map/ppermute | solution.py:65
  54.0 2.1 %collective-permute-done.1 = f32[128,128]{1,0:T(8,128)S(1)} collective-permute-done((f32[128,128]{1,0:T(8,128)S(1)}, f32[128,128]{1,0:T(8,128)S(1)}, u32[]{:S(2)}, u32[]{:S(2)}) %collective-permute-start.1) | collective-permute-done | bytes 65568 | tf_op jit(solution)/shard_map/ppermute | solution.py:65
  56.0 7.4 %collective-permute-start.2 = (f32[128,128]{1,0:T(8,128)S(1)}, f32[128,128]{1,0:T(8,128)S(1)}, u32[]{:S(2)}, u32[]{:S(2)}) collective-permute-start(f32[128,128]{1,0:T(8,128)S(1)} %add.163), channel_id=1, source_target_pairs={{0,4},{1,5},{2,6},{3,7},{4,0},{5,1},{6,2},{7,3},{8,12},{9,13},{10,... | collective-permute-start | bytes 196616 | tf_op jit(solution)/shard_map/ppermute | solution.py:65
  63.5 1.8 %collective-permute-done.2 = f32[128,128]{1,0:T(8,128)S(1)} collective-permute-done((f32[128,128]{1,0:T(8,128)S(1)}, f32[128,128]{1,0:T(8,128)S(1)}, u32[]{:S(2)}, u32[]{:S(2)}) %collective-permute-start.2) | collective-permute-done | bytes 65568 | tf_op jit(solution)/shard_map/ppermute | solution.py:65
  65.2 0.6 add.164.g_ref
  65.9 14.9 %shard_map.85 = (f32[128,128]{1,0:T(8,128)}, f32[128,128]{1,0:T(8,128)}) custom-call(f32[128,128]{1,0:T(8,128)} %add.164.g_ref), custom_call_target="tpu_custom_call" | custom-call | tf_op jit(solution)/shard_map/pallas_call | solution.py:99
  80.8 1.4 %fusion.27 = f32[1024,128]{1,0:T(8,128)S(1)} fusion(f32[1024,128]{1,0:T(8,128)S(1)} %bitcast.21, f32[128,128]{1,0:T(8,128)} %get-tuple-element.5), kind=kOutput, calls=%fused_computation.72 | convolution fusion | flops 201326592 | bytes 1114112 | tf_op jit(solution)/shard_map/dot_general | solution.py:174
  82.3 1.2 %fusion.11 = bf16[128,1024]{1,0:T(8,128)(2,1)} fusion(bf16[512,1024]{1,0:T(8,128)(2,1)S(1)} %get-tuple-element.12, bf16[512,1024]{1,0:T(8,128)(2,1)S(1)} %get-tuple-element.11, f32[1024,128]{1,0:T(8,128)S(1)} %fusion.27), kind=kOutput, calls=%fused_computation.29 | convolution fusion | flops 272891904 | bytes 2883584 | tf_op jit(solution)/shard_map/dot_general | solution.py:186
  83.4 6.9 %all-to-all-start.2 = ((bf16[8,16,1024]{2,1,0:T(8,128)(2,1)}), bf16[8,16,1024]{2,1,0:T(8,128)(2,1)S(1)}, u32[]{:S(2)}, u32[]{:S(2)}) async-start(bf16[8,16,1024]{2,1,0:T(8,128)(2,1)} %bitcast.11), calls=%async_computation.2 | async-start | bytes 524288 | tf_op jit(solution)/shard_map/all_to_all | solution.py:190
  90.9 0.6 broadcast_multiply_fusion
  91.6 8.3 %all-to-all-done.2 = bf16[8,16,1024]{2,1,0:T(8,128)(2,1)S(1)} async-done(((bf16[8,16,1024]{2,1,0:T(8,128)(2,1)}), bf16[8,16,1024]{2,1,0:T(8,128)(2,1)S(1)}, u32[]{:S(2)}, u32[]{:S(2)}) %all-to-all-start.2) | async-done | bytes 262176 | tf_op jit(solution)/shard_map/all_to_all | solution.py:190
  99.9 0.7 convert_reduce_fusion
  (10 shorter events, 0.8 us)
Async XLA Ops:
  0.6 9.0 %copy-start = (bf16[1024,128]{1,0:T(8,128)(2,1)S(1)}, bf16[1024,128]{1,0:T(8,128)(2,1)}, u32[]{:S(2)}) copy-start(bf16[1024,128]{1,0:T(8,128)(2,1)} %param.8) | copy-start | bytes 786436
  46.5 4.4 %collective-permute-start = (f32[128,128]{1,0:T(8,128)S(1)}, f32[128,128]{1,0:T(8,128)S(1)}, u32[]{:S(2)}, u32[]{:S(2)}) collective-permute-start(f32[128,128]{1,0:T(8,128)S(1)} %convolution_bitcast_fusion), channel_id=1, source_target_pairs={{0,1},{1,0},{2,3},{3,2},{4,5},{5,4},{6,7},{7,6},{8,9},{9,8},{10,11... | collective-permute-start | bytes 196616 | tf_op jit(solution)/shard_map/ppermute | solution.py:65
  50.9 5.2 %collective-permute-start.1 = (f32[128,128]{1,0:T(8,128)S(1)}, f32[128,128]{1,0:T(8,128)S(1)}, u32[]{:S(2)}, u32[]{:S(2)}) collective-permute-start(f32[128,128]{1,0:T(8,128)S(1)} %add.162), channel_id=1, source_target_pairs={{0,2},{1,3},{2,0},{3,1},{4,6},{5,7},{6,4},{7,5},{8,10},{9,11},{10,... | collective-permute-start | bytes 196616 | tf_op jit(solution)/shard_map/ppermute | solution.py:65
  56.0 9.2 %collective-permute-start.2 = (f32[128,128]{1,0:T(8,128)S(1)}, f32[128,128]{1,0:T(8,128)S(1)}, u32[]{:S(2)}, u32[]{:S(2)}) collective-permute-start(f32[128,128]{1,0:T(8,128)S(1)} %add.163), channel_id=1, source_target_pairs={{0,4},{1,5},{2,6},{3,7},{4,0},{5,1},{6,2},{7,3},{8,12},{9,13},{10,... | collective-permute-start | bytes 196616 | tf_op jit(solution)/shard_map/ppermute | solution.py:65
  82.2 8.7 %copy-start.1 = (f32[128,128]{1,0:T(8,128)S(1)}, f32[128,128]{1,0:T(8,128)}, u32[]{:S(2)}) copy-start(f32[128,128]{1,0:T(8,128)} %get-tuple-element.6) | copy-start | bytes 196612
  83.4 16.4 %all-to-all-start.2 = ((bf16[8,16,1024]{2,1,0:T(8,128)(2,1)}), bf16[8,16,1024]{2,1,0:T(8,128)(2,1)S(1)}, u32[]{:S(2)}, u32[]{:S(2)}) async-start(bf16[8,16,1024]{2,1,0:T(8,128)(2,1)} %bitcast.11), calls=%async_computation.2 | async-start | bytes 524288 | tf_op jit(solution)/shard_map/all_to_all | solution.py:190

commit v9 on v8

--- a/solution.py
+++ b/solution.py
@@ -76,22 +76,35 @@
     lane = lax.broadcasted_iota(jnp.int32, (1, n), 1)
     sub = lax.broadcasted_iota(jnp.int32, (n, 1), 0)
 
-    def step(j, carry):
-        a = lt_ref[...]
-        row = lt_ref[pl.ds(j, 1), :]
-        d = jnp.sum(jnp.where(lane == j, row, 0.0), axis=1, keepdims=True)
-        r = lax.rsqrt(d)
-        l = jnp.where(lane >= j, row * r, 0.0)
-        colj = jnp.sum(jnp.where(cols == j, a, 0.0), axis=1, keepdims=True)
-        c = jnp.where(sub > j, colj * r, 0.0)
-        b_row = inv_ref[pl.ds(j, 1), :] * r
-        lt_ref[...] = a - c * l
-        inv_ref[...] = inv_ref[...] - c * b_row
-        lt_ref[pl.ds(j, 1), :] = l
-        inv_ref[pl.ds(j, 1), :] = b_row
+    def step(t, carry):
+        j = 2 * t
+        a_mat = lt_ref[...]
+        r0 = lt_ref[pl.ds(j, 1), :]
+        r1 = lt_ref[pl.ds(j + 1, 1), :]
+        piv = jnp.sum(jnp.where(lane == j, r0, 0.0), axis=1, keepdims=True)
+        off = jnp.sum(jnp.where(lane == j + 1, r0, 0.0), axis=1, keepdims=True)
+        nxt = jnp.sum(jnp.where(lane == j + 1, r1, 0.0), axis=1, keepdims=True)
+        ra = lax.rsqrt(piv)
+        ratio = off * ra * ra
+        rd = lax.rsqrt(piv * nxt - off * off) * (piv * ra)
+        l0 = jnp.where(lane >= j, r0 * ra, 0.0)
+        l1 = jnp.where(lane >= j + 1, (r1 - r0 * ratio) * rd, 0.0)
+        col0 = jnp.sum(jnp.where(cols == j, a_mat, 0.0), axis=1, keepdims=True)
+        col1 = jnp.sum(jnp.where(cols == j + 1, a_mat, 0.0), axis=1, keepdims=True)
+        below = sub > j + 1
+        c0 = jnp.where(below, col0 * ra, 0.0)
+        c1 = jnp.where(below, (col1 - col0 * ratio) * rd, 0.0)
+        b0 = inv_ref[pl.ds(j, 1), :] * ra
+        b1 = (inv_ref[pl.ds(j + 1, 1), :] - b0 * (off * ra)) * rd
+        lt_ref[...] = a_mat - c0 * l0 - c1 * l1
+        inv_ref[...] = inv_ref[...] - c0 * b0 - c1 * b1
+        lt_ref[pl.ds(j, 1), :] = l0
+        lt_ref[pl.ds(j + 1, 1), :] = l1
+        inv_ref[pl.ds(j, 1), :] = b0
+        inv_ref[pl.ds(j + 1, 1), :] = b1
         return carry
 
-    lax.fori_loop(0, n, step, 0)
+    lax.fori_loop(0, n // 2, step, 0)
 
 
 def chol_inv(g):

time: 101 us -> 96.1 us (0.951)
  Pallas kernels: 14.9 us -> 9.54 us
    pallas_call x1, Pallas kernels: 14.9 us -> 9.54 us  [chol_inv(): pl.pallas_call(chol_inv_kernel, out_shape=(jax.ShapeDtypeStruct((n, n), j...]
where the time goes in v9:
time: 96.1 us; the launch traced here: 95.1 us
  blocking collectives  35 us (36%)
  starting transfers between devices  19.1 us (20%)
  waiting for transfers between devices  14.8 us (15%)
  Pallas kernels  9.54 us (10%)
  other arithmetic  9.51 us (10%)
  matrix products  4.3 us (4%)
  between operations  2.05 us (2%)
    all_to_all x1, blocking collectives, summed_on_arrival(): lax.all_to_all(parts, axis, split_axis=0, concat_axis=0, tiled=True)  20 us
    all_to_all x1, blocking collectives, sent_to_all(): return lax.all_to_all(copies, axis, split_axis=0, concat_axis=0, tiled=True)  15 us
    ppermute x3, starting transfers between devices, butterfly_sum(): value = value + lax.ppermute(value, axis, pairs)  12.2 us
    pallas_call x1, Pallas kernels, chol_inv(): pl.pallas_call(chol_inv_kernel, out_shape=(jax.ShapeDtypeStruct((n, n), j...  9.54 us
    all_to_all x1, waiting for transfers between devices, on_device(): lax.all_to_all(parts, 'pix', split_axis=0, concat_axis=0, tiled=True)  8.3 us
    all_to_all x1, starting transfers between devices, on_device(): lax.all_to_all(parts, 'pix', split_axis=0, concat_axis=0, tiled=True)  6.87 us
    ppermute x3, waiting for transfers between devices, butterfly_sum(): value = value + lax.ppermute(value, axis, pairs)  6.48 us
    convert_element_type x1, other arithmetic, jacobian_planes(): return (real_part.astype(jnp.bfloat16), imag_part.astype(jnp.bfloat16))  4.08 us
  transfers between devices with their start and end apart: 4, of which 4 were waited for; matrix products, arithmetic and copies ran while one was open for 1% of the time, Pallas kernels for 0%

profile of v9, /device:TPU:1, one launch (start us, length us, event | category | flops | bytes accessed | tf_op | source)
XLA Modules:
  0.0 95.1 jit_solution(13554017245150125208)
XLA Ops:
  1.3 0.7 fusion.21
  2.0 0.7 multiply_divide_fusion
  3.4 0.7 fusion.14
  4.1 0.8 fusion.26
  4.9 0.7 exponential_multiply_fusion
  5.6 4.1 %multiply_convert_fusion.1 = (bf16[512,1024]{1,0:T(8,128)(2,1)S(1)}, bf16[512,1024]{1,0:T(8,128)(2,1)S(1)}) fusion(f32[1024]{0:T(1024)S(1)} %bitcast.29, f32[1024]{0:T(1024)S(1)} %bitcast.28, f32[512]{0:T(512)S(1)} %exponential_multiply_fusion, s32[1024]{0:T(1024)S(1)} %get-tuple-element.16, s32[512]{0:T(512)S(1)} %fusion.21, ...), kind=kLoop, calls=%fused_computation.21 | loop fusion | flops 28835840 | bytes 2125828 | tf_op jit(solution)/shard_map/convert_element_type | solution.py:158
  9.7 0.7 fusion.10
  10.4 20.0 %all_to_all.15 = f32[32,32,128]{2,1,0:T(8,128)S(1)} all-to-all(f32[32,32,128]{2,1,0:T(8,128)S(1)} %bitcast.22), channel_id=1, replica_groups=mesh['act'=32,'pix'=8] {'act'}, dimensions={0} | all-to-all | bytes 1048576 | tf_op jit(solution)/shard_map/all_to_all | solution.py:49
  30.5 15.0 %all_to_all.16 = f32[32,32,128]{2,1,0:T(8,128)S(1)} all-to-all(f32[32,32,128]{2,1,0:T(8,128)S(1)} %broadcast_in_dim.2), channel_id=1, replica_groups=mesh['act'=32,'pix'=8] {'act'}, dimensions={0} | all-to-all | bytes 1048576 | tf_op jit(solution)/shard_map/all_to_all | solution.py:28
  45.5 1.0 %convolution_bitcast_fusion = f32[128,128]{1,0:T(8,128)S(1)} fusion(f32[32,32,128]{2,1,0:T(8,128)S(1)} %all_to_all.16), kind=kOutput, calls=%fused_computation.30 | convolution fusion | flops 201326592 | bytes 589824 | tf_op jit(solution)/shard_map/dot_general | solution.py:162
  46.5 1.7 %collective-permute-start = (f32[128,128]{1,0:T(8,128)S(1)}, f32[128,128]{1,0:T(8,128)S(1)}, u32[]{:S(2)}, u32[]{:S(2)}) collective-permute-start(f32[128,128]{1,0:T(8,128)S(1)} %convolution_bitcast_fusion), channel_id=1, source_target_pairs={{0,1},{1,0},{2,3},{3,2},{4,5},{5,4},{6,7},{7,6},{8,9},{9,8},{10,11... | collective-permute-start | bytes 196616 | tf_op jit(solution)/shard_map/ppermute | solution.py:65
  48.2 2.6 %collective-permute-done = f32[128,128]{1,0:T(8,128)S(1)} collective-permute-done((f32[128,128]{1,0:T(8,128)S(1)}, f32[128,128]{1,0:T(8,128)S(1)}, u32[]{:S(2)}, u32[]{:S(2)}) %collective-permute-start) | collective-permute-done | bytes 65568 | tf_op jit(solution)/shard_map/ppermute | solution.py:65
  50.9 3.1 %collective-permute-start.1 = (f32[128,128]{1,0:T(8,128)S(1)}, f32[128,128]{1,0:T(8,128)S(1)}, u32[]{:S(2)}, u32[]{:S(2)}) collective-permute-start(f32[128,128]{1,0:T(8,128)S(1)} %add.162), channel_id=1, source_target_pairs={{0,2},{1,3},{2,0},{3,1},{4,6},{5,7},{6,4},{7,5},{8,10},{9,11},{10,... | collective-permute-start | bytes 196616 | tf_op jit(solution)/shard_map/ppermute | solution.py:65
  54.0 2.1 %collective-permute-done.1 = f32[128,128]{1,0:T(8,128)S(1)} collective-permute-done((f32[128,128]{1,0:T(8,128)S(1)}, f32[128,128]{1,0:T(8,128)S(1)}, u32[]{:S(2)}, u32[]{:S(2)}) %collective-permute-start.1) | collective-permute-done | bytes 65568 | tf_op jit(solution)/shard_map/ppermute | solution.py:65
  56.0 7.4 %collective-permute-start.2 = (f32[128,128]{1,0:T(8,128)S(1)}, f32[128,128]{1,0:T(8,128)S(1)}, u32[]{:S(2)}, u32[]{:S(2)}) collective-permute-start(f32[128,128]{1,0:T(8,128)S(1)} %add.163), channel_id=1, source_target_pairs={{0,4},{1,5},{2,6},{3,7},{4,0},{5,1},{6,2},{7,3},{8,12},{9,13},{10,... | collective-permute-start | bytes 196616 | tf_op jit(solution)/shard_map/ppermute | solution.py:65
  63.5 1.8 %collective-permute-done.2 = f32[128,128]{1,0:T(8,128)S(1)} collective-permute-done((f32[128,128]{1,0:T(8,128)S(1)}, f32[128,128]{1,0:T(8,128)S(1)}, u32[]{:S(2)}, u32[]{:S(2)}) %collective-permute-start.2) | collective-permute-done | bytes 65568 | tf_op jit(solution)/shard_map/ppermute | solution.py:65
  65.2 0.6 add.164.g_ref
  65.9 9.5 %shard_map.85 = (f32[128,128]{1,0:T(8,128)}, f32[128,128]{1,0:T(8,128)}) custom-call(f32[128,128]{1,0:T(8,128)} %add.164.g_ref), custom_call_target="tpu_custom_call" | custom-call | tf_op jit(solution)/shard_map/pallas_call | solution.py:112
  75.4 1.4 %fusion.27 = f32[1024,128]{1,0:T(8,128)S(1)} fusion(f32[1024,128]{1,0:T(8,128)S(1)} %bitcast.21, f32[128,128]{1,0:T(8,128)} %get-tuple-element.5), kind=kOutput, calls=%fused_computation.72 | convolution fusion | flops 201326592 | bytes 1114112 | tf_op jit(solution)/shard_map/dot_general | solution.py:187
  76.9 1.2 %fusion.11 = bf16[128,1024]{1,0:T(8,128)(2,1)} fusion(bf16[512,1024]{1,0:T(8,128)(2,1)S(1)} %get-tuple-element.12, bf16[512,1024]{1,0:T(8,128)(2,1)S(1)} %get-tuple-element.11, f32[1024,128]{1,0:T(8,128)S(1)} %fusion.27), kind=kOutput, calls=%fused_computation.29 | convolution fusion | flops 272891904 | bytes 2883584 | tf_op jit(solution)/shard_map/dot_general | solution.py:199
  78.0 6.9 %all-to-all-start.2 = ((bf16[8,16,1024]{2,1,0:T(8,128)(2,1)}), bf16[8,16,1024]{2,1,0:T(8,128)(2,1)S(1)}, u32[]{:S(2)}, u32[]{:S(2)}) async-start(bf16[8,16,1024]{2,1,0:T(8,128)(2,1)} %bitcast.11), calls=%async_computation.2 | async-start | bytes 524288 | tf_op jit(solution)/shard_map/all_to_all | solution.py:203
  85.5 0.6 broadcast_multiply_fusion
  86.2 8.3 %all-to-all-done.2 = bf16[8,16,1024]{2,1,0:T(8,128)(2,1)S(1)} async-done(((bf16[8,16,1024]{2,1,0:T(8,128)(2,1)}), bf16[8,16,1024]{2,1,0:T(8,128)(2,1)S(1)}, u32[]{:S(2)}, u32[]{:S(2)}) %all-to-all-start.2) | async-done | bytes 262176 | tf_op jit(solution)/shard_map/all_to_all | solution.py:203
  94.5 0.7 convert_reduce_fusion
  (10 shorter events, 0.8 us)
Async XLA Ops:
  0.6 9.0 %copy-start = (bf16[1024,128]{1,0:T(8,128)(2,1)S(1)}, bf16[1024,128]{1,0:T(8,128)(2,1)}, u32[]{:S(2)}) copy-start(bf16[1024,128]{1,0:T(8,128)(2,1)} %param.8) | copy-start | bytes 786436
  46.5 4.4 %collective-permute-start = (f32[128,128]{1,0:T(8,128)S(1)}, f32[128,128]{1,0:T(8,128)S(1)}, u32[]{:S(2)}, u32[]{:S(2)}) collective-permute-start(f32[128,128]{1,0:T(8,128)S(1)} %convolution_bitcast_fusion), channel_id=1, source_target_pairs={{0,1},{1,0},{2,3},{3,2},{4,5},{5,4},{6,7},{7,6},{8,9},{9,8},{10,11... | collective-permute-start | bytes 196616 | tf_op jit(solution)/shard_map/ppermute | solution.py:65
  50.9 5.2 %collective-permute-start.1 = (f32[128,128]{1,0:T(8,128)S(1)}, f32[128,128]{1,0:T(8,128)S(1)}, u32[]{:S(2)}, u32[]{:S(2)}) collective-permute-start(f32[128,128]{1,0:T(8,128)S(1)} %add.162), channel_id=1, source_target_pairs={{0,2},{1,3},{2,0},{3,1},{4,6},{5,7},{6,4},{7,5},{8,10},{9,11},{10,... | collective-permute-start | bytes 196616 | tf_op jit(solution)/shard_map/ppermute | solution.py:65
  56.0 9.2 %collective-permute-start.2 = (f32[128,128]{1,0:T(8,128)S(1)}, f32[128,128]{1,0:T(8,128)S(1)}, u32[]{:S(2)}, u32[]{:S(2)}) collective-permute-start(f32[128,128]{1,0:T(8,128)S(1)} %add.163), channel_id=1, source_target_pairs={{0,4},{1,5},{2,6},{3,7},{4,0},{5,1},{6,2},{7,3},{8,12},{9,13},{10,... | collective-permute-start | bytes 196616 | tf_op jit(solution)/shard_map/ppermute | solution.py:65
  76.8 8.7 %copy-start.1 = (f32[128,128]{1,0:T(8,128)S(1)}, f32[128,128]{1,0:T(8,128)}, u32[]{:S(2)}) copy-start(f32[128,128]{1,0:T(8,128)} %get-tuple-element.6) | copy-start | bytes 196612
  78.0 16.4 %all-to-all-start.2 = ((bf16[8,16,1024]{2,1,0:T(8,128)(2,1)}), bf16[8,16,1024]{2,1,0:T(8,128)(2,1)S(1)}, u32[]{:S(2)}, u32[]{:S(2)}) async-start(bf16[8,16,1024]{2,1,0:T(8,128)(2,1)} %bitcast.11), calls=%async_computation.2 | async-start | bytes 524288 | tf_op jit(solution)/shard_map/all_to_all | solution.py:203

commit v10 on v8

--- a/solution.py
+++ b/solution.py
@@ -67,6 +67,9 @@
     return value
 
 
+STEP = 4
+
+
 def chol_inv_kernel(g_ref, lt_ref, inv_ref):
     n = g_ref.shape[0]
     lt_ref[...] = g_ref[...]
@@ -76,22 +79,52 @@
     lane = lax.broadcasted_iota(jnp.int32, (1, n), 1)
     sub = lax.broadcasted_iota(jnp.int32, (n, 1), 0)
 
-    def step(j, carry):
-        a = lt_ref[...]
-        row = lt_ref[pl.ds(j, 1), :]
-        d = jnp.sum(jnp.where(lane == j, row, 0.0), axis=1, keepdims=True)
-        r = lax.rsqrt(d)
-        l = jnp.where(lane >= j, row * r, 0.0)
-        colj = jnp.sum(jnp.where(cols == j, a, 0.0), axis=1, keepdims=True)
-        c = jnp.where(sub > j, colj * r, 0.0)
-        b_row = inv_ref[pl.ds(j, 1), :] * r
-        lt_ref[...] = a - c * l
-        inv_ref[...] = inv_ref[...] - c * b_row
-        lt_ref[pl.ds(j, 1), :] = l
-        inv_ref[pl.ds(j, 1), :] = b_row
+    def step(t, carry):
+        j = STEP * t
+        a_mat = lt_ref[...]
+        r = [lt_ref[pl.ds(j + i, 1), :] for i in range(STEP)]
+        blk = {}
+        for i in range(STEP):
+            for k in range(i, STEP):
+                blk[i, k] = jnp.sum(jnp.where(lane == j + k, r[i], 0.0), axis=1, keepdims=True)
+        low, inv = {}, []
+        for i in range(STEP):
+            s = blk[i, i]
+            for k in range(i):
+                s = s - low[i, k] * low[i, k]
+            inv.append(lax.rsqrt(s))
+            for m in range(i + 1, STEP):
+                v = blk[i, m]
+                for k in range(i):
+                    v = v - low[m, k] * low[i, k]
+                low[m, i] = v * inv[i]
+        below = sub >= j + STEP
+        l_rows, b_rows, c_cols = [], [], []
+        for i in range(STEP):
+            lv = r[i]
+            bv = inv_ref[pl.ds(j + i, 1), :]
+            cv = jnp.sum(jnp.where(cols == j + i, a_mat, 0.0), axis=1, keepdims=True)
+            for k in range(i):
+                lv = lv - low[i, k] * l_rows[k]
+                bv = bv - low[i, k] * b_rows[k]
+                cv = cv - low[i, k] * c_cols[k]
+            l_rows.append(jnp.where(lane >= j + i, lv * inv[i], 0.0))
+            b_rows.append(bv * inv[i])
+            c_cols.append(cv * inv[i])
+        new_a = a_mat
+        new_b = inv_ref[...]
+        for i in range(STEP):
+            c = jnp.where(below, c_cols[i], 0.0)
+            new_a = new_a - c * l_rows[i]
+            new_b = new_b - c * b_rows[i]
+        lt_ref[...] = new_a
+        inv_ref[...] = new_b
+        for i in range(STEP):
+            lt_ref[pl.ds(j + i, 1), :] = l_rows[i]
+            inv_ref[pl.ds(j + i, 1), :] = b_rows[i]
         return carry
 
-    lax.fori_loop(0, n, step, 0)
+    lax.fori_loop(0, n // STEP, step, 0)
 
 
 def chol_inv(g):

time: 101 us -> 94.1 us (0.932)
  Pallas kernels: 14.9 us -> 7.57 us
    pallas_call x1, Pallas kernels: 14.9 us -> 7.57 us  [chol_inv(): pl.pallas_call(chol_inv_kernel, out_shape=(jax.ShapeDtypeStruct((n, n), j...]
where the time goes in v10:
time: 94.1 us; the launch traced here: 93.2 us
  blocking collectives  35 us (37%)
  starting transfers between devices  19.1 us (20%)
  waiting for transfers between devices  14.8 us (16%)
  other arithmetic  9.51 us (10%)
  Pallas kernels  7.57 us (8%)
  matrix products  4.3 us (5%)
  between operations  2.05 us (2%)
    all_to_all x1, blocking collectives, summed_on_arrival(): lax.all_to_all(parts, axis, split_axis=0, concat_axis=0, tiled=True)  20 us
    all_to_all x1, blocking collectives, sent_to_all(): return lax.all_to_all(copies, axis, split_axis=0, concat_axis=0, tiled=True)  15 us
    ppermute x3, starting transfers between devices, butterfly_sum(): value = value + lax.ppermute(value, axis, pairs)  12.2 us
    all_to_all x1, waiting for transfers between devices, on_device(): lax.all_to_all(parts, 'pix', split_axis=0, concat_axis=0, tiled=True)  8.31 us
    pallas_call x1, Pallas kernels, chol_inv(): pl.pallas_call(chol_inv_kernel, out_shape=(jax.ShapeDtypeStruct((n, n), j...  7.57 us
    all_to_all x1, starting transfers between devices, on_device(): lax.all_to_all(parts, 'pix', split_axis=0, concat_axis=0, tiled=True)  6.87 us
    ppermute x3, waiting for transfers between devices, butterfly_sum(): value = value + lax.ppermute(value, axis, pairs)  6.48 us
    convert_element_type x1, other arithmetic, jacobian_planes(): return (real_part.astype(jnp.bfloat16), imag_part.astype(jnp.bfloat16))  4.08 us
  transfers between devices with their start and end apart: 4, of which 4 were waited for; matrix products, arithmetic and copies ran while one was open for 1% of the time, Pallas kernels for 0%

profile of v10, /device:TPU:1, one launch (start us, length us, event | category | flops | bytes accessed | tf_op | source)
XLA Modules:
  0.0 93.2 jit_solution(8278223065495274223)
XLA Ops:
  1.3 0.7 fusion.21
  2.0 0.7 multiply_divide_fusion
  3.4 0.7 fusion.14
  4.1 0.8 fusion.26
  4.9 0.7 exponential_multiply_fusion
  5.6 4.1 %multiply_convert_fusion.1 = (bf16[512,1024]{1,0:T(8,128)(2,1)S(1)}, bf16[512,1024]{1,0:T(8,128)(2,1)S(1)}) fusion(f32[1024]{0:T(1024)S(1)} %bitcast.29, f32[1024]{0:T(1024)S(1)} %bitcast.28, f32[512]{0:T(512)S(1)} %exponential_multiply_fusion, s32[1024]{0:T(1024)S(1)} %get-tuple-element.16, s32[512]{0:T(512)S(1)} %fusion.21, ...), kind=kLoop, calls=%fused_computation.21 | loop fusion | flops 28835840 | bytes 2125828 | tf_op jit(solution)/shard_map/convert_element_type | solution.py:178
  9.7 0.7 fusion.10
  10.4 20.0 %all_to_all.15 = f32[32,32,128]{2,1,0:T(8,128)S(1)} all-to-all(f32[32,32,128]{2,1,0:T(8,128)S(1)} %bitcast.22), channel_id=1, replica_groups=mesh['act'=32,'pix'=8] {'act'}, dimensions={0} | all-to-all | bytes 1048576 | tf_op jit(solution)/shard_map/all_to_all | solution.py:49
  30.5 15.0 %all_to_all.16 = f32[32,32,128]{2,1,0:T(8,128)S(1)} all-to-all(f32[32,32,128]{2,1,0:T(8,128)S(1)} %broadcast_in_dim.2), channel_id=1, replica_groups=mesh['act'=32,'pix'=8] {'act'}, dimensions={0} | all-to-all | bytes 1048576 | tf_op jit(solution)/shard_map/all_to_all | solution.py:28
  45.5 1.0 %convolution_bitcast_fusion = f32[128,128]{1,0:T(8,128)S(1)} fusion(f32[32,32,128]{2,1,0:T(8,128)S(1)} %all_to_all.16), kind=kOutput, calls=%fused_computation.30 | convolution fusion | flops 201326592 | bytes 589824 | tf_op jit(solution)/shard_map/dot_general | solution.py:182
  46.5 1.7 %collective-permute-start = (f32[128,128]{1,0:T(8,128)S(1)}, f32[128,128]{1,0:T(8,128)S(1)}, u32[]{:S(2)}, u32[]{:S(2)}) collective-permute-start(f32[128,128]{1,0:T(8,128)S(1)} %convolution_bitcast_fusion), channel_id=1, source_target_pairs={{0,1},{1,0},{2,3},{3,2},{4,5},{5,4},{6,7},{7,6},{8,9},{9,8},{10,11... | collective-permute-start | bytes 196616 | tf_op jit(solution)/shard_map/ppermute | solution.py:65
  48.2 2.6 %collective-permute-done = f32[128,128]{1,0:T(8,128)S(1)} collective-permute-done((f32[128,128]{1,0:T(8,128)S(1)}, f32[128,128]{1,0:T(8,128)S(1)}, u32[]{:S(2)}, u32[]{:S(2)}) %collective-permute-start) | collective-permute-done | bytes 65568 | tf_op jit(solution)/shard_map/ppermute | solution.py:65
  50.9 3.1 %collective-permute-start.1 = (f32[128,128]{1,0:T(8,128)S(1)}, f32[128,128]{1,0:T(8,128)S(1)}, u32[]{:S(2)}, u32[]{:S(2)}) collective-permute-start(f32[128,128]{1,0:T(8,128)S(1)} %add.162), channel_id=1, source_target_pairs={{0,2},{1,3},{2,0},{3,1},{4,6},{5,7},{6,4},{7,5},{8,10},{9,11},{10,... | collective-permute-start | bytes 196616 | tf_op jit(solution)/shard_map/ppermute | solution.py:65
  54.0 2.1 %collective-permute-done.1 = f32[128,128]{1,0:T(8,128)S(1)} collective-permute-done((f32[128,128]{1,0:T(8,128)S(1)}, f32[128,128]{1,0:T(8,128)S(1)}, u32[]{:S(2)}, u32[]{:S(2)}) %collective-permute-start.1) | collective-permute-done | bytes 65568 | tf_op jit(solution)/shard_map/ppermute | solution.py:65
  56.0 7.4 %collective-permute-start.2 = (f32[128,128]{1,0:T(8,128)S(1)}, f32[128,128]{1,0:T(8,128)S(1)}, u32[]{:S(2)}, u32[]{:S(2)}) collective-permute-start(f32[128,128]{1,0:T(8,128)S(1)} %add.163), channel_id=1, source_target_pairs={{0,4},{1,5},{2,6},{3,7},{4,0},{5,1},{6,2},{7,3},{8,12},{9,13},{10,... | collective-permute-start | bytes 196616 | tf_op jit(solution)/shard_map/ppermute | solution.py:65
  63.5 1.8 %collective-permute-done.2 = f32[128,128]{1,0:T(8,128)S(1)} collective-permute-done((f32[128,128]{1,0:T(8,128)S(1)}, f32[128,128]{1,0:T(8,128)S(1)}, u32[]{:S(2)}, u32[]{:S(2)}) %collective-permute-start.2) | collective-permute-done | bytes 65568 | tf_op jit(solution)/shard_map/ppermute | solution.py:65
  65.2 0.6 add.164.g_ref
  65.9 7.6 %shard_map.85 = (f32[128,128]{1,0:T(8,128)}, f32[128,128]{1,0:T(8,128)}) custom-call(f32[128,128]{1,0:T(8,128)} %add.164.g_ref), custom_call_target="tpu_custom_call" | custom-call | tf_op jit(solution)/shard_map/pallas_call | solution.py:132
  73.4 1.4 %fusion.27 = f32[1024,128]{1,0:T(8,128)S(1)} fusion(f32[1024,128]{1,0:T(8,128)S(1)} %bitcast.21, f32[128,128]{1,0:T(8,128)} %get-tuple-element.5), kind=kOutput, calls=%fused_computation.72 | convolution fusion | flops 201326592 | bytes 1114112 | tf_op jit(solution)/shard_map/dot_general | solution.py:207
  74.9 1.2 %fusion.11 = bf16[128,1024]{1,0:T(8,128)(2,1)} fusion(bf16[512,1024]{1,0:T(8,128)(2,1)S(1)} %get-tuple-element.12, bf16[512,1024]{1,0:T(8,128)(2,1)S(1)} %get-tuple-element.11, f32[1024,128]{1,0:T(8,128)S(1)} %fusion.27), kind=kOutput, calls=%fused_computation.29 | convolution fusion | flops 272891904 | bytes 2883584 | tf_op jit(solution)/shard_map/dot_general | solution.py:219
  76.1 6.9 %all-to-all-start.2 = ((bf16[8,16,1024]{2,1,0:T(8,128)(2,1)}), bf16[8,16,1024]{2,1,0:T(8,128)(2,1)S(1)}, u32[]{:S(2)}, u32[]{:S(2)}) async-start(bf16[8,16,1024]{2,1,0:T(8,128)(2,1)} %bitcast.11), calls=%async_computation.2 | async-start | bytes 524288 | tf_op jit(solution)/shard_map/all_to_all | solution.py:223
  83.6 0.6 broadcast_multiply_fusion
  84.2 8.3 %all-to-all-done.2 = bf16[8,16,1024]{2,1,0:T(8,128)(2,1)S(1)} async-done(((bf16[8,16,1024]{2,1,0:T(8,128)(2,1)}), bf16[8,16,1024]{2,1,0:T(8,128)(2,1)S(1)}, u32[]{:S(2)}, u32[]{:S(2)}) %all-to-all-start.2) | async-done | bytes 262176 | tf_op jit(solution)/shard_map/all_to_all | solution.py:223
  92.5 0.7 convert_reduce_fusion
  (10 shorter events, 0.8 us)
Async XLA Ops:
  0.6 9.0 %copy-start = (bf16[1024,128]{1,0:T(8,128)(2,1)S(1)}, bf16[1024,128]{1,0:T(8,128)(2,1)}, u32[]{:S(2)}) copy-start(bf16[1024,128]{1,0:T(8,128)(2,1)} %param.8) | copy-start | bytes 786436
  46.5 4.4 %collective-permute-start = (f32[128,128]{1,0:T(8,128)S(1)}, f32[128,128]{1,0:T(8,128)S(1)}, u32[]{:S(2)}, u32[]{:S(2)}) collective-permute-start(f32[128,128]{1,0:T(8,128)S(1)} %convolution_bitcast_fusion), channel_id=1, source_target_pairs={{0,1},{1,0},{2,3},{3,2},{4,5},{5,4},{6,7},{7,6},{8,9},{9,8},{10,11... | collective-permute-start | bytes 196616 | tf_op jit(solution)/shard_map/ppermute | solution.py:65
  50.9 5.2 %collective-permute-start.1 = (f32[128,128]{1,0:T(8,128)S(1)}, f32[128,128]{1,0:T(8,128)S(1)}, u32[]{:S(2)}, u32[]{:S(2)}) collective-permute-start(f32[128,128]{1,0:T(8,128)S(1)} %add.162), channel_id=1, source_target_pairs={{0,2},{1,3},{2,0},{3,1},{4,6},{5,7},{6,4},{7,5},{8,10},{9,11},{10,... | collective-permute-start | bytes 196616 | tf_op jit(solution)/shard_map/ppermute | solution.py:65
  56.0 9.2 %collective-permute-start.2 = (f32[128,128]{1,0:T(8,128)S(1)}, f32[128,128]{1,0:T(8,128)S(1)}, u32[]{:S(2)}, u32[]{:S(2)}) collective-permute-start(f32[128,128]{1,0:T(8,128)S(1)} %add.163), channel_id=1, source_target_pairs={{0,4},{1,5},{2,6},{3,7},{4,0},{5,1},{6,2},{7,3},{8,12},{9,13},{10,... | collective-permute-start | bytes 196616 | tf_op jit(solution)/shard_map/ppermute | solution.py:65
  74.9 8.7 %copy-start.1 = (f32[128,128]{1,0:T(8,128)S(1)}, f32[128,128]{1,0:T(8,128)}, u32[]{:S(2)}) copy-start(f32[128,128]{1,0:T(8,128)} %get-tuple-element.6) | copy-start | bytes 196612
  76.1 16.4 %all-to-all-start.2 = ((bf16[8,16,1024]{2,1,0:T(8,128)(2,1)}), bf16[8,16,1024]{2,1,0:T(8,128)(2,1)S(1)}, u32[]{:S(2)}, u32[]{:S(2)}) async-start(bf16[8,16,1024]{2,1,0:T(8,128)(2,1)} %bitcast.11), calls=%async_computation.2 | async-start | bytes 524288 | tf_op jit(solution)/shard_map/all_to_all | solution.py:223

commit v11 on v10

--- a/solution.py
+++ b/solution.py
@@ -178,6 +178,49 @@
     return real_part.astype(jnp.bfloat16), imag_part.astype(jnp.bfloat16)
 
 
+BLOCK = 64
+
+def jac_kernel(pix_ref, code_ref, field_ref, scale_ref, flux_ref, omega_ref, jac_ref, sketch_ref):
+    npix = pix_ref.shape[1]
+    wave_scale = scale_ref[0]
+    flux_level = flux_ref[0]
+    pixels = pix_ref[...]
+    delta_u = pixels // FOCAL - FOCAL // 2
+    delta_v = pixels % FOCAL - FOCAL // 2
+    radius = (delta_u * delta_u + delta_v * delta_v).astype(jnp.float32)
+    amplitude = flux_level * jnp.exp(-INFL_RATE * radius / (FOCAL * FOCAL))
+    defocus = radius * (TWO_PI * DEFOCUS_RATE / (FOCAL * FOCAL)) / wave_scale
+    zero = jnp.zeros_like(radius)
+    terms = jnp.concatenate(
+        [delta_u.astype(jnp.float32), delta_v.astype(jnp.float32), amplitude, defocus, zero, zero, zero, zero], axis=0
+    ).T
+    codes = code_ref[...]
+    mirror = (codes // (GRID * GRID)).astype(jnp.float32)
+    col_x = (codes // GRID % GRID - GRID // 2).astype(jnp.float32)
+    col_y = (codes % GRID - GRID // 2).astype(jnp.float32)
+    e_re = field_ref[0:1, :]
+    e_im = field_ref[1:2, :]
+    rate = TWO_PI / FOCAL * wave_scale
+    for b in range(npix // BLOCK):
+        t = terms[b * BLOCK : (b + 1) * BLOCK]
+        du, dv, amp, defo = t[:, 0:1], t[:, 1:2], t[:, 2:3], t[:, 3:4]
+        phase = mirror * defo - rate * (du * col_x + dv * col_y)
+        sine, cosine = sin_cos(phase)
+        jac_ref[b * BLOCK : (b + 1) * BLOCK, :] = (amp * (e_re * cosine - e_im * sine)).astype(jnp.bfloat16)
+        jac_ref[npix + b * BLOCK : npix + (b + 1) * BLOCK, :] = (amp * (e_re * sine + e_im * cosine)).astype(jnp.bfloat16)
+    sketch_ref[...] = jnp.dot(jac_ref[...], omega_ref[...], preferred_element_type=jnp.float32)
+
+def jac_and_sketch(pixel_row, codes_row, field, scale, flux, omega):
+    npix = pixel_row.shape[1]; nact = codes_row.shape[1]
+    vm = pl.BlockSpec(memory_space=pltpu.VMEM)
+    return pl.pallas_call(
+        jac_kernel,
+        out_shape=(jax.ShapeDtypeStruct((2 * npix, nact), jnp.bfloat16), jax.ShapeDtypeStruct((2 * npix, omega.shape[1]), jnp.float32)),
+        in_specs=[vm, vm, vm, pl.BlockSpec(memory_space=pltpu.SMEM), pl.BlockSpec(memory_space=pltpu.SMEM), vm],
+        out_specs=(vm, vm),
+    )(pixel_row, codes_row, field, scale, flux, omega)
+
+
 def gram_of(sketch):
     return lax.dot_general(
         sketch,
@@ -196,11 +239,9 @@
     pix_count = lax.axis_size("pix")
     total_rows = rows_dev * pix_count
     share_pix = npix // act_count
-    real_rows, imag_rows = jacobian_planes(
-        pixels, channel_scale[0], channel_flux[0], act_map, pupil_field[0, 0], pupil_field[0, 1]
-    )
-    jac = jnp.concatenate([real_rows, imag_rows], axis=0)
-    partial_sketch = jnp.dot(jac, omega, preferred_element_type=jnp.float32)
+    jac, partial_sketch = jac_and_sketch(
+        pixel_index, act_map[None, :], pupil_field[0], channel_scale, channel_flux, omega
+    )
     sketch = sum_by_parts(partial_sketch, "act")
     gram_matrix = butterfly_sum(gram_of(sketch), "pix")
     upper_factor, lower_inverse = chol_inv(gram_matrix)

time: 94.1 us -> 92.7 us (0.985)
  other arithmetic: 9.51 us -> 2.63 us
  Pallas kernels: 7.57 us -> 14.3 us
    pallas_call x0 -> x1, Pallas kernels: none -> 6.73 us  [jac_and_sketch(): pl.pallas_call(jac_kernel, out_shape=(jax.ShapeDtypeStruct((2 * npix, nac...]
    convert_element_type x2 -> x0, other arithmetic: 4.79 us -> none  [the longest x1 4.08 us: jacobian_planes(): return (real_part.astype(jnp.bfloat16), imag_part.astype(jnp.bfloat16))]
where the time goes in v11:
time: 92.7 us; the launch traced here: 91.8 us
  blocking collectives  35.3 us (38%)
  starting transfers between devices  19.1 us (21%)
  waiting for transfers between devices  14.7 us (16%)
  Pallas kernels  14.3 us (15%)
  matrix products  3.62 us (4%)
  other arithmetic  2.63 us (3%)
  between operations  1.98 us (2%)
    all_to_all x1, blocking collectives, summed_on_arrival(): lax.all_to_all(parts, axis, split_axis=0, concat_axis=0, tiled=True)  20.2 us
    all_to_all x1, blocking collectives, sent_to_all(): return lax.all_to_all(copies, axis, split_axis=0, concat_axis=0, tiled=True)  15.1 us
    ppermute x3, starting transfers between devices, butterfly_sum(): value = value + lax.ppermute(value, axis, pairs)  12.2 us
    all_to_all x1, waiting for transfers between devices, on_device(): lax.all_to_all(parts, 'pix', split_axis=0, concat_axis=0, tiled=True)  8.27 us
    pallas_call x1, Pallas kernels, chol_inv(): pl.pallas_call(chol_inv_kernel, out_shape=(jax.ShapeDtypeStruct((n, n), j...  7.58 us
    all_to_all x1, starting transfers between devices, on_device(): lax.all_to_all(parts, 'pix', split_axis=0, concat_axis=0, tiled=True)  6.88 us
    pallas_call x1, Pallas kernels, jac_and_sketch(): pl.pallas_call(jac_kernel, out_shape=(jax.ShapeDtypeStruct((2 * npix, nac...  6.73 us
    ppermute x3, waiting for transfers between devices, butterfly_sum(): value = value + lax.ppermute(value, axis, pairs)  6.48 us
  transfers between devices with their start and end apart: 4, of which 4 were waited for; matrix products, arithmetic and copies ran while one was open for 1% of the time, Pallas kernels for 0%

profile of v11, /device:TPU:1, one launch (start us, length us, event | category | flops | bytes accessed | tf_op | source)
XLA Modules:
  0.0 91.8 jit_solution(13309127055404485100)
XLA Ops:
  1.9 6.7 %shard_map.85 = (bf16[1024,1024]{1,0:T(8,128)(2,1)}, f32[1024,128]{1,0:T(8,128)}) custom-call(s32[1,512]{1,0:T(1,128)} %pix_ref.1, s32[1,1024]{1,0:T(1,128)} %bitcast.21, f32[2,1024]{1,0:T(2,128)} %bitcast.20, f32[1]{0:T(128)S(6)} %copy.9.scale_ref, f32[1]{0:T(128)S(6)} %copy.10.flux_ref, bf16[1024,128]{1,0:T(8,128)(2,1)} %omega_ref.1), custom_call_target="tpu_custom_call" | custom-call | tf_op jit(solution)/shard_map/pallas_call | solution.py:216
  8.7 20.2 %all_to_all.15 = f32[32,32,128]{2,1,0:T(8,128)S(1)} all-to-all(f32[32,32,128]{2,1,0:T(8,128)} %bitcast.16), channel_id=1, replica_groups=mesh['act'=32,'pix'=8] {'act'}, dimensions={0} | all-to-all | bytes 1048576 | tf_op jit(solution)/shard_map/all_to_all | solution.py:49
  28.9 0.1 broadcast_in_dim.7
  28.9 0.0 copy-start
  28.9 15.1 %all_to_all.16 = f32[32,32,128]{2,1,0:T(8,128)S(1)} all-to-all(f32[32,32,128]{2,1,0:T(8,128)S(1)} %broadcast_in_dim.7), channel_id=1, replica_groups=mesh['act'=32,'pix'=8] {'act'}, dimensions={0} | all-to-all | bytes 1048576 | tf_op jit(solution)/shard_map/all_to_all | solution.py:28
  44.1 1.0 %convolution_bitcast_fusion = f32[128,128]{1,0:T(8,128)S(1)} fusion(f32[32,32,128]{2,1,0:T(8,128)S(1)} %all_to_all.16), kind=kOutput, calls=%fused_computation.1 | convolution fusion | flops 201326592 | bytes 589824 | tf_op jit(solution)/shard_map/dot_general | solution.py:225
  45.1 1.7 %collective-permute-start = (f32[128,128]{1,0:T(8,128)S(1)}, f32[128,128]{1,0:T(8,128)S(1)}, u32[]{:S(2)}, u32[]{:S(2)}) collective-permute-start(f32[128,128]{1,0:T(8,128)S(1)} %convolution_bitcast_fusion), channel_id=1, source_target_pairs={{0,1},{1,0},{2,3},{3,2},{4,5},{5,4},{6,7},{7,6},{8,9},{9,8},{10,11... | collective-permute-start | bytes 196616 | tf_op jit(solution)/shard_map/ppermute | solution.py:65
  46.8 2.6 %collective-permute-done = f32[128,128]{1,0:T(8,128)S(1)} collective-permute-done((f32[128,128]{1,0:T(8,128)S(1)}, f32[128,128]{1,0:T(8,128)S(1)}, u32[]{:S(2)}, u32[]{:S(2)}) %collective-permute-start) | collective-permute-done | bytes 65568 | tf_op jit(solution)/shard_map/ppermute | solution.py:65
  49.5 3.1 %collective-permute-start.1 = (f32[128,128]{1,0:T(8,128)S(1)}, f32[128,128]{1,0:T(8,128)S(1)}, u32[]{:S(2)}, u32[]{:S(2)}) collective-permute-start(f32[128,128]{1,0:T(8,128)S(1)} %add.17), channel_id=1, source_target_pairs={{0,2},{1,3},{2,0},{3,1},{4,6},{5,7},{6,4},{7,5},{8,10},{9,11},{10,... | collective-permute-start | bytes 196616 | tf_op jit(solution)/shard_map/ppermute | solution.py:65
  52.6 2.1 %collective-permute-done.1 = f32[128,128]{1,0:T(8,128)S(1)} collective-permute-done((f32[128,128]{1,0:T(8,128)S(1)}, f32[128,128]{1,0:T(8,128)S(1)}, u32[]{:S(2)}, u32[]{:S(2)}) %collective-permute-start.1) | collective-permute-done | bytes 65568 | tf_op jit(solution)/shard_map/ppermute | solution.py:65
  54.7 7.4 %collective-permute-start.2 = (f32[128,128]{1,0:T(8,128)S(1)}, f32[128,128]{1,0:T(8,128)S(1)}, u32[]{:S(2)}, u32[]{:S(2)}) collective-permute-start(f32[128,128]{1,0:T(8,128)S(1)} %add.18), channel_id=1, source_target_pairs={{0,4},{1,5},{2,6},{3,7},{4,0},{5,1},{6,2},{7,3},{8,12},{9,13},{10,... | collective-permute-start | bytes 196616 | tf_op jit(solution)/shard_map/ppermute | solution.py:65
  62.1 1.8 %collective-permute-done.2 = f32[128,128]{1,0:T(8,128)S(1)} collective-permute-done((f32[128,128]{1,0:T(8,128)S(1)}, f32[128,128]{1,0:T(8,128)S(1)}, u32[]{:S(2)}, u32[]{:S(2)}) %collective-permute-start.2) | collective-permute-done | bytes 65568 | tf_op jit(solution)/shard_map/ppermute | solution.py:65
  63.8 0.6 add.19.g_ref
  64.5 7.6 %shard_map.86 = (f32[128,128]{1,0:T(8,128)}, f32[128,128]{1,0:T(8,128)}) custom-call(f32[128,128]{1,0:T(8,128)} %add.19.g_ref), custom_call_target="tpu_custom_call" | custom-call | tf_op jit(solution)/shard_map/pallas_call | solution.py:132
  72.1 0.0 copy-start.1
  72.1 1.4 %fusion.1 = f32[1024,128]{1,0:T(8,128)S(1)} fusion(f32[1024,128]{1,0:T(8,128)S(1)} %bitcast.15, f32[128,128]{1,0:T(8,128)} %get-tuple-element.8), kind=kOutput, calls=%fused_computation.8 | convolution fusion | flops 201326592 | bytes 1114112 | tf_op jit(solution)/shard_map/dot_general | solution.py:248
  73.5 0.0 copy-done
  73.5 1.2 %convolution_convert_fusion = bf16[128,1024]{1,0:T(8,128)(2,1)} fusion(bf16[1024,1024]{1,0:T(8,128)(2,1)S(1)} %copy-done, f32[1024,128]{1,0:T(8,128)S(1)} %fusion.1), kind=kOutput, calls=%fused_computation | convolution fusion | flops 268697600 | bytes 2883584 | tf_op jit(solution)/shard_map/dot_general | solution.py:260
  74.7 6.9 %all-to-all-start.2 = ((bf16[8,16,1024]{2,1,0:T(8,128)(2,1)}), bf16[8,16,1024]{2,1,0:T(8,128)(2,1)S(1)}, u32[]{:S(2)}, u32[]{:S(2)}) async-start(bf16[8,16,1024]{2,1,0:T(8,128)(2,1)} %bitcast.8), calls=%async_computation.2 | async-start | bytes 524288 | tf_op jit(solution)/shard_map/all_to_all | solution.py:264
  81.6 0.6 maximum_multiply_fusion
  82.2 0.0 copy-done.1
  82.2 0.6 broadcast_multiply_fusion
  82.8 8.3 %all-to-all-done.2 = bf16[8,16,1024]{2,1,0:T(8,128)(2,1)S(1)} async-done(((bf16[8,16,1024]{2,1,0:T(8,128)(2,1)}), bf16[8,16,1024]{2,1,0:T(8,128)(2,1)S(1)}, u32[]{:S(2)}, u32[]{:S(2)}) %all-to-all-start.2) | async-done | bytes 262176 | tf_op jit(solution)/shard_map/all_to_all | solution.py:264
  91.1 0.7 convert_reduce_fusion
  (4 shorter events, 0.1 us)
Async XLA Ops:
  28.9 44.6 %copy-start = (bf16[1024,1024]{1,0:T(8,128)(2,1)S(1)}, bf16[1024,1024]{1,0:T(8,128)(2,1)}, u32[]{:S(2)}) copy-start(bf16[1024,1024]{1,0:T(8,128)(2,1)} %get-tuple-element.9) | copy-start | bytes 6291460
  45.1 4.4 %collective-permute-start = (f32[128,128]{1,0:T(8,128)S(1)}, f32[128,128]{1,0:T(8,128)S(1)}, u32[]{:S(2)}, u32[]{:S(2)}) collective-permute-start(f32[128,128]{1,0:T(8,128)S(1)} %convolution_bitcast_fusion), channel_id=1, source_target_pairs={{0,1},{1,0},{2,3},{3,2},{4,5},{5,4},{6,7},{7,6},{8,9},{9,8},{10,11... | collective-permute-start | bytes 196616 | tf_op jit(solution)/shard_map/ppermute | solution.py:65
  49.5 5.2 %collective-permute-start.1 = (f32[128,128]{1,0:T(8,128)S(1)}, f32[128,128]{1,0:T(8,128)S(1)}, u32[]{:S(2)}, u32[]{:S(2)}) collective-permute-start(f32[128,128]{1,0:T(8,128)S(1)} %add.17), channel_id=1, source_target_pairs={{0,2},{1,3},{2,0},{3,1},{4,6},{5,7},{6,4},{7,5},{8,10},{9,11},{10,... | collective-permute-start | bytes 196616 | tf_op jit(solution)/shard_map/ppermute | solution.py:65
  54.7 9.2 %collective-permute-start.2 = (f32[128,128]{1,0:T(8,128)S(1)}, f32[128,128]{1,0:T(8,128)S(1)}, u32[]{:S(2)}, u32[]{:S(2)}) collective-permute-start(f32[128,128]{1,0:T(8,128)S(1)} %add.18), channel_id=1, source_target_pairs={{0,4},{1,5},{2,6},{3,7},{4,0},{5,1},{6,2},{7,3},{8,12},{9,13},{10,... | collective-permute-start | bytes 196616 | tf_op jit(solution)/shard_map/ppermute | solution.py:65
  72.1 10.1 %copy-start.1 = (f32[128,128]{1,0:T(8,128)S(1)}, f32[128,128]{1,0:T(8,128)}, u32[]{:S(2)}) copy-start(f32[128,128]{1,0:T(8,128)} %get-tuple-element.10) | copy-start | bytes 196612
  74.7 16.4 %all-to-all-start.2 = ((bf16[8,16,1024]{2,1,0:T(8,128)(2,1)}), bf16[8,16,1024]{2,1,0:T(8,128)(2,1)S(1)}, u32[]{:S(2)}, u32[]{:S(2)}) async-start(bf16[8,16,1024]{2,1,0:T(8,128)(2,1)} %bitcast.8), calls=%async_computation.2 | async-start | bytes 524288 | tf_op jit(solution)/shard_map/all_to_all | solution.py:264

commit v12 on v11

--- a/solution.py
+++ b/solution.py
@@ -55,6 +55,21 @@
     padded = rows_for(lines, lax.axis_size(axes))
     whole = collect(summed_on_arrival(padded, axes, 0), axes, 0)
     return lax.slice_in_dim(whole, 0, len(lines)).reshape(value.shape)
+
+
+def paired_sum(value, axis):
+    count = lax.axis_size(axis)
+    pair = value + lax.ppermute(value, axis, [(i, i ^ 1) for i in range(count)])
+    pairs = count // 2
+    got = [pair] + [
+        lax.ppermute(pair, axis, [(i, i ^ (2 * m)) for i in range(count)]) for m in range(1, pairs)
+    ]
+    mine = lax.axis_index(axis) // 2
+    total = None
+    for q in range(pairs):
+        term = sum(jnp.where((mine ^ m) == q, got[m], 0.0) for m in range(pairs))
+        total = term if total is None else total + term
+    return total
 
 
 def butterfly_sum(value, axis):
@@ -243,7 +258,7 @@
         pixel_index, act_map[None, :], pupil_field[0], channel_scale, channel_flux, omega
     )
     sketch = sum_by_parts(partial_sketch, "act")
-    gram_matrix = butterfly_sum(gram_of(sketch), "pix")
+    gram_matrix = paired_sum(gram_of(sketch), "pix")
     upper_factor, lower_inverse = chol_inv(gram_matrix)
     basis = lax.dot_general(
         sketch,

time: 92.7 us -> 92 us (level)
  starting transfers between devices: 19.1 us -> 16.2 us
  waiting for transfers between devices: 14.7 us -> 17.4 us
    ppermute x3 -> x4, starting transfers between devices: 12.2 us -> 9.56 us  [the longest x3 7.84 us: paired_sum(): lax.ppermute(pair, axis, [(i, i ^ 2 * m) for i in range(count)])]
    ppermute x3 -> x4, waiting for transfers between devices: 6.48 us -> 8.13 us  [the longest x3 5.48 us: paired_sum(): lax.ppermute(pair, axis, [(i, i ^ 2 * m) for i in range(count)])]
    all_to_all x1, waiting for transfers between devices: 8.27 us -> 9.24 us  [on_device(): lax.all_to_all(parts, 'pix', split_axis=0, concat_axis=0, tiled=True)]
  transfers between devices with their start and end apart: 4 -> 5, of which waited for: 4 -> 4; matrix products, arithmetic and copies ran while one was open for 1% -> 1% of each run, Pallas kernels for 0% -> 0%
where the time goes in v12:
time: 92 us; the launch traced here: 91.6 us
  blocking collectives  35.3 us (38%)
  waiting for transfers between devices  17.4 us (19%)
  starting transfers between devices  16.2 us (18%)
  Pallas kernels  14.3 us (16%)
  matrix products  3.63 us (4%)
  other arithmetic  2.69 us (3%)
  between operations  1.98 us (2%)
    all_to_all x1, blocking collectives, summed_on_arrival(): lax.all_to_all(parts, axis, split_axis=0, concat_axis=0, tiled=True)  20.2 us
    all_to_all x1, blocking collectives, sent_to_all(): return lax.all_to_all(copies, axis, split_axis=0, concat_axis=0, tiled=True)  15.1 us
    all_to_all x1, waiting for transfers between devices, on_device(): lax.all_to_all(parts, 'pix', split_axis=0, concat_axis=0, tiled=True)  9.24 us
    ppermute x3, starting transfers between devices, paired_sum(): lax.ppermute(pair, axis, [(i, i ^ 2 * m) for i in range(count)])  7.84 us
    pallas_call x1, Pallas kernels, chol_inv(): pl.pallas_call(chol_inv_kernel, out_shape=(jax.ShapeDtypeStruct((n, n), j...  7.57 us
    pallas_call x1, Pallas kernels, jac_and_sketch(): pl.pallas_call(jac_kernel, out_shape=(jax.ShapeDtypeStruct((2 * npix, nac...  6.75 us
    all_to_all x1, starting transfers between devices, on_device(): lax.all_to_all(parts, 'pix', split_axis=0, concat_axis=0, tiled=True)  6.67 us
    ppermute x3, waiting for transfers between devices, paired_sum(): lax.ppermute(pair, axis, [(i, i ^ 2 * m) for i in range(count)])  5.48 us
  transfers between devices with their start and end apart: 5, of which 4 were waited for; matrix products, arithmetic and copies ran while one was open for 1% of the time, Pallas kernels for 0%

profile of v12, /device:TPU:1, one launch (start us, length us, event | category | flops | bytes accessed | tf_op | source)
XLA Modules:
  0.0 91.6 jit_solution(2495912588188388530)
XLA Ops:
  1.9 6.7 %shard_map.85 = (bf16[1024,1024]{1,0:T(8,128)(2,1)}, f32[1024,128]{1,0:T(8,128)}) custom-call(s32[1,512]{1,0:T(1,128)} %pix_ref.1, s32[1,1024]{1,0:T(1,128)} %bitcast.21, f32[2,1024]{1,0:T(2,128)} %bitcast.20, f32[1]{0:T(128)S(6)} %copy.9.scale_ref, f32[1]{0:T(128)S(6)} %copy.10.flux_ref, bf16[1024,128]{1,0:T(8,128)(2,1)} %omega_ref.1), custom_call_target="tpu_custom_call" | custom-call | tf_op jit(solution)/shard_map/pallas_call | solution.py:231
  8.7 20.2 %all_to_all.15 = f32[32,32,128]{2,1,0:T(8,128)S(1)} all-to-all(f32[32,32,128]{2,1,0:T(8,128)} %bitcast.16), channel_id=1, replica_groups=mesh['act'=32,'pix'=8] {'act'}, dimensions={0} | all-to-all | bytes 1048576 | tf_op jit(solution)/shard_map/all_to_all | solution.py:49
  28.9 0.1 broadcast_in_dim.26
  28.9 0.0 copy-start
  29.0 15.1 %all_to_all.16 = f32[32,32,128]{2,1,0:T(8,128)S(1)} all-to-all(f32[32,32,128]{2,1,0:T(8,128)S(1)} %broadcast_in_dim.26), channel_id=1, replica_groups=mesh['act'=32,'pix'=8] {'act'}, dimensions={0} | all-to-all | bytes 1048576 | tf_op jit(solution)/shard_map/all_to_all | solution.py:28
  44.1 1.0 %convolution_bitcast_fusion = f32[128,128]{1,0:T(8,128)S(1)} fusion(f32[32,32,128]{2,1,0:T(8,128)S(1)} %all_to_all.16), kind=kOutput, calls=%fused_computation.1 | convolution fusion | flops 201326592 | bytes 589824 | tf_op jit(solution)/shard_map/dot_general | solution.py:240
  45.1 1.7 %collective-permute-start = (f32[128,128]{1,0:T(8,128)S(1)}, f32[128,128]{1,0:T(8,128)S(1)}, u32[]{:S(2)}, u32[]{:S(2)}) collective-permute-start(f32[128,128]{1,0:T(8,128)S(1)} %convolution_bitcast_fusion), channel_id=1, source_target_pairs={{0,1},{1,0},{2,3},{3,2},{4,5},{5,4},{6,7},{7,6},{8,9},{9,8},{10,11... | collective-permute-start | bytes 196616 | tf_op jit(solution)/shard_map/ppermute | solution.py:62
  46.8 2.6 %collective-permute-done = f32[128,128]{1,0:T(8,128)S(1)} collective-permute-done((f32[128,128]{1,0:T(8,128)S(1)}, f32[128,128]{1,0:T(8,128)S(1)}, u32[]{:S(2)}, u32[]{:S(2)}) %collective-permute-start) | collective-permute-done | bytes 65568 | tf_op jit(solution)/shard_map/ppermute | solution.py:62
  49.5 3.1 %collective-permute-start.1 = (f32[128,128]{1,0:T(8,128)S(1)}, f32[128,128]{1,0:T(8,128)S(1)}, u32[]{:S(2)}, u32[]{:S(2)}) collective-permute-start(f32[128,128]{1,0:T(8,128)S(1)} %add.57), channel_id=1, source_target_pairs={{0,2},{1,3},{2,0},{3,1},{4,6},{5,7},{6,4},{7,5},{8,10},{9,11},{10,... | collective-permute-start | bytes 196616 | tf_op jit(solution)/shard_map/ppermute | solution.py:65
  52.6 4.8 %collective-permute-start.2 = (f32[128,128]{1,0:T(8,128)S(1)}, f32[128,128]{1,0:T(8,128)S(1)}, u32[]{:S(2)}, u32[]{:S(2)}) collective-permute-start(f32[128,128]{1,0:T(8,128)S(1)} %add.57), channel_id=1, source_target_pairs={{0,4},{1,5},{2,6},{3,7},{4,0},{5,1},{6,2},{7,3},{8,12},{9,13},{10,... | collective-permute-start | bytes 196616 | tf_op jit(solution)/shard_map/ppermute | solution.py:65
  57.3 0.0 collective-permute-start.3
  57.3 0.0 collective-permute-done.1
  57.3 2.9 %collective-permute-done.2 = f32[128,128]{1,0:T(8,128)S(1)} collective-permute-done((f32[128,128]{1,0:T(8,128)S(1)}, f32[128,128]{1,0:T(8,128)S(1)}, u32[]{:S(2)}, u32[]{:S(2)}) %collective-permute-start.2) | collective-permute-done | bytes 65568 | tf_op jit(solution)/shard_map/ppermute | solution.py:65
  60.2 2.6 %collective-permute-done.3 = f32[128,128]{1,0:T(8,128)S(1)} collective-permute-done((f32[128,128]{1,0:T(8,128)S(1)}, f32[128,128]{1,0:T(8,128)S(1)}, u32[]{:S(2)}, u32[]{:S(2)}) %collective-permute-start.3) | collective-permute-done | bytes 65568 | tf_op jit(solution)/shard_map/ppermute | solution.py:65
  62.8 0.7 add_add_fusion.g_ref
  63.5 7.6 %shard_map.86 = (f32[128,128]{1,0:T(8,128)}, f32[128,128]{1,0:T(8,128)}) custom-call(f32[128,128]{1,0:T(8,128)} %add_add_fusion.g_ref), custom_call_target="tpu_custom_call" | custom-call | tf_op jit(solution)/shard_map/pallas_call | solution.py:147
  71.1 1.4 %fusion.1 = f32[1024,128]{1,0:T(8,128)S(1)} fusion(f32[1024,128]{1,0:T(8,128)S(1)} %bitcast.15, f32[128,128]{1,0:T(8,128)} %get-tuple-element.8), kind=kOutput, calls=%fused_computation.9 | convolution fusion | flops 201326592 | bytes 1114112 | tf_op jit(solution)/shard_map/dot_general | solution.py:263
  72.5 0.0 copy-done
  72.6 1.2 %convolution_convert_fusion = bf16[128,1024]{1,0:T(8,128)(2,1)} fusion(bf16[1024,1024]{1,0:T(8,128)(2,1)S(1)} %copy-done, f32[1024,128]{1,0:T(8,128)S(1)} %fusion.1), kind=kOutput, calls=%fused_computation | convolution fusion | flops 268697600 | bytes 2883584 | tf_op jit(solution)/shard_map/dot_general | solution.py:275
  73.7 6.7 %all-to-all-start.2 = ((bf16[8,16,1024]{2,1,0:T(8,128)(2,1)}), bf16[8,16,1024]{2,1,0:T(8,128)(2,1)S(1)}, u32[]{:S(2)}, u32[]{:S(2)}) async-start(bf16[8,16,1024]{2,1,0:T(8,128)(2,1)} %bitcast.8), calls=%async_computation.2 | async-start | bytes 524288 | tf_op jit(solution)/shard_map/all_to_all | solution.py:279
  80.4 0.6 maximum_multiply_fusion
  81.0 0.6 broadcast_multiply_fusion
  81.7 9.2 %all-to-all-done.2 = bf16[8,16,1024]{2,1,0:T(8,128)(2,1)S(1)} async-done(((bf16[8,16,1024]{2,1,0:T(8,128)(2,1)}), bf16[8,16,1024]{2,1,0:T(8,128)(2,1)S(1)}, u32[]{:S(2)}, u32[]{:S(2)}) %all-to-all-start.2) | async-done | bytes 262176 | tf_op jit(solution)/shard_map/all_to_all | solution.py:279
  90.9 0.7 convert_reduce_fusion
  (5 shorter events, 0.1 us)
Async XLA Ops:
  28.9 43.6 %copy-start = (bf16[1024,1024]{1,0:T(8,128)(2,1)S(1)}, bf16[1024,1024]{1,0:T(8,128)(2,1)}, u32[]{:S(2)}) copy-start(bf16[1024,1024]{1,0:T(8,128)(2,1)} %get-tuple-element.9) | copy-start | bytes 6291460
  45.1 4.4 %collective-permute-start = (f32[128,128]{1,0:T(8,128)S(1)}, f32[128,128]{1,0:T(8,128)S(1)}, u32[]{:S(2)}, u32[]{:S(2)}) collective-permute-start(f32[128,128]{1,0:T(8,128)S(1)} %convolution_bitcast_fusion), channel_id=1, source_target_pairs={{0,1},{1,0},{2,3},{3,2},{4,5},{5,4},{6,7},{7,6},{8,9},{9,8},{10,11... | collective-permute-start | bytes 196616 | tf_op jit(solution)/shard_map/ppermute | solution.py:62
  49.5 7.8 %collective-permute-start.1 = (f32[128,128]{1,0:T(8,128)S(1)}, f32[128,128]{1,0:T(8,128)S(1)}, u32[]{:S(2)}, u32[]{:S(2)}) collective-permute-start(f32[128,128]{1,0:T(8,128)S(1)} %add.57), channel_id=1, source_target_pairs={{0,2},{1,3},{2,0},{3,1},{4,6},{5,7},{6,4},{7,5},{8,10},{9,11},{10,... | collective-permute-start | bytes 196616 | tf_op jit(solution)/shard_map/ppermute | solution.py:65
  52.6 7.6 %collective-permute-start.2 = (f32[128,128]{1,0:T(8,128)S(1)}, f32[128,128]{1,0:T(8,128)S(1)}, u32[]{:S(2)}, u32[]{:S(2)}) collective-permute-start(f32[128,128]{1,0:T(8,128)S(1)} %add.57), channel_id=1, source_target_pairs={{0,4},{1,5},{2,6},{3,7},{4,0},{5,1},{6,2},{7,3},{8,12},{9,13},{10,... | collective-permute-start | bytes 196616 | tf_op jit(solution)/shard_map/ppermute | solution.py:65
  57.3 5.5 %collective-permute-start.3 = (f32[128,128]{1,0:T(8,128)S(1)}, f32[128,128]{1,0:T(8,128)S(1)}, u32[]{:S(2)}, u32[]{:S(2)}) collective-permute-start(f32[128,128]{1,0:T(8,128)S(1)} %add.57), channel_id=1, source_target_pairs={{0,6},{1,7},{2,4},{3,5},{4,2},{5,3},{6,0},{7,1},{8,14},{9,15},{10,... | collective-permute-start | bytes 196616 | tf_op jit(solution)/shard_map/ppermute | solution.py:65
  71.1 9.9 %copy-start.1 = (f32[128,128]{1,0:T(8,128)S(1)}, f32[128,128]{1,0:T(8,128)}, u32[]{:S(2)}) copy-start(f32[128,128]{1,0:T(8,128)} %get-tuple-element.10) | copy-start | bytes 196612
  73.7 17.2 %all-to-all-start.2 = ((bf16[8,16,1024]{2,1,0:T(8,128)(2,1)}), bf16[8,16,1024]{2,1,0:T(8,128)(2,1)S(1)}, u32[]{:S(2)}, u32[]{:S(2)}) async-start(bf16[8,16,1024]{2,1,0:T(8,128)(2,1)} %bitcast.8), calls=%async_computation.2 | async-start | bytes 524288 | tf_op jit(solution)/shard_map/all_to_all | solution.py:279

commit v13 on v11

--- a/solution.py
+++ b/solution.py
@@ -1,3 +1,4 @@
+import functools
 import math
 
 import jax
@@ -55,6 +56,14 @@
     padded = rows_for(lines, lax.axis_size(axes))
     whole = collect(summed_on_arrival(padded, axes, 0), axes, 0)
     return lax.slice_in_dim(whole, 0, len(lines)).reshape(value.shape)
+
+
+def pair_sums(value, axis):
+    count = lax.axis_size(axis)
+    pair = value + lax.ppermute(value, axis, [(i, i ^ 1) for i in range(count)])
+    return [pair] + [
+        lax.ppermute(pair, axis, [(i, i ^ (2 * m)) for i in range(count)]) for m in range(1, count // 2)
+    ]
 
 
 def butterfly_sum(value, axis):
@@ -70,9 +79,19 @@
 STEP = 4
 
 
-def chol_inv_kernel(g_ref, lt_ref, inv_ref):
-    n = g_ref.shape[0]
-    lt_ref[...] = g_ref[...]
+def chol_inv_kernel(axis, *refs):
+    *got, lt_ref, inv_ref = refs
+    pairs = len(got)
+    mine = lax.axis_index(axis) // 2
+    total = None
+    for q in range(pairs):
+        which = mine ^ q
+        term = got[pairs - 1][...]
+        for k in reversed(range(pairs - 1)):
+            term = jnp.where(which == k, got[k][...], term)
+        total = term if total is None else total + term
+    n = total.shape[0]
+    lt_ref[...] = total
     rows = lax.broadcasted_iota(jnp.int32, (n, n), 0)
     cols = lax.broadcasted_iota(jnp.int32, (n, n), 1)
     inv_ref[...] = jnp.where(rows == cols, 1.0, 0.0).astype(jnp.float32)
@@ -127,17 +146,17 @@
     lax.fori_loop(0, n // STEP, step, 0)
 
 
-def chol_inv(g):
-    n = g.shape[0]
+def chol_inv(got, axis):
+    n = got[0].shape[0]
     return pl.pallas_call(
-        chol_inv_kernel,
+        functools.partial(chol_inv_kernel, axis),
         out_shape=(
             jax.ShapeDtypeStruct((n, n), jnp.float32),
             jax.ShapeDtypeStruct((n, n), jnp.float32),
         ),
-        in_specs=[pl.BlockSpec(memory_space=pltpu.VMEM)],
+        in_specs=[pl.BlockSpec(memory_space=pltpu.VMEM)] * len(got),
         out_specs=(pl.BlockSpec(memory_space=pltpu.VMEM), pl.BlockSpec(memory_space=pltpu.VMEM)),
-    )(g)
+    )(*got)
 
 
 HALF_PI_HI = 1.5703125
@@ -243,8 +262,7 @@
         pixel_index, act_map[None, :], pupil_field[0], channel_scale, channel_flux, omega
     )
     sketch = sum_by_parts(partial_sketch, "act")
-    gram_matrix = butterfly_sum(gram_of(sketch), "pix")
-    upper_factor, lower_inverse = chol_inv(gram_matrix)
+    upper_factor, lower_inverse = chol_inv(pair_sums(gram_of(sketch), "pix"), "pix")
     basis = lax.dot_general(
         sketch,
         lower_inverse,

time: 92.7 us -> 92.2 us (level)
  starting transfers between devices: 19.1 us -> 16.2 us
  waiting for transfers between devices: 14.7 us -> 17.4 us
    ppermute x3 -> x4, starting transfers between devices: 12.2 us -> 9.56 us  [the longest x3 7.84 us: pair_sums(): lax.ppermute(pair, axis, [(i, i ^ 2 * m) for i in range(count)])]
    ppermute x3 -> x4, waiting for transfers between devices: 6.48 us -> 8.12 us  [the longest x3 5.47 us: pair_sums(): lax.ppermute(pair, axis, [(i, i ^ 2 * m) for i in range(count)])]
    all_to_all x1, waiting for transfers between devices: 8.27 us -> 9.25 us  [on_device(): lax.all_to_all(parts, 'pix', split_axis=0, concat_axis=0, tiled=True)]
  transfers between devices with their start and end apart: 4 -> 5, of which waited for: 4 -> 4; matrix products, arithmetic and copies ran while one was open for 1% -> 1% of each run, Pallas kernels for 0% -> 0%
where the time goes in v13:
time: 92.2 us; the launch traced here: 91.8 us
  blocking collectives  35.3 us (38%)
  waiting for transfers between devices  17.4 us (19%)
  starting transfers between devices  16.2 us (18%)
  Pallas kernels  14.5 us (16%)
  matrix products  3.63 us (4%)
  between operations  2 us (2%)
  other arithmetic  1.98 us (2%)
    all_to_all x1, blocking collectives, summed_on_arrival(): lax.all_to_all(parts, axis, split_axis=0, concat_axis=0, tiled=True)  20.2 us
    all_to_all x1, blocking collectives, sent_to_all(): return lax.all_to_all(copies, axis, split_axis=0, concat_axis=0, tiled=True)  15.1 us
    all_to_all x1, waiting for transfers between devices, on_device(): lax.all_to_all(parts, 'pix', split_axis=0, concat_axis=0, tiled=True)  9.25 us
    ppermute x3, starting transfers between devices, pair_sums(): lax.ppermute(pair, axis, [(i, i ^ 2 * m) for i in range(count)])  7.84 us
    pallas_call x1, Pallas kernels, chol_inv(): pl.pallas_call(functools.partial(chol_inv_kernel, axis), out_shape=(jax.S...  7.8 us
    pallas_call x1, Pallas kernels, jac_and_sketch(): pl.pallas_call(jac_kernel, out_shape=(jax.ShapeDtypeStruct((2 * npix, nac...  6.74 us
    all_to_all x1, starting transfers between devices, on_device(): lax.all_to_all(parts, 'pix', split_axis=0, concat_axis=0, tiled=True)  6.67 us
    ppermute x3, waiting for transfers between devices, pair_sums(): lax.ppermute(pair, axis, [(i, i ^ 2 * m) for i in range(count)])  5.47 us
  transfers between devices with their start and end apart: 5, of which 4 were waited for; matrix products, arithmetic and copies ran while one was open for 1% of the time, Pallas kernels for 0%

profile of v13, /device:TPU:1, one launch (start us, length us, event | category | flops | bytes accessed | tf_op | source)
XLA Modules:
  0.0 91.8 jit_solution(7143119626601643278)
XLA Ops:
  1.9 6.7 %shard_map.85 = (bf16[1024,1024]{1,0:T(8,128)(2,1)}, f32[1024,128]{1,0:T(8,128)}) custom-call(s32[1,512]{1,0:T(1,128)} %pix_ref.1, s32[1,1024]{1,0:T(1,128)} %bitcast.21, f32[2,1024]{1,0:T(2,128)} %bitcast.20, f32[1]{0:T(128)S(6)} %copy.9.scale_ref, f32[1]{0:T(128)S(6)} %copy.10.flux_ref, bf16[1024,128]{1,0:T(8,128)(2,1)} %omega_ref.1), custom_call_target="tpu_custom_call" | custom-call | tf_op jit(solution)/shard_map/pallas_call | solution.py:235
  8.7 20.2 %all_to_all.15 = f32[32,32,128]{2,1,0:T(8,128)S(1)} all-to-all(f32[32,32,128]{2,1,0:T(8,128)} %bitcast.16), channel_id=1, replica_groups=mesh['act'=32,'pix'=8] {'act'}, dimensions={0} | all-to-all | bytes 1048576 | tf_op jit(solution)/shard_map/all_to_all | solution.py:50
  28.9 0.0 copy-start
  28.9 0.1 broadcast_in_dim.7
  29.0 15.1 %all_to_all.16 = f32[32,32,128]{2,1,0:T(8,128)S(1)} all-to-all(f32[32,32,128]{2,1,0:T(8,128)S(1)} %broadcast_in_dim.7), channel_id=1, replica_groups=mesh['act'=32,'pix'=8] {'act'}, dimensions={0} | all-to-all | bytes 1048576 | tf_op jit(solution)/shard_map/all_to_all | solution.py:29
  44.1 1.0 %convolution_bitcast_fusion = f32[128,128]{1,0:T(8,128)S(1)} fusion(f32[32,32,128]{2,1,0:T(8,128)S(1)} %all_to_all.16), kind=kOutput, calls=%fused_computation.1 | convolution fusion | flops 201326592 | bytes 589824 | tf_op jit(solution)/shard_map/dot_general | solution.py:244
  45.1 1.7 %collective-permute-start = (f32[128,128]{1,0:T(8,128)S(1)}, f32[128,128]{1,0:T(8,128)S(1)}, u32[]{:S(2)}, u32[]{:S(2)}) collective-permute-start(f32[128,128]{1,0:T(8,128)S(1)} %convolution_bitcast_fusion), channel_id=1, source_target_pairs={{0,1},{1,0},{2,3},{3,2},{4,5},{5,4},{6,7},{7,6},{8,9},{9,8},{10,11... | collective-permute-start | bytes 196616 | tf_op jit(solution)/shard_map/ppermute | solution.py:63
  46.8 2.6 %collective-permute-done = f32[128,128]{1,0:T(8,128)S(1)} collective-permute-done((f32[128,128]{1,0:T(8,128)S(1)}, f32[128,128]{1,0:T(8,128)S(1)}, u32[]{:S(2)}, u32[]{:S(2)}) %collective-permute-start) | collective-permute-done | bytes 65568 | tf_op jit(solution)/shard_map/ppermute | solution.py:63
  49.5 0.0 copy-start.1
  49.5 3.1 %collective-permute-start.1 = (f32[128,128]{1,0:T(8,128)S(1)}, f32[128,128]{1,0:T(8,128)S(1)}, u32[]{:S(2)}, u32[]{:S(2)}) collective-permute-start(f32[128,128]{1,0:T(8,128)S(1)} %add.11.refs_0_), channel_id=1, source_target_pairs={{0,2},{1,3},{2,0},{3,1},{4,6},{5,7},{6,4},{7,5},{8,10},{9,11},{10,... | collective-permute-start | bytes 196616 | tf_op jit(solution)/shard_map/ppermute | solution.py:65
  52.6 4.8 %collective-permute-start.2 = (f32[128,128]{1,0:T(8,128)S(1)}, f32[128,128]{1,0:T(8,128)S(1)}, u32[]{:S(2)}, u32[]{:S(2)}) collective-permute-start(f32[128,128]{1,0:T(8,128)S(1)} %add.11.refs_0_), channel_id=1, source_target_pairs={{0,4},{1,5},{2,6},{3,7},{4,0},{5,1},{6,2},{7,3},{8,12},{9,13},{10,... | collective-permute-start | bytes 196616 | tf_op jit(solution)/shard_map/ppermute | solution.py:65
  57.3 0.0 collective-permute-start.3
  57.3 0.0 collective-permute-done.1.refs_1_
  57.4 2.9 %collective-permute-done.2.refs_2_ = f32[128,128]{1,0:T(8,128)S(1)} collective-permute-done((f32[128,128]{1,0:T(8,128)S(1)}, f32[128,128]{1,0:T(8,128)S(1)}, u32[]{:S(2)}, u32[]{:S(2)}) %collective-permute-start.2) | collective-permute-done | bytes 65568 | tf_op jit(solution)/shard_map/ppermute | solution.py:65
  60.2 2.6 %collective-permute-done.3.refs_3_ = f32[128,128]{1,0:T(8,128)S(1)} collective-permute-done((f32[128,128]{1,0:T(8,128)S(1)}, f32[128,128]{1,0:T(8,128)S(1)}, u32[]{:S(2)}, u32[]{:S(2)}) %collective-permute-start.3) | collective-permute-done | bytes 65568 | tf_op jit(solution)/shard_map/ppermute | solution.py:65
  62.9 0.6 copy-done.5
  63.5 7.8 %shard_map.86 = (f32[128,128]{1,0:T(8,128)}, f32[128,128]{1,0:T(8,128)}) custom-call(f32[128,128]{1,0:T(8,128)} %copy-done.1, f32[128,128]{1,0:T(8,128)} %copy-done.3, f32[128,128]{1,0:T(8,128)} %copy-done.4, f32[128,128]{1,0:T(8,128)} %copy-done.5), custom_call_target="tpu_custom_call" | custom-call | tf_op jit(solution)/shard_map/pallas_call | solution.py:151
  71.3 1.5 %fusion.1 = f32[1024,128]{1,0:T(8,128)S(1)} fusion(f32[1024,128]{1,0:T(8,128)S(1)} %bitcast.15, f32[128,128]{1,0:T(8,128)} %get-tuple-element.8), kind=kOutput, calls=%fused_computation.8 | convolution fusion | flops 201326592 | bytes 1114112 | tf_op jit(solution)/shard_map/dot_general | solution.py:266
  72.7 1.2 %convolution_convert_fusion = bf16[128,1024]{1,0:T(8,128)(2,1)} fusion(bf16[1024,1024]{1,0:T(8,128)(2,1)S(1)} %copy-done, f32[1024,128]{1,0:T(8,128)S(1)} %fusion.1), kind=kOutput, calls=%fused_computation | convolution fusion | flops 268697600 | bytes 2883584 | tf_op jit(solution)/shard_map/dot_general | solution.py:278
  73.9 6.7 %all-to-all-start.2 = ((bf16[8,16,1024]{2,1,0:T(8,128)(2,1)}), bf16[8,16,1024]{2,1,0:T(8,128)(2,1)S(1)}, u32[]{:S(2)}, u32[]{:S(2)}) async-start(bf16[8,16,1024]{2,1,0:T(8,128)(2,1)} %bitcast.8), calls=%async_computation.2 | async-start | bytes 524288 | tf_op jit(solution)/shard_map/all_to_all | solution.py:282
  80.6 0.6 maximum_multiply_fusion
  81.2 0.6 broadcast_multiply_fusion
  81.8 9.2 %all-to-all-done.2 = bf16[8,16,1024]{2,1,0:T(8,128)(2,1)S(1)} async-done(((bf16[8,16,1024]{2,1,0:T(8,128)(2,1)}), bf16[8,16,1024]{2,1,0:T(8,128)(2,1)S(1)}, u32[]{:S(2)}, u32[]{:S(2)}) %all-to-all-start.2) | async-done | bytes 262176 | tf_op jit(solution)/shard_map/all_to_all | solution.py:282
  91.1 0.7 convert_reduce_fusion
  (12 shorter events, 0.1 us)
Async XLA Ops:
  28.9 43.8 %copy-start = (bf16[1024,1024]{1,0:T(8,128)(2,1)S(1)}, bf16[1024,1024]{1,0:T(8,128)(2,1)}, u32[]{:S(2)}) copy-start(bf16[1024,1024]{1,0:T(8,128)(2,1)} %get-tuple-element.9) | copy-start | bytes 6291460
  45.1 4.4 %collective-permute-start = (f32[128,128]{1,0:T(8,128)S(1)}, f32[128,128]{1,0:T(8,128)S(1)}, u32[]{:S(2)}, u32[]{:S(2)}) collective-permute-start(f32[128,128]{1,0:T(8,128)S(1)} %convolution_bitcast_fusion), channel_id=1, source_target_pairs={{0,1},{1,0},{2,3},{3,2},{4,5},{5,4},{6,7},{7,6},{8,9},{9,8},{10,11... | collective-permute-start | bytes 196616 | tf_op jit(solution)/shard_map/ppermute | solution.py:63
  49.5 13.3 %copy-start.1 = (f32[128,128]{1,0:T(8,128)}, f32[128,128]{1,0:T(8,128)S(1)}, u32[]{:S(2)}) copy-start(f32[128,128]{1,0:T(8,128)S(1)} %add.11.refs_0_) | copy-start | bytes 196612
  49.5 7.8 %collective-permute-start.1 = (f32[128,128]{1,0:T(8,128)S(1)}, f32[128,128]{1,0:T(8,128)S(1)}, u32[]{:S(2)}, u32[]{:S(2)}) collective-permute-start(f32[128,128]{1,0:T(8,128)S(1)} %add.11.refs_0_), channel_id=1, source_target_pairs={{0,2},{1,3},{2,0},{3,1},{4,6},{5,7},{6,4},{7,5},{8,10},{9,11},{10,... | collective-permute-start | bytes 196616 | tf_op jit(solution)/shard_map/ppermute | solution.py:65
  52.6 7.6 %collective-permute-start.2 = (f32[128,128]{1,0:T(8,128)S(1)}, f32[128,128]{1,0:T(8,128)S(1)}, u32[]{:S(2)}, u32[]{:S(2)}) collective-permute-start(f32[128,128]{1,0:T(8,128)S(1)} %add.11.refs_0_), channel_id=1, source_target_pairs={{0,4},{1,5},{2,6},{3,7},{4,0},{5,1},{6,2},{7,3},{8,12},{9,13},{10,... | collective-permute-start | bytes 196616 | tf_op jit(solution)/shard_map/ppermute | solution.py:65
  57.3 5.5 %collective-permute-start.3 = (f32[128,128]{1,0:T(8,128)S(1)}, f32[128,128]{1,0:T(8,128)S(1)}, u32[]{:S(2)}, u32[]{:S(2)}) collective-permute-start(f32[128,128]{1,0:T(8,128)S(1)} %add.11.refs_0_), channel_id=1, source_target_pairs={{0,6},{1,7},{2,4},{3,5},{4,2},{5,3},{6,0},{7,1},{8,14},{9,15},{10,... | collective-permute-start | bytes 196616 | tf_op jit(solution)/shard_map/ppermute | solution.py:65
  57.4 5.5 %copy-start.3 = (f32[128,128]{1,0:T(8,128)}, f32[128,128]{1,0:T(8,128)S(1)}, u32[]{:S(2)}) copy-start(f32[128,128]{1,0:T(8,128)S(1)} %collective-permute-done.1.refs_1_) | copy-start | bytes 196612
  60.2 2.6 %copy-start.4 = (f32[128,128]{1,0:T(8,128)}, f32[128,128]{1,0:T(8,128)S(1)}, u32[]{:S(2)}) copy-start(f32[128,128]{1,0:T(8,128)S(1)} %collective-permute-done.2.refs_2_) | copy-start | bytes 196612
  62.8 0.6 copy-start.5
  71.3 9.9 %copy-start.2 = (f32[128,128]{1,0:T(8,128)S(1)}, f32[128,128]{1,0:T(8,128)}, u32[]{:S(2)}) copy-start(f32[128,128]{1,0:T(8,128)} %get-tuple-element.10) | copy-start | bytes 196612
  73.9 17.2 %all-to-all-start.2 = ((bf16[8,16,1024]{2,1,0:T(8,128)(2,1)}), bf16[8,16,1024]{2,1,0:T(8,128)(2,1)S(1)}, u32[]{:S(2)}, u32[]{:S(2)}) async-start(bf16[8,16,1024]{2,1,0:T(8,128)(2,1)} %bitcast.8), calls=%async_computation.2 | async-start | bytes 524288 | tf_op jit(solution)/shard_map/all_to_all | solution.py:282

commit v14 on v12

--- a/solution.py
+++ b/solution.py
@@ -225,11 +225,69 @@
         jac_ref[npix + b * BLOCK : npix + (b + 1) * BLOCK, :] = (amp * (e_re * sine + e_im * cosine)).astype(jnp.bfloat16)
     sketch_ref[...] = jnp.dot(jac_ref[...], omega_ref[...], preferred_element_type=jnp.float32)
 
+def split2(t):
+    hi = t.astype(jnp.bfloat16)
+    lo = (t - hi.astype(jnp.float32)).astype(jnp.bfloat16)
+    return jnp.concatenate([hi, lo], axis=1)
+
+def jac_table_kernel(pix_ref, code_ref, field_ref, scale_ref, flux_ref, omega_ref, jac_ref, sketch_ref):
+    npix = pix_ref.shape[1]
+    nact = code_ref.shape[1]
+    g = GRID
+    wave_scale = scale_ref[0]
+    flux_level = flux_ref[0]
+    pixels = pix_ref[...]
+    delta_u = pixels // FOCAL - FOCAL // 2
+    delta_v = pixels % FOCAL - FOCAL // 2
+    radius = (delta_u * delta_u + delta_v * delta_v).astype(jnp.float32)
+    amplitude = flux_level * jnp.exp(-INFL_RATE * radius / (FOCAL * FOCAL))
+    defocus = radius * (TWO_PI * DEFOCUS_RATE / (FOCAL * FOCAL)) / wave_scale
+    zero = jnp.zeros_like(radius)
+    terms = jnp.concatenate(
+        [delta_u.astype(jnp.float32), delta_v.astype(jnp.float32), amplitude, defocus, zero, zero, zero, zero], axis=0
+    ).T
+    du, dv, amp, defo = terms[:, 0:1], terms[:, 1:2], terms[:, 2:3], terms[:, 3:4]
+    rate = TWO_PI / FOCAL * wave_scale
+    offs = (lax.broadcasted_iota(jnp.int32, (1, g), 1) - g // 2).astype(jnp.float32)
+    su, cu = sin_cos(-rate * (du * offs))
+    sv, cv = sin_cos(-rate * (dv * offs))
+    sf, cf = sin_cos(defo)
+    ure = jnp.concatenate([cu, cu * cf - su * sf], axis=1)
+    uim = jnp.concatenate([su, cu * sf + su * cf], axis=1)
+    codes = code_ref[...]
+    mirror = codes // (g * g)
+    col_x = codes // g % g
+    col_y = codes % g
+    pick_x = lax.broadcasted_iota(jnp.int32, (2 * g, nact), 0) == mirror * g + col_x
+    pick_y = lax.broadcasted_iota(jnp.int32, (g, nact), 0) == col_y
+    ox = pick_x.astype(jnp.bfloat16)
+    oy = pick_y.astype(jnp.bfloat16)
+    ox2 = jnp.concatenate([ox, ox], axis=0)
+    oy2 = jnp.concatenate([oy, oy], axis=0)
+    f32 = jnp.float32
+    tu_re, tu_im, tv_re, tv_im = split2(ure), split2(uim), split2(cv), split2(sv)
+    e_re = field_ref[0:1, :]
+    e_im = field_ref[1:2, :]
+    rb = 128
+    for b in range(npix // rb):
+        sl = slice(b * rb, (b + 1) * rb)
+        u_re = jnp.dot(tu_re[sl], ox2, preferred_element_type=f32)
+        u_im = jnp.dot(tu_im[sl], ox2, preferred_element_type=f32)
+        v_re = jnp.dot(tv_re[sl], oy2, preferred_element_type=f32)
+        v_im = jnp.dot(tv_im[sl], oy2, preferred_element_type=f32)
+        w_re = u_re * v_re - u_im * v_im
+        w_im = u_re * v_im + u_im * v_re
+        a_b = amp[sl]
+        jac_ref[b * rb : (b + 1) * rb, :] = (a_b * (e_re * w_re - e_im * w_im)).astype(jnp.bfloat16)
+        jac_ref[npix + b * rb : npix + (b + 1) * rb, :] = (a_b * (e_re * w_im + e_im * w_re)).astype(jnp.bfloat16)
+    sketch_ref[...] = jnp.dot(jac_ref[...], omega_ref[...], preferred_element_type=jnp.float32)
+
+
 def jac_and_sketch(pixel_row, codes_row, field, scale, flux, omega):
     npix = pixel_row.shape[1]; nact = codes_row.shape[1]
     vm = pl.BlockSpec(memory_space=pltpu.VMEM)
     return pl.pallas_call(
-        jac_kernel,
+        jac_table_kernel,
         out_shape=(jax.ShapeDtypeStruct((2 * npix, nact), jnp.bfloat16), jax.ShapeDtypeStruct((2 * npix, omega.shape[1]), jnp.float32)),
         in_specs=[vm, vm, vm, pl.BlockSpec(memory_space=pltpu.SMEM), pl.BlockSpec(memory_space=pltpu.SMEM), vm],
         out_specs=(vm, vm),

time: 92 us -> 91.5 us (level)
  no operation moved by 1% of the time
where the time goes in v14:
time: 91.5 us; the launch traced here: 91 us
  blocking collectives  35.3 us (39%)
  waiting for transfers between devices  17.4 us (19%)
  starting transfers between devices  16.3 us (18%)
  Pallas kernels  13.7 us (15%)
  matrix products  3.63 us (4%)
  other arithmetic  2.69 us (3%)
  between operations  1.98 us (2%)
    all_to_all x1, blocking collectives, summed_on_arrival(): lax.all_to_all(parts, axis, split_axis=0, concat_axis=0, tiled=True)  20.2 us
    all_to_all x1, blocking collectives, sent_to_all(): return lax.all_to_all(copies, axis, split_axis=0, concat_axis=0, tiled=True)  15.1 us
    all_to_all x1, waiting for transfers between devices, on_device(): lax.all_to_all(parts, 'pix', split_axis=0, concat_axis=0, tiled=True)  9.25 us
    ppermute x3, starting transfers between devices, paired_sum(): lax.ppermute(pair, axis, [(i, i ^ 2 * m) for i in range(count)])  7.84 us
    pallas_call x1, Pallas kernels, chol_inv(): pl.pallas_call(chol_inv_kernel, out_shape=(jax.ShapeDtypeStruct((n, n), j...  7.57 us
    all_to_all x1, starting transfers between devices, on_device(): lax.all_to_all(parts, 'pix', split_axis=0, concat_axis=0, tiled=True)  6.68 us
    pallas_call x1, Pallas kernels, jac_and_sketch(): pl.pallas_call(jac_table_kernel, out_shape=(jax.ShapeDtypeStruct((2 * npi...  6.18 us
    ppermute x3, waiting for transfers between devices, paired_sum(): lax.ppermute(pair, axis, [(i, i ^ 2 * m) for i in range(count)])  5.47 us
  transfers between devices with their start and end apart: 5, of which 4 were waited for; matrix products, arithmetic and copies ran while one was open for 1% of the time, Pallas kernels for 0%

profile of v14, /device:TPU:1, one launch (start us, length us, event | category | flops | bytes accessed | tf_op | source)
XLA Modules:
  0.0 91.0 jit_solution(6131822592885951949)
XLA Ops:
  1.9 6.2 %shard_map.85 = (bf16[1024,1024]{1,0:T(8,128)(2,1)}, f32[1024,128]{1,0:T(8,128)}) custom-call(s32[1,512]{1,0:T(1,128)} %pix_ref.1, s32[1,1024]{1,0:T(1,128)} %bitcast.21, f32[2,1024]{1,0:T(2,128)} %bitcast.20, f32[1]{0:T(128)S(6)} %copy.9.scale_ref, f32[1]{0:T(128)S(6)} %copy.10.flux_ref, bf16[1024,128]{1,0:T(8,128)(2,1)} %omega_ref.1), custom_call_target="tpu_custom_call" | custom-call | tf_op jit(solution)/shard_map/pallas_call | solution.py:289
  8.1 20.2 %all_to_all.15 = f32[32,32,128]{2,1,0:T(8,128)S(1)} all-to-all(f32[32,32,128]{2,1,0:T(8,128)} %bitcast.16), channel_id=1, replica_groups=mesh['act'=32,'pix'=8] {'act'}, dimensions={0} | all-to-all | bytes 1048576 | tf_op jit(solution)/shard_map/all_to_all | solution.py:49
  28.3 0.1 broadcast_in_dim.26
  28.4 0.0 copy-start
  28.4 15.1 %all_to_all.16 = f32[32,32,128]{2,1,0:T(8,128)S(1)} all-to-all(f32[32,32,128]{2,1,0:T(8,128)S(1)} %broadcast_in_dim.26), channel_id=1, replica_groups=mesh['act'=32,'pix'=8] {'act'}, dimensions={0} | all-to-all | bytes 1048576 | tf_op jit(solution)/shard_map/all_to_all | solution.py:28
  43.5 1.0 %convolution_bitcast_fusion = f32[128,128]{1,0:T(8,128)S(1)} fusion(f32[32,32,128]{2,1,0:T(8,128)S(1)} %all_to_all.16), kind=kOutput, calls=%fused_computation.1 | convolution fusion | flops 201326592 | bytes 589824 | tf_op jit(solution)/shard_map/dot_general | solution.py:298
  44.5 1.7 %collective-permute-start = (f32[128,128]{1,0:T(8,128)S(1)}, f32[128,128]{1,0:T(8,128)S(1)}, u32[]{:S(2)}, u32[]{:S(2)}) collective-permute-start(f32[128,128]{1,0:T(8,128)S(1)} %convolution_bitcast_fusion), channel_id=1, source_target_pairs={{0,1},{1,0},{2,3},{3,2},{4,5},{5,4},{6,7},{7,6},{8,9},{9,8},{10,11... | collective-permute-start | bytes 196616 | tf_op jit(solution)/shard_map/ppermute | solution.py:62
  46.3 2.6 %collective-permute-done = f32[128,128]{1,0:T(8,128)S(1)} collective-permute-done((f32[128,128]{1,0:T(8,128)S(1)}, f32[128,128]{1,0:T(8,128)S(1)}, u32[]{:S(2)}, u32[]{:S(2)}) %collective-permute-start) | collective-permute-done | bytes 65568 | tf_op jit(solution)/shard_map/ppermute | solution.py:62
  48.9 3.1 %collective-permute-start.1 = (f32[128,128]{1,0:T(8,128)S(1)}, f32[128,128]{1,0:T(8,128)S(1)}, u32[]{:S(2)}, u32[]{:S(2)}) collective-permute-start(f32[128,128]{1,0:T(8,128)S(1)} %add.57), channel_id=1, source_target_pairs={{0,2},{1,3},{2,0},{3,1},{4,6},{5,7},{6,4},{7,5},{8,10},{9,11},{10,... | collective-permute-start | bytes 196616 | tf_op jit(solution)/shard_map/ppermute | solution.py:65
  52.0 4.8 %collective-permute-start.2 = (f32[128,128]{1,0:T(8,128)S(1)}, f32[128,128]{1,0:T(8,128)S(1)}, u32[]{:S(2)}, u32[]{:S(2)}) collective-permute-start(f32[128,128]{1,0:T(8,128)S(1)} %add.57), channel_id=1, source_target_pairs={{0,4},{1,5},{2,6},{3,7},{4,0},{5,1},{6,2},{7,3},{8,12},{9,13},{10,... | collective-permute-start | bytes 196616 | tf_op jit(solution)/shard_map/ppermute | solution.py:65
  56.8 0.0 collective-permute-start.3
  56.8 0.0 collective-permute-done.1
  56.8 2.9 %collective-permute-done.2 = f32[128,128]{1,0:T(8,128)S(1)} collective-permute-done((f32[128,128]{1,0:T(8,128)S(1)}, f32[128,128]{1,0:T(8,128)S(1)}, u32[]{:S(2)}, u32[]{:S(2)}) %collective-permute-start.2) | collective-permute-done | bytes 65568 | tf_op jit(solution)/shard_map/ppermute | solution.py:65
  59.6 2.6 %collective-permute-done.3 = f32[128,128]{1,0:T(8,128)S(1)} collective-permute-done((f32[128,128]{1,0:T(8,128)S(1)}, f32[128,128]{1,0:T(8,128)S(1)}, u32[]{:S(2)}, u32[]{:S(2)}) %collective-permute-start.3) | collective-permute-done | bytes 65568 | tf_op jit(solution)/shard_map/ppermute | solution.py:65
  62.2 0.7 add_add_fusion.g_ref
  62.9 7.6 %shard_map.86 = (f32[128,128]{1,0:T(8,128)}, f32[128,128]{1,0:T(8,128)}) custom-call(f32[128,128]{1,0:T(8,128)} %add_add_fusion.g_ref), custom_call_target="tpu_custom_call" | custom-call | tf_op jit(solution)/shard_map/pallas_call | solution.py:147
  70.5 1.4 %fusion.1 = f32[1024,128]{1,0:T(8,128)S(1)} fusion(f32[1024,128]{1,0:T(8,128)S(1)} %bitcast.15, f32[128,128]{1,0:T(8,128)} %get-tuple-element.8), kind=kOutput, calls=%fused_computation.9 | convolution fusion | flops 201326592 | bytes 1114112 | tf_op jit(solution)/shard_map/dot_general | solution.py:321
  72.0 0.0 copy-done
  72.0 1.2 %convolution_convert_fusion = bf16[128,1024]{1,0:T(8,128)(2,1)} fusion(bf16[1024,1024]{1,0:T(8,128)(2,1)S(1)} %copy-done, f32[1024,128]{1,0:T(8,128)S(1)} %fusion.1), kind=kOutput, calls=%fused_computation | convolution fusion | flops 268697600 | bytes 2883584 | tf_op jit(solution)/shard_map/dot_general | solution.py:333
  73.1 6.7 %all-to-all-start.2 = ((bf16[8,16,1024]{2,1,0:T(8,128)(2,1)}), bf16[8,16,1024]{2,1,0:T(8,128)(2,1)S(1)}, u32[]{:S(2)}, u32[]{:S(2)}) async-start(bf16[8,16,1024]{2,1,0:T(8,128)(2,1)} %bitcast.8), calls=%async_computation.2 | async-start | bytes 524288 | tf_op jit(solution)/shard_map/all_to_all | solution.py:337
  79.8 0.6 maximum_multiply_fusion
  80.5 0.6 broadcast_multiply_fusion
  81.1 9.2 %all-to-all-done.2 = bf16[8,16,1024]{2,1,0:T(8,128)(2,1)S(1)} async-done(((bf16[8,16,1024]{2,1,0:T(8,128)(2,1)}), bf16[8,16,1024]{2,1,0:T(8,128)(2,1)S(1)}, u32[]{:S(2)}, u32[]{:S(2)}) %all-to-all-start.2) | async-done | bytes 262176 | tf_op jit(solution)/shard_map/all_to_all | solution.py:337
  90.3 0.7 convert_reduce_fusion
  (5 shorter events, 0.1 us)
Async XLA Ops:
  28.4 43.6 %copy-start = (bf16[1024,1024]{1,0:T(8,128)(2,1)S(1)}, bf16[1024,1024]{1,0:T(8,128)(2,1)}, u32[]{:S(2)}) copy-start(bf16[1024,1024]{1,0:T(8,128)(2,1)} %get-tuple-element.9) | copy-start | bytes 6291460
  44.5 4.4 %collective-permute-start = (f32[128,128]{1,0:T(8,128)S(1)}, f32[128,128]{1,0:T(8,128)S(1)}, u32[]{:S(2)}, u32[]{:S(2)}) collective-permute-start(f32[128,128]{1,0:T(8,128)S(1)} %convolution_bitcast_fusion), channel_id=1, source_target_pairs={{0,1},{1,0},{2,3},{3,2},{4,5},{5,4},{6,7},{7,6},{8,9},{9,8},{10,11... | collective-permute-start | bytes 196616 | tf_op jit(solution)/shard_map/ppermute | solution.py:62
  48.9 7.8 %collective-permute-start.1 = (f32[128,128]{1,0:T(8,128)S(1)}, f32[128,128]{1,0:T(8,128)S(1)}, u32[]{:S(2)}, u32[]{:S(2)}) collective-permute-start(f32[128,128]{1,0:T(8,128)S(1)} %add.57), channel_id=1, source_target_pairs={{0,2},{1,3},{2,0},{3,1},{4,6},{5,7},{6,4},{7,5},{8,10},{9,11},{10,... | collective-permute-start | bytes 196616 | tf_op jit(solution)/shard_map/ppermute | solution.py:65
  52.0 7.6 %collective-permute-start.2 = (f32[128,128]{1,0:T(8,128)S(1)}, f32[128,128]{1,0:T(8,128)S(1)}, u32[]{:S(2)}, u32[]{:S(2)}) collective-permute-start(f32[128,128]{1,0:T(8,128)S(1)} %add.57), channel_id=1, source_target_pairs={{0,4},{1,5},{2,6},{3,7},{4,0},{5,1},{6,2},{7,3},{8,12},{9,13},{10,... | collective-permute-start | bytes 196616 | tf_op jit(solution)/shard_map/ppermute | solution.py:65
  56.8 5.5 %collective-permute-start.3 = (f32[128,128]{1,0:T(8,128)S(1)}, f32[128,128]{1,0:T(8,128)S(1)}, u32[]{:S(2)}, u32[]{:S(2)}) collective-permute-start(f32[128,128]{1,0:T(8,128)S(1)} %add.57), channel_id=1, source_target_pairs={{0,6},{1,7},{2,4},{3,5},{4,2},{5,3},{6,0},{7,1},{8,14},{9,15},{10,... | collective-permute-start | bytes 196616 | tf_op jit(solution)/shard_map/ppermute | solution.py:65
  70.5 10.0 %copy-start.1 = (f32[128,128]{1,0:T(8,128)S(1)}, f32[128,128]{1,0:T(8,128)}, u32[]{:S(2)}) copy-start(f32[128,128]{1,0:T(8,128)} %get-tuple-element.10) | copy-start | bytes 196612
  73.1 17.2 %all-to-all-start.2 = ((bf16[8,16,1024]{2,1,0:T(8,128)(2,1)}), bf16[8,16,1024]{2,1,0:T(8,128)(2,1)S(1)}, u32[]{:S(2)}, u32[]{:S(2)}) async-start(bf16[8,16,1024]{2,1,0:T(8,128)(2,1)} %bitcast.8), calls=%async_computation.2 | async-start | bytes 524288 | tf_op jit(solution)/shard_map/all_to_all | solution.py:337

commit v15 on v12

--- a/solution.py
+++ b/solution.py
@@ -164,8 +164,8 @@
     rest = (angle - turns * HALF_PI_HI) - turns * HALF_PI_LO
     quadrant = turns.astype(jnp.int32) & 3
     sq = rest * rest
-    sine = rest + rest * sq * (-1.0 / 6 + sq * (1.0 / 120 + sq * (-1.0 / 5040 + sq * (1.0 / 362880))))
-    cosine = 1.0 + sq * (-0.5 + sq * (1.0 / 24 + sq * (-1.0 / 720 + sq * (1.0 / 40320))))
+    sine = rest + rest * sq * (-1.0 / 6 + sq * (1.0 / 120 + sq * (-1.0 / 5040)))
+    cosine = 1.0 + sq * (-0.5 + sq * (1.0 / 24 + sq * (-1.0 / 720)))
     swap = (quadrant & 1) == 1
     sin_v = jnp.where(swap, cosine, sine)
     cos_v = jnp.where(swap, sine, cosine)

time: 92 us -> 91.7 us (level)
  no operation moved by 1% of the time
where the time goes in v15:
time: 91.7 us; the launch traced here: 91.3 us
  blocking collectives  35.3 us (38%)
  waiting for transfers between devices  17.4 us (19%)
  starting transfers between devices  16.2 us (18%)
  Pallas kernels  14 us (15%)
  matrix products  3.63 us (4%)
  other arithmetic  2.69 us (3%)
  between operations  1.98 us (2%)
    all_to_all x1, blocking collectives, summed_on_arrival(): lax.all_to_all(parts, axis, split_axis=0, concat_axis=0, tiled=True)  20.2 us
    all_to_all x1, blocking collectives, sent_to_all(): return lax.all_to_all(copies, axis, split_axis=0, concat_axis=0, tiled=True)  15.1 us
    all_to_all x1, waiting for transfers between devices, on_device(): lax.all_to_all(parts, 'pix', split_axis=0, concat_axis=0, tiled=True)  9.24 us
    ppermute x3, starting transfers between devices, paired_sum(): lax.ppermute(pair, axis, [(i, i ^ 2 * m) for i in range(count)])  7.84 us
    pallas_call x1, Pallas kernels, chol_inv(): pl.pallas_call(chol_inv_kernel, out_shape=(jax.ShapeDtypeStruct((n, n), j...  7.57 us
    all_to_all x1, starting transfers between devices, on_device(): lax.all_to_all(parts, 'pix', split_axis=0, concat_axis=0, tiled=True)  6.67 us
    pallas_call x1, Pallas kernels, jac_and_sketch(): pl.pallas_call(jac_kernel, out_shape=(jax.ShapeDtypeStruct((2 * npix, nac...  6.42 us
    ppermute x3, waiting for transfers between devices, paired_sum(): lax.ppermute(pair, axis, [(i, i ^ 2 * m) for i in range(count)])  5.48 us
  transfers between devices with their start and end apart: 5, of which 4 were waited for; matrix products, arithmetic and copies ran while one was open for 1% of the time, Pallas kernels for 0%

profile of v15, /device:TPU:1, one launch (start us, length us, event | category | flops | bytes accessed | tf_op | source)
XLA Modules:
  0.0 91.3 jit_solution(8880013411630429960)
XLA Ops:
  1.9 6.4 %shard_map.85 = (bf16[1024,1024]{1,0:T(8,128)(2,1)}, f32[1024,128]{1,0:T(8,128)}) custom-call(s32[1,512]{1,0:T(1,128)} %pix_ref.1, s32[1,1024]{1,0:T(1,128)} %bitcast.21, f32[2,1024]{1,0:T(2,128)} %bitcast.20, f32[1]{0:T(128)S(6)} %copy.9.scale_ref, f32[1]{0:T(128)S(6)} %copy.10.flux_ref, bf16[1024,128]{1,0:T(8,128)(2,1)} %omega_ref.1), custom_call_target="tpu_custom_call" | custom-call | tf_op jit(solution)/shard_map/pallas_call | solution.py:231
  8.3 20.2 %all_to_all.15 = f32[32,32,128]{2,1,0:T(8,128)S(1)} all-to-all(f32[32,32,128]{2,1,0:T(8,128)} %bitcast.16), channel_id=1, replica_groups=mesh['act'=32,'pix'=8] {'act'}, dimensions={0} | all-to-all | bytes 1048576 | tf_op jit(solution)/shard_map/all_to_all | solution.py:49
  28.6 0.1 broadcast_in_dim.26
  28.6 0.0 copy-start
  28.6 15.1 %all_to_all.16 = f32[32,32,128]{2,1,0:T(8,128)S(1)} all-to-all(f32[32,32,128]{2,1,0:T(8,128)S(1)} %broadcast_in_dim.26), channel_id=1, replica_groups=mesh['act'=32,'pix'=8] {'act'}, dimensions={0} | all-to-all | bytes 1048576 | tf_op jit(solution)/shard_map/all_to_all | solution.py:28
  43.8 1.0 %convolution_bitcast_fusion = f32[128,128]{1,0:T(8,128)S(1)} fusion(f32[32,32,128]{2,1,0:T(8,128)S(1)} %all_to_all.16), kind=kOutput, calls=%fused_computation.1 | convolution fusion | flops 201326592 | bytes 589824 | tf_op jit(solution)/shard_map/dot_general | solution.py:240
  44.8 1.7 %collective-permute-start = (f32[128,128]{1,0:T(8,128)S(1)}, f32[128,128]{1,0:T(8,128)S(1)}, u32[]{:S(2)}, u32[]{:S(2)}) collective-permute-start(f32[128,128]{1,0:T(8,128)S(1)} %convolution_bitcast_fusion), channel_id=1, source_target_pairs={{0,1},{1,0},{2,3},{3,2},{4,5},{5,4},{6,7},{7,6},{8,9},{9,8},{10,11... | collective-permute-start | bytes 196616 | tf_op jit(solution)/shard_map/ppermute | solution.py:62
  46.5 2.6 %collective-permute-done = f32[128,128]{1,0:T(8,128)S(1)} collective-permute-done((f32[128,128]{1,0:T(8,128)S(1)}, f32[128,128]{1,0:T(8,128)S(1)}, u32[]{:S(2)}, u32[]{:S(2)}) %collective-permute-start) | collective-permute-done | bytes 65568 | tf_op jit(solution)/shard_map/ppermute | solution.py:62
  49.2 3.1 %collective-permute-start.1 = (f32[128,128]{1,0:T(8,128)S(1)}, f32[128,128]{1,0:T(8,128)S(1)}, u32[]{:S(2)}, u32[]{:S(2)}) collective-permute-start(f32[128,128]{1,0:T(8,128)S(1)} %add.57), channel_id=1, source_target_pairs={{0,2},{1,3},{2,0},{3,1},{4,6},{5,7},{6,4},{7,5},{8,10},{9,11},{10,... | collective-permute-start | bytes 196616 | tf_op jit(solution)/shard_map/ppermute | solution.py:65
  52.3 4.8 %collective-permute-start.2 = (f32[128,128]{1,0:T(8,128)S(1)}, f32[128,128]{1,0:T(8,128)S(1)}, u32[]{:S(2)}, u32[]{:S(2)}) collective-permute-start(f32[128,128]{1,0:T(8,128)S(1)} %add.57), channel_id=1, source_target_pairs={{0,4},{1,5},{2,6},{3,7},{4,0},{5,1},{6,2},{7,3},{8,12},{9,13},{10,... | collective-permute-start | bytes 196616 | tf_op jit(solution)/shard_map/ppermute | solution.py:65
  57.0 0.0 collective-permute-start.3
  57.0 0.0 collective-permute-done.1
  57.0 2.9 %collective-permute-done.2 = f32[128,128]{1,0:T(8,128)S(1)} collective-permute-done((f32[128,128]{1,0:T(8,128)S(1)}, f32[128,128]{1,0:T(8,128)S(1)}, u32[]{:S(2)}, u32[]{:S(2)}) %collective-permute-start.2) | collective-permute-done | bytes 65568 | tf_op jit(solution)/shard_map/ppermute | solution.py:65
  59.9 2.6 %collective-permute-done.3 = f32[128,128]{1,0:T(8,128)S(1)} collective-permute-done((f32[128,128]{1,0:T(8,128)S(1)}, f32[128,128]{1,0:T(8,128)S(1)}, u32[]{:S(2)}, u32[]{:S(2)}) %collective-permute-start.3) | collective-permute-done | bytes 65568 | tf_op jit(solution)/shard_map/ppermute | solution.py:65
  62.5 0.7 add_add_fusion.g_ref
  63.2 7.6 %shard_map.86 = (f32[128,128]{1,0:T(8,128)}, f32[128,128]{1,0:T(8,128)}) custom-call(f32[128,128]{1,0:T(8,128)} %add_add_fusion.g_ref), custom_call_target="tpu_custom_call" | custom-call | tf_op jit(solution)/shard_map/pallas_call | solution.py:147
  70.8 1.4 %fusion.1 = f32[1024,128]{1,0:T(8,128)S(1)} fusion(f32[1024,128]{1,0:T(8,128)S(1)} %bitcast.15, f32[128,128]{1,0:T(8,128)} %get-tuple-element.8), kind=kOutput, calls=%fused_computation.9 | convolution fusion | flops 201326592 | bytes 1114112 | tf_op jit(solution)/shard_map/dot_general | solution.py:263
  72.2 0.0 copy-done
  72.2 1.2 %convolution_convert_fusion = bf16[128,1024]{1,0:T(8,128)(2,1)} fusion(bf16[1024,1024]{1,0:T(8,128)(2,1)S(1)} %copy-done, f32[1024,128]{1,0:T(8,128)S(1)} %fusion.1), kind=kOutput, calls=%fused_computation | convolution fusion | flops 268697600 | bytes 2883584 | tf_op jit(solution)/shard_map/dot_general | solution.py:275
  73.4 6.7 %all-to-all-start.2 = ((bf16[8,16,1024]{2,1,0:T(8,128)(2,1)}), bf16[8,16,1024]{2,1,0:T(8,128)(2,1)S(1)}, u32[]{:S(2)}, u32[]{:S(2)}) async-start(bf16[8,16,1024]{2,1,0:T(8,128)(2,1)} %bitcast.8), calls=%async_computation.2 | async-start | bytes 524288 | tf_op jit(solution)/shard_map/all_to_all | solution.py:279
  80.1 0.6 maximum_multiply_fusion
  80.7 0.6 broadcast_multiply_fusion
  81.4 9.2 %all-to-all-done.2 = bf16[8,16,1024]{2,1,0:T(8,128)(2,1)S(1)} async-done(((bf16[8,16,1024]{2,1,0:T(8,128)(2,1)}), bf16[8,16,1024]{2,1,0:T(8,128)(2,1)S(1)}, u32[]{:S(2)}, u32[]{:S(2)}) %all-to-all-start.2) | async-done | bytes 262176 | tf_op jit(solution)/shard_map/all_to_all | solution.py:279
  90.6 0.7 convert_reduce_fusion
  (5 shorter events, 0.1 us)
Async XLA Ops:
  28.6 43.6 %copy-start = (bf16[1024,1024]{1,0:T(8,128)(2,1)S(1)}, bf16[1024,1024]{1,0:T(8,128)(2,1)}, u32[]{:S(2)}) copy-start(bf16[1024,1024]{1,0:T(8,128)(2,1)} %get-tuple-element.9) | copy-start | bytes 6291460
  44.8 4.4 %collective-permute-start = (f32[128,128]{1,0:T(8,128)S(1)}, f32[128,128]{1,0:T(8,128)S(1)}, u32[]{:S(2)}, u32[]{:S(2)}) collective-permute-start(f32[128,128]{1,0:T(8,128)S(1)} %convolution_bitcast_fusion), channel_id=1, source_target_pairs={{0,1},{1,0},{2,3},{3,2},{4,5},{5,4},{6,7},{7,6},{8,9},{9,8},{10,11... | collective-permute-start | bytes 196616 | tf_op jit(solution)/shard_map/ppermute | solution.py:62
  49.2 7.8 %collective-permute-start.1 = (f32[128,128]{1,0:T(8,128)S(1)}, f32[128,128]{1,0:T(8,128)S(1)}, u32[]{:S(2)}, u32[]{:S(2)}) collective-permute-start(f32[128,128]{1,0:T(8,128)S(1)} %add.57), channel_id=1, source_target_pairs={{0,2},{1,3},{2,0},{3,1},{4,6},{5,7},{6,4},{7,5},{8,10},{9,11},{10,... | collective-permute-start | bytes 196616 | tf_op jit(solution)/shard_map/ppermute | solution.py:65
  52.3 7.6 %collective-permute-start.2 = (f32[128,128]{1,0:T(8,128)S(1)}, f32[128,128]{1,0:T(8,128)S(1)}, u32[]{:S(2)}, u32[]{:S(2)}) collective-permute-start(f32[128,128]{1,0:T(8,128)S(1)} %add.57), channel_id=1, source_target_pairs={{0,4},{1,5},{2,6},{3,7},{4,0},{5,1},{6,2},{7,3},{8,12},{9,13},{10,... | collective-permute-start | bytes 196616 | tf_op jit(solution)/shard_map/ppermute | solution.py:65
  57.0 5.5 %collective-permute-start.3 = (f32[128,128]{1,0:T(8,128)S(1)}, f32[128,128]{1,0:T(8,128)S(1)}, u32[]{:S(2)}, u32[]{:S(2)}) collective-permute-start(f32[128,128]{1,0:T(8,128)S(1)} %add.57), channel_id=1, source_target_pairs={{0,6},{1,7},{2,4},{3,5},{4,2},{5,3},{6,0},{7,1},{8,14},{9,15},{10,... | collective-permute-start | bytes 196616 | tf_op jit(solution)/shard_map/ppermute | solution.py:65
  70.8 9.9 %copy-start.1 = (f32[128,128]{1,0:T(8,128)S(1)}, f32[128,128]{1,0:T(8,128)}, u32[]{:S(2)}) copy-start(f32[128,128]{1,0:T(8,128)} %get-tuple-element.10) | copy-start | bytes 196612
  73.4 17.2 %all-to-all-start.2 = ((bf16[8,16,1024]{2,1,0:T(8,128)(2,1)}), bf16[8,16,1024]{2,1,0:T(8,128)(2,1)S(1)}, u32[]{:S(2)}, u32[]{:S(2)}) async-start(bf16[8,16,1024]{2,1,0:T(8,128)(2,1)} %bitcast.8), calls=%async_computation.2 | async-start | bytes 524288 | tf_op jit(solution)/shard_map/all_to_all | solution.py:279

commit v16 on v12

--- a/solution.py
+++ b/solution.py
@@ -264,7 +264,7 @@
         sketch,
         lower_inverse,
         (((1,), (1,)), ((), ())),
-        precision=lax.Precision.HIGHEST,
+        precision=lax.Precision.HIGH,
         preferred_element_type=jnp.float32,
     )
     first = lax.axis_index("act") * share_pix

time: 92 us -> 91.8 us (level)
  no operation moved by 1% of the time
where the time goes in v16:
time: 91.8 us; the launch traced here: 91.4 us
  blocking collectives  35.3 us (38%)
  waiting for transfers between devices  17.4 us (19%)
  starting transfers between devices  16.2 us (18%)
  Pallas kernels  14.3 us (16%)
  matrix products  3.44 us (4%)
  other arithmetic  2.69 us (3%)
  between operations  1.98 us (2%)
    all_to_all x1, blocking collectives, summed_on_arrival(): lax.all_to_all(parts, axis, split_axis=0, concat_axis=0, tiled=True)  20.2 us
    all_to_all x1, blocking collectives, sent_to_all(): return lax.all_to_all(copies, axis, split_axis=0, concat_axis=0, tiled=True)  15.1 us
    all_to_all x1, waiting for transfers between devices, on_device(): lax.all_to_all(parts, 'pix', split_axis=0, concat_axis=0, tiled=True)  9.25 us
    ppermute x3, starting transfers between devices, paired_sum(): lax.ppermute(pair, axis, [(i, i ^ 2 * m) for i in range(count)])  7.84 us
    pallas_call x1, Pallas kernels, chol_inv(): pl.pallas_call(chol_inv_kernel, out_shape=(jax.ShapeDtypeStruct((n, n), j...  7.57 us
    pallas_call x1, Pallas kernels, jac_and_sketch(): pl.pallas_call(jac_kernel, out_shape=(jax.ShapeDtypeStruct((2 * npix, nac...  6.75 us
    all_to_all x1, starting transfers between devices, on_device(): lax.all_to_all(parts, 'pix', split_axis=0, concat_axis=0, tiled=True)  6.67 us
    ppermute x3, waiting for transfers between devices, paired_sum(): lax.ppermute(pair, axis, [(i, i ^ 2 * m) for i in range(count)])  5.48 us
  transfers between devices with their start and end apart: 5, of which 4 were waited for; matrix products, arithmetic and copies ran while one was open for 1% of the time, Pallas kernels for 0%

profile of v16, /device:TPU:1, one launch (start us, length us, event | category | flops | bytes accessed | tf_op | source)
XLA Modules:
  0.0 91.4 jit_solution(1267379079749055287)
XLA Ops:
  1.9 6.7 %shard_map.85 = (bf16[1024,1024]{1,0:T(8,128)(2,1)}, f32[1024,128]{1,0:T(8,128)}) custom-call(s32[1,512]{1,0:T(1,128)} %pix_ref.1, s32[1,1024]{1,0:T(1,128)} %bitcast.21, f32[2,1024]{1,0:T(2,128)} %bitcast.20, f32[1]{0:T(128)S(6)} %copy.9.scale_ref, f32[1]{0:T(128)S(6)} %copy.10.flux_ref, bf16[1024,128]{1,0:T(8,128)(2,1)} %omega_ref.1), custom_call_target="tpu_custom_call" | custom-call | tf_op jit(solution)/shard_map/pallas_call | solution.py:231
  8.7 20.2 %all_to_all.15 = f32[32,32,128]{2,1,0:T(8,128)S(1)} all-to-all(f32[32,32,128]{2,1,0:T(8,128)} %bitcast.16), channel_id=1, replica_groups=mesh['act'=32,'pix'=8] {'act'}, dimensions={0} | all-to-all | bytes 1048576 | tf_op jit(solution)/shard_map/all_to_all | solution.py:49
  28.9 0.1 broadcast_in_dim.26
  28.9 0.0 copy-start
  29.0 15.1 %all_to_all.16 = f32[32,32,128]{2,1,0:T(8,128)S(1)} all-to-all(f32[32,32,128]{2,1,0:T(8,128)S(1)} %broadcast_in_dim.26), channel_id=1, replica_groups=mesh['act'=32,'pix'=8] {'act'}, dimensions={0} | all-to-all | bytes 1048576 | tf_op jit(solution)/shard_map/all_to_all | solution.py:28
  44.1 1.0 %convolution_bitcast_fusion = f32[128,128]{1,0:T(8,128)S(1)} fusion(f32[32,32,128]{2,1,0:T(8,128)S(1)} %all_to_all.16), kind=kOutput, calls=%fused_computation.1 | convolution fusion | flops 201326592 | bytes 589824 | tf_op jit(solution)/shard_map/dot_general | solution.py:240
  45.1 1.7 %collective-permute-start = (f32[128,128]{1,0:T(8,128)S(1)}, f32[128,128]{1,0:T(8,128)S(1)}, u32[]{:S(2)}, u32[]{:S(2)}) collective-permute-start(f32[128,128]{1,0:T(8,128)S(1)} %convolution_bitcast_fusion), channel_id=1, source_target_pairs={{0,1},{1,0},{2,3},{3,2},{4,5},{5,4},{6,7},{7,6},{8,9},{9,8},{10,11... | collective-permute-start | bytes 196616 | tf_op jit(solution)/shard_map/ppermute | solution.py:62
  46.8 2.6 %collective-permute-done = f32[128,128]{1,0:T(8,128)S(1)} collective-permute-done((f32[128,128]{1,0:T(8,128)S(1)}, f32[128,128]{1,0:T(8,128)S(1)}, u32[]{:S(2)}, u32[]{:S(2)}) %collective-permute-start) | collective-permute-done | bytes 65568 | tf_op jit(solution)/shard_map/ppermute | solution.py:62
  49.5 3.1 %collective-permute-start.1 = (f32[128,128]{1,0:T(8,128)S(1)}, f32[128,128]{1,0:T(8,128)S(1)}, u32[]{:S(2)}, u32[]{:S(2)}) collective-permute-start(f32[128,128]{1,0:T(8,128)S(1)} %add.57), channel_id=1, source_target_pairs={{0,2},{1,3},{2,0},{3,1},{4,6},{5,7},{6,4},{7,5},{8,10},{9,11},{10,... | collective-permute-start | bytes 196616 | tf_op jit(solution)/shard_map/ppermute | solution.py:65
  52.6 4.8 %collective-permute-start.2 = (f32[128,128]{1,0:T(8,128)S(1)}, f32[128,128]{1,0:T(8,128)S(1)}, u32[]{:S(2)}, u32[]{:S(2)}) collective-permute-start(f32[128,128]{1,0:T(8,128)S(1)} %add.57), channel_id=1, source_target_pairs={{0,4},{1,5},{2,6},{3,7},{4,0},{5,1},{6,2},{7,3},{8,12},{9,13},{10,... | collective-permute-start | bytes 196616 | tf_op jit(solution)/shard_map/ppermute | solution.py:65
  57.3 0.0 collective-permute-start.3
  57.3 0.0 collective-permute-done.1
  57.3 2.9 %collective-permute-done.2 = f32[128,128]{1,0:T(8,128)S(1)} collective-permute-done((f32[128,128]{1,0:T(8,128)S(1)}, f32[128,128]{1,0:T(8,128)S(1)}, u32[]{:S(2)}, u32[]{:S(2)}) %collective-permute-start.2) | collective-permute-done | bytes 65568 | tf_op jit(solution)/shard_map/ppermute | solution.py:65
  60.2 2.6 %collective-permute-done.3 = f32[128,128]{1,0:T(8,128)S(1)} collective-permute-done((f32[128,128]{1,0:T(8,128)S(1)}, f32[128,128]{1,0:T(8,128)S(1)}, u32[]{:S(2)}, u32[]{:S(2)}) %collective-permute-start.3) | collective-permute-done | bytes 65568 | tf_op jit(solution)/shard_map/ppermute | solution.py:65
  62.8 0.7 add_add_fusion.g_ref
  63.5 7.6 %shard_map.86 = (f32[128,128]{1,0:T(8,128)}, f32[128,128]{1,0:T(8,128)}) custom-call(f32[128,128]{1,0:T(8,128)} %add_add_fusion.g_ref), custom_call_target="tpu_custom_call" | custom-call | tf_op jit(solution)/shard_map/pallas_call | solution.py:147
  71.1 1.2 %fusion.1 = f32[1024,128]{1,0:T(8,128)S(1)} fusion(f32[1024,128]{1,0:T(8,128)S(1)} %bitcast.15, f32[128,128]{1,0:T(8,128)} %get-tuple-element.8), kind=kOutput, calls=%fused_computation.9 | convolution fusion | flops 100663296 | bytes 1114112 | tf_op jit(solution)/shard_map/dot_general | solution.py:263
  72.3 0.0 copy-done
  72.4 1.2 %convolution_convert_fusion = bf16[128,1024]{1,0:T(8,128)(2,1)} fusion(bf16[1024,1024]{1,0:T(8,128)(2,1)S(1)} %copy-done, f32[1024,128]{1,0:T(8,128)S(1)} %fusion.1), kind=kOutput, calls=%fused_computation | convolution fusion | flops 268697600 | bytes 2883584 | tf_op jit(solution)/shard_map/dot_general | solution.py:275
  73.5 6.7 %all-to-all-start.2 = ((bf16[8,16,1024]{2,1,0:T(8,128)(2,1)}), bf16[8,16,1024]{2,1,0:T(8,128)(2,1)S(1)}, u32[]{:S(2)}, u32[]{:S(2)}) async-start(bf16[8,16,1024]{2,1,0:T(8,128)(2,1)} %bitcast.8), calls=%async_computation.2 | async-start | bytes 524288 | tf_op jit(solution)/shard_map/all_to_all | solution.py:279
  80.2 0.6 maximum_multiply_fusion
  80.8 0.6 broadcast_multiply_fusion
  81.5 9.2 %all-to-all-done.2 = bf16[8,16,1024]{2,1,0:T(8,128)(2,1)S(1)} async-done(((bf16[8,16,1024]{2,1,0:T(8,128)(2,1)}), bf16[8,16,1024]{2,1,0:T(8,128)(2,1)S(1)}, u32[]{:S(2)}, u32[]{:S(2)}) %all-to-all-start.2) | async-done | bytes 262176 | tf_op jit(solution)/shard_map/all_to_all | solution.py:279
  90.7 0.7 convert_reduce_fusion
  (5 shorter events, 0.1 us)
Async XLA Ops:
  28.9 43.4 %copy-start = (bf16[1024,1024]{1,0:T(8,128)(2,1)S(1)}, bf16[1024,1024]{1,0:T(8,128)(2,1)}, u32[]{:S(2)}) copy-start(bf16[1024,1024]{1,0:T(8,128)(2,1)} %get-tuple-element.9) | copy-start | bytes 6291460
  45.1 4.4 %collective-permute-start = (f32[128,128]{1,0:T(8,128)S(1)}, f32[128,128]{1,0:T(8,128)S(1)}, u32[]{:S(2)}, u32[]{:S(2)}) collective-permute-start(f32[128,128]{1,0:T(8,128)S(1)} %convolution_bitcast_fusion), channel_id=1, source_target_pairs={{0,1},{1,0},{2,3},{3,2},{4,5},{5,4},{6,7},{7,6},{8,9},{9,8},{10,11... | collective-permute-start | bytes 196616 | tf_op jit(solution)/shard_map/ppermute | solution.py:62
  49.5 7.8 %collective-permute-start.1 = (f32[128,128]{1,0:T(8,128)S(1)}, f32[128,128]{1,0:T(8,128)S(1)}, u32[]{:S(2)}, u32[]{:S(2)}) collective-permute-start(f32[128,128]{1,0:T(8,128)S(1)} %add.57), channel_id=1, source_target_pairs={{0,2},{1,3},{2,0},{3,1},{4,6},{5,7},{6,4},{7,5},{8,10},{9,11},{10,... | collective-permute-start | bytes 196616 | tf_op jit(solution)/shard_map/ppermute | solution.py:65
  52.6 7.6 %collective-permute-start.2 = (f32[128,128]{1,0:T(8,128)S(1)}, f32[128,128]{1,0:T(8,128)S(1)}, u32[]{:S(2)}, u32[]{:S(2)}) collective-permute-start(f32[128,128]{1,0:T(8,128)S(1)} %add.57), channel_id=1, source_target_pairs={{0,4},{1,5},{2,6},{3,7},{4,0},{5,1},{6,2},{7,3},{8,12},{9,13},{10,... | collective-permute-start | bytes 196616 | tf_op jit(solution)/shard_map/ppermute | solution.py:65
  57.3 5.5 %collective-permute-start.3 = (f32[128,128]{1,0:T(8,128)S(1)}, f32[128,128]{1,0:T(8,128)S(1)}, u32[]{:S(2)}, u32[]{:S(2)}) collective-permute-start(f32[128,128]{1,0:T(8,128)S(1)} %add.57), channel_id=1, source_target_pairs={{0,6},{1,7},{2,4},{3,5},{4,2},{5,3},{6,0},{7,1},{8,14},{9,15},{10,... | collective-permute-start | bytes 196616 | tf_op jit(solution)/shard_map/ppermute | solution.py:65
  71.1 9.8 %copy-start.1 = (f32[128,128]{1,0:T(8,128)S(1)}, f32[128,128]{1,0:T(8,128)}, u32[]{:S(2)}) copy-start(f32[128,128]{1,0:T(8,128)} %get-tuple-element.10) | copy-start | bytes 196612
  73.5 17.2 %all-to-all-start.2 = ((bf16[8,16,1024]{2,1,0:T(8,128)(2,1)}), bf16[8,16,1024]{2,1,0:T(8,128)(2,1)S(1)}, u32[]{:S(2)}, u32[]{:S(2)}) async-start(bf16[8,16,1024]{2,1,0:T(8,128)(2,1)} %bitcast.8), calls=%async_computation.2 | async-start | bytes 524288 | tf_op jit(solution)/shard_map/all_to_all | solution.py:279
